TPU v7x, 512 devices: a whole 4x4x16 slice. The times are simulated.
512 devices in a mesh: cand: 8 (over y, core), doc: 64 (over z, x).
Axes of the slice: x: 4, y: 4, z: 16, core: 2. Of those that a mesh axis runs over, the one named last changes fastest.
Arguments:
- queries: bfloat16 [8192, 8192], P('doc'), may hold values from -6 to 50
- keys_values: bfloat16 [2, 8192, 1024], P(None, 'doc', 'cand'), may hold values from -6 to 50
- factors: float32 [8, 64], P('cand'), may hold values from 1 to 16
- lengths: int32 [16], replicated, may hold values from 1 to 1024, 8192 in all
Outputs:
- attended: bfloat16 [8, 8192, 8192], P('cand', 'doc')
All inputs are finite; a program needn't handle non-finite values.
Results may differ from a plain program's by a relative error of at most 0.0053.
Values may be sent and summed in bfloat16 or wider, within the bound.
No kernel may reach another device: no remote copies, remote signals or barrier semaphores. Data moves between devices by JAX's collectives and lax.ppermute only.
A program may use at most 64 MiB of HBM per device.

v0:
```python
import math

import jax
import jax.numpy as jnp
from jax import lax
from jax.sharding import PartitionSpec as P

H = 64
KVH = 8
HD = 128
SPAN = 8


ROPE_BASE = 500000.0


def passed_along(value, axis, steps):
    count = lax.axis_size(axis)
    first, last = (max(0, -steps), min(count, count - steps))
    return lax.ppermute(value, axis, [(source, source + steps) for source in range(first, last)])


def locate(index_rows, lengths):
    ends = jnp.cumsum(lengths)
    starts = ends - lengths
    docid = jnp.sum((index_rows[:, None] >= ends[None, :]).astype(jnp.int32), axis=1)
    onehot = docid[:, None] == jnp.arange(lengths.shape[0], dtype=jnp.int32)[None, :]
    first_row = jnp.sum(jnp.where(onehot, starts[None, :], 0), axis=1)
    valid = index_rows >= 0
    return (jnp.where(valid, docid, -1), jnp.where(valid, index_rows - first_row, 0))


def rotate(values, offsets, factor):
    row_count = values.shape[0]
    heads_here = values.shape[1] // HD
    half_dim = HD // 2
    shaped = values.reshape(row_count, heads_here, HD).astype(jnp.float32)
    inverse = jnp.power(ROPE_BASE, -2.0 * jnp.arange(half_dim, dtype=jnp.float32) / HD) / factor
    angles = offsets.astype(jnp.float32)[:, None] * inverse[None, :]
    cosine = jnp.cos(angles)[:, None, :]
    sine = jnp.sin(angles)[:, None, :]
    first_half = shaped[..., :half_dim]
    second_half = shaped[..., half_dim:]
    turned = jnp.concatenate(
        [first_half * cosine - second_half * sine, second_half * cosine + first_half * sine],
        axis=-1,
    )
    return turned.reshape(row_count, heads_here * HD).astype(jnp.bfloat16)


def attend(query_rot, key_rot, value_rows, query_doc, query_index, key_doc, key_index):
    row_count = query_rot.shape[0]
    key_count = key_rot.shape[0]
    group_size = H // KVH
    q_grouped = query_rot.reshape(row_count, KVH, group_size, HD).transpose(1, 0, 2, 3)
    k_grouped = key_rot.reshape(key_count, KVH, HD).transpose(1, 0, 2)
    v_grouped = value_rows.reshape(key_count, KVH, HD).transpose(1, 0, 2)
    allowed = (
        (key_doc[None, :] == query_doc[:, None])
        & (key_index[None, :] <= query_index[:, None])
        & (key_doc[None, :] >= 0)
    )
    scale = 1.0 / math.sqrt(HD)

    def per_group(operands):
        q_part, k_part, v_part = operands
        scores = (
            jnp.einsum("rgd,wd->rgw", q_part, k_part, preferred_element_type=jnp.float32) * scale
        )
        scores = jnp.where(allowed[:, None, :], scores, -1e30)
        largest = jnp.max(scores, axis=-1, keepdims=True)
        expw = jnp.exp(scores - largest)
        total = jnp.sum(expw, axis=-1, keepdims=True)
        weights = expw.astype(jnp.bfloat16)
        numer = jnp.einsum("rgw,wd->rgd", weights, v_part, preferred_element_type=jnp.float32)
        return (numer / total).astype(jnp.bfloat16)

    mixed = lax.map(per_group, (q_grouped, k_grouped, v_grouped))
    return mixed.transpose(1, 0, 2, 3).reshape(row_count, H * HD)


def on_device(queries, keys_values, factors, lengths):
    row_count = queries.shape[0]
    device = lax.axis_index("doc")
    query_index = device * row_count + jnp.arange(row_count, dtype=jnp.int32)
    key_index = (device - SPAN) * row_count + jnp.arange((SPAN + 1) * row_count, dtype=jnp.int32)
    whole = lax.all_gather(keys_values, "cand", axis=2, tiled=True)
    pieces = []
    for distance in range(SPAN, 0, -1):
        pieces.append(passed_along(whole, "doc", distance))
    pieces.append(whole)
    window = jnp.concatenate(pieces, axis=1)
    query_doc, query_offset = locate(query_index, lengths)
    key_doc, key_offset = locate(key_index, lengths)
    factor = factors[0]
    query_rot = rotate(queries, query_offset, factor)
    key_rot = rotate(window[0], key_offset, factor)
    mixed = attend(query_rot, key_rot, window[1], query_doc, query_index, key_doc, key_index)
    return mixed[None]


def solution(mesh):
    placed = (P("doc", None), P(None, "doc", "cand"), P("cand", None), P())
    return jax.shard_map(
        on_device, mesh=mesh, in_specs=placed, out_specs=P("cand", "doc", None), check_vma=False
    )
```

profile of v0, /device:TPU:448, one launch (start us, length us, event | category | flops | bytes accessed | tf_op | source)
XLA Modules:
  0.0 222.4 jit_solution(7817300378528015322)
XLA Ops:
  0.0 0.9 copy.19
  1.0 13.6 %all_gather.3 = bf16[2,128,1024]{1,2,0:T(8,128)(2,1)S(1)} all-gather(bf16[2,128,128]{1,2,0:T(8,128)(2,1)S(1)} %copy.19), channel_id=1, replica_groups=mesh['cand'=8,'doc'=64] {'cand'}, dimensions={2}, use_global_device_ids=true | all-gather | bytes 589824 | tf_op jit(solution)/shard_map/all_gather | solution.py:87
  14.6 1.3 collective-permute-start
  15.9 5.1 %collective-permute-start.1 = (bf16[2,128,1024]{1,2,0:T(8,128)(2,1)S(1)}, bf16[2,128,1024]{1,2,0:T(8,128)(2,1)S(1)}, u32[]{:S(2)}, u32[]{:S(2)}) collective-permute-start(bf16[2,128,1024]{1,2,0:T(8,128)(2,1)S(1)} %all_gather.3), channel_id=1, source_target_pairs={{0,7},{1,8},{2,9},{3,10},{4,11},{5,12},{6,13},{7,14},{8,15},{9,16}... | collective-permute-start | bytes 1572872 | tf_op jit(solution)/shard_map/ppermute | solution.py:20
  21.0 1.9 collective-permute-start.2
  22.9 1.9 collective-permute-start.3
  24.9 1.9 collective-permute-start.4
  26.8 2.0 convert_bitcast_fusion
  28.8 0.7 copy.27
  29.6 4.6 %fusion.35 = (f32[128,64,64]{2,1,0:T(8,128)}, f32[128,64,64]{2,1,0:T(8,128)}) fusion(f32[128,64,128]{2,1,0:T(8,128)S(1)} %bitcast.48), kind=kLoop, calls=%fused_computation.60 | loop fusion | bytes 8388608 | tf_op jit(solution)/shard_map/slice | solution.py:42
  34.8 0.3 multiply_cosine_fusion.1
  35.1 8.3 %subtract_convert_fusion = (bf16[128,64,64]{2,0,1:T(8,128)(2,1)S(1)}, bf16[128,64,64]{2,0,1:T(8,128)(2,1)S(1)}) fusion(f32[128,64,64]{2,1,0:T(8,128)} %get-tuple-element.116, f32[128,64,64]{2,1,0:T(8,128)} %get-tuple-element.115, f32[128,64]{1,0:T(8,128)S(1)} %get-tuple-element.120, f32[128,64]{1,0:T(8,128)S(1)} %get-tuple-element.119), kind=kLoop, calls=%fused_computation.23 | loop fusion | flops 4194304 | bytes 6356992 | tf_op jit(solution)/shard_map/convert.4
  43.5 1.1 multiply_cosine_fusion
  44.6 2.5 %pad_maximum_fusion = bf16[128,64,128]{2,0,1:T(8,128)(2,1)} fusion(bf16[128,64,64]{2,0,1:T(8,128)(2,1)S(1)} %get-tuple-element.110, bf16[128,64,64]{2,0,1:T(8,128)(2,1)S(1)} %get-tuple-element.109), kind=kLoop, calls=%fused_computation.27 | loop fusion | flops 4194304 | bytes 4194304 | tf_op jit(solution)/shard_map/concatenate | solution.py:44
  47.1 2.1 collective-permute-start.5
  49.2 1.1 constant_dynamic-update-slice_fusion.8
  50.3 16.4 %collective-permute-done.1 = bf16[2,128,1024]{1,2,0:T(8,128)(2,1)S(1)} collective-permute-done((bf16[2,128,1024]{1,2,0:T(8,128)(2,1)S(1)}, bf16[2,128,1024]{1,2,0:T(8,128)(2,1)S(1)}, u32[]{:S(2)}, u32[]{:S(2)}) %collective-permute-start.1) | collective-permute-done | bytes 524320 | tf_op jit(solution)/shard_map/ppermute | solution.py:20
  66.7 1.9 collective-permute-start.6
  68.7 0.1 constant_dynamic-update-slice_fusion.7
  68.8 22.0 %collective-permute-done.2 = bf16[2,128,1024]{1,2,0:T(8,128)(2,1)S(1)} collective-permute-done((bf16[2,128,1024]{1,2,0:T(8,128)(2,1)S(1)}, bf16[2,128,1024]{1,2,0:T(8,128)(2,1)S(1)}, u32[]{:S(2)}, u32[]{:S(2)}) %collective-permute-start.2) | collective-permute-done | bytes 524320 | tf_op jit(solution)/shard_map/ppermute | solution.py:20
  90.8 1.9 collective-permute-start.7
  92.9 20.1 %collective-permute-done.3 = bf16[2,128,1024]{1,2,0:T(8,128)(2,1)S(1)} collective-permute-done((bf16[2,128,1024]{1,2,0:T(8,128)(2,1)S(1)}, bf16[2,128,1024]{1,2,0:T(8,128)(2,1)S(1)}, u32[]{:S(2)}, u32[]{:S(2)}) %collective-permute-start.3) | collective-permute-done | bytes 524320 | tf_op jit(solution)/shard_map/ppermute | solution.py:20
  113.2 6.8 %collective-permute-done.5 = bf16[2,128,1024]{1,2,0:T(8,128)(2,1)S(1)} collective-permute-done((bf16[2,128,1024]{1,2,0:T(8,128)(2,1)S(1)}, bf16[2,128,1024]{1,2,0:T(8,128)(2,1)S(1)}, u32[]{:S(2)}, u32[]{:S(2)}) %collective-permute-start.5) | collective-permute-done | bytes 524320 | tf_op jit(solution)/shard_map/ppermute | solution.py:20
  120.1 14.6 %collective-permute-done.6 = bf16[2,128,1024]{1,2,0:T(8,128)(2,1)S(1)} collective-permute-done((bf16[2,128,1024]{1,2,0:T(8,128)(2,1)S(1)}, bf16[2,128,1024]{1,2,0:T(8,128)(2,1)S(1)}, u32[]{:S(2)}, u32[]{:S(2)}) %collective-permute-start.6) | collective-permute-done | bytes 524320 | tf_op jit(solution)/shard_map/ppermute | solution.py:20
  134.9 31.8 %collective-permute-done.7 = bf16[2,128,1024]{1,2,0:T(8,128)(2,1)S(1)} collective-permute-done((bf16[2,128,1024]{1,2,0:T(8,128)(2,1)S(1)}, bf16[2,128,1024]{1,2,0:T(8,128)(2,1)S(1)}, u32[]{:S(2)}, u32[]{:S(2)}) %collective-permute-start.7) | collective-permute-done | bytes 524320 | tf_op jit(solution)/shard_map/ppermute | solution.py:20
  166.9 1.8 fusion.34
  168.7 0.3 convert.18
  169.0 0.6 subtract_convert_fusion.1
  169.7 0.2 maximum_bitcast_fusion
  169.9 47.3 %while.11 = (s32[]{:T(128)}, bf16[8,128,8,128]{3,1,2,0:T(8,128)(2,1)}, bf16[8,128,8,128]{3,1,2,0:T(8,128)(2,1)}, bf16[8,1152,128]{1,2,0:T(8,128)(2,1)S(1)}, bf16...) while((s32[]{:T(128)}, ...), condition=%wide.region_8.9_spmd.clone, body=%wide.region_5.8_spmd.clone.sunk | while | flops 613087232 | bytes 15598837 | solution.py:78
  169.9 0.2 and_and_fusion.2
  170.1 2.1 fusion.43
  172.2 1.0 fusion.44
  173.2 2.6 %fusion.45 = bf16[8,128,8,128]{3,1,2,0:T(8,128)(2,1)} fusion(bf16[8,128,8,128]{3,1,2,0:T(8,128)(2,1)} %get-tuple-element.200, s32[]{:T(128)S(6)} %copy.43, f32[128,8,1152]{2,0,1:T(8,128)S(1)} %get-tuple-element.186, f32[128,8]{0,1:T(8,128)S(1)} %get-tuple-element.187, bf16[8,1152,128]{1,2,0:T(8,128)(2,1)} %get-tuple-element.214, ...), kind=kOutput, calls=%fused_computation.11.clone.1 | convolution fusion | flops 304611328 | bytes 5284864 | tf_op jit(solution)/shard_map/while/body/eval_jaxpr/rgw,wd->rgd/dot_general | solution.py:75
  175.8 0.2 and_and_fusion.2
  176.1 2.1 fusion.43
  178.1 1.0 fusion.44
  179.1 2.6 %fusion.45 = bf16[8,128,8,128]{3,1,2,0:T(8,128)(2,1)} fusion(bf16[8,128,8,128]{3,1,2,0:T(8,128)(2,1)} %get-tuple-element.200, s32[]{:T(128)S(6)} %copy.43, f32[128,8,1152]{2,0,1:T(8,128)S(1)} %get-tuple-element.186, f32[128,8]{0,1:T(8,128)S(1)} %get-tuple-element.187, bf16[8,1152,128]{1,2,0:T(8,128)(2,1)} %get-tuple-element.214, ...), kind=kOutput, calls=%fused_computation.11.clone.1 | convolution fusion | flops 304611328 | bytes 5284864 | tf_op jit(solution)/shard_map/while/body/eval_jaxpr/rgw,wd->rgd/dot_general | solution.py:75
  181.7 0.2 and_and_fusion.2
  182.0 2.1 fusion.43
  184.0 1.0 fusion.44
  185.1 2.6 %fusion.45 = bf16[8,128,8,128]{3,1,2,0:T(8,128)(2,1)} fusion(bf16[8,128,8,128]{3,1,2,0:T(8,128)(2,1)} %get-tuple-element.200, s32[]{:T(128)S(6)} %copy.43, f32[128,8,1152]{2,0,1:T(8,128)S(1)} %get-tuple-element.186, f32[128,8]{0,1:T(8,128)S(1)} %get-tuple-element.187, bf16[8,1152,128]{1,2,0:T(8,128)(2,1)} %get-tuple-element.214, ...), kind=kOutput, calls=%fused_computation.11.clone.1 | convolution fusion | flops 304611328 | bytes 5284864 | tf_op jit(solution)/shard_map/while/body/eval_jaxpr/rgw,wd->rgd/dot_general | solution.py:75
  187.7 0.2 and_and_fusion.2
  187.9 2.1 fusion.43
  190.0 1.0 fusion.44
  191.0 2.6 %fusion.45 = bf16[8,128,8,128]{3,1,2,0:T(8,128)(2,1)} fusion(bf16[8,128,8,128]{3,1,2,0:T(8,128)(2,1)} %get-tuple-element.200, s32[]{:T(128)S(6)} %copy.43, f32[128,8,1152]{2,0,1:T(8,128)S(1)} %get-tuple-element.186, f32[128,8]{0,1:T(8,128)S(1)} %get-tuple-element.187, bf16[8,1152,128]{1,2,0:T(8,128)(2,1)} %get-tuple-element.214, ...), kind=kOutput, calls=%fused_computation.11.clone.1 | convolution fusion | flops 304611328 | bytes 5284864 | tf_op jit(solution)/shard_map/while/body/eval_jaxpr/rgw,wd->rgd/dot_general | solution.py:75
  193.6 0.2 and_and_fusion.2
  193.8 2.1 fusion.43
  195.9 1.0 fusion.44
  196.9 2.6 %fusion.45 = bf16[8,128,8,128]{3,1,2,0:T(8,128)(2,1)} fusion(bf16[8,128,8,128]{3,1,2,0:T(8,128)(2,1)} %get-tuple-element.200, s32[]{:T(128)S(6)} %copy.43, f32[128,8,1152]{2,0,1:T(8,128)S(1)} %get-tuple-element.186, f32[128,8]{0,1:T(8,128)S(1)} %get-tuple-element.187, bf16[8,1152,128]{1,2,0:T(8,128)(2,1)} %get-tuple-element.214, ...), kind=kOutput, calls=%fused_computation.11.clone.1 | convolution fusion | flops 304611328 | bytes 5284864 | tf_op jit(solution)/shard_map/while/body/eval_jaxpr/rgw,wd->rgd/dot_general | solution.py:75
  199.5 0.2 and_and_fusion.2
  199.7 2.1 fusion.43
  201.8 1.0 fusion.44
  202.8 2.6 %fusion.45 = bf16[8,128,8,128]{3,1,2,0:T(8,128)(2,1)} fusion(bf16[8,128,8,128]{3,1,2,0:T(8,128)(2,1)} %get-tuple-element.200, s32[]{:T(128)S(6)} %copy.43, f32[128,8,1152]{2,0,1:T(8,128)S(1)} %get-tuple-element.186, f32[128,8]{0,1:T(8,128)S(1)} %get-tuple-element.187, bf16[8,1152,128]{1,2,0:T(8,128)(2,1)} %get-tuple-element.214, ...), kind=kOutput, calls=%fused_computation.11.clone.1 | convolution fusion | flops 304611328 | bytes 5284864 | tf_op jit(solution)/shard_map/while/body/eval_jaxpr/rgw,wd->rgd/dot_general | solution.py:75
  205.4 0.2 and_and_fusion.2
  205.6 2.1 fusion.43
  207.7 1.0 fusion.44
  208.7 2.6 %fusion.45 = bf16[8,128,8,128]{3,1,2,0:T(8,128)(2,1)} fusion(bf16[8,128,8,128]{3,1,2,0:T(8,128)(2,1)} %get-tuple-element.200, s32[]{:T(128)S(6)} %copy.43, f32[128,8,1152]{2,0,1:T(8,128)S(1)} %get-tuple-element.186, f32[128,8]{0,1:T(8,128)S(1)} %get-tuple-element.187, bf16[8,1152,128]{1,2,0:T(8,128)(2,1)} %get-tuple-element.214, ...), kind=kOutput, calls=%fused_computation.11.clone.1 | convolution fusion | flops 304611328 | bytes 5284864 | tf_op jit(solution)/shard_map/while/body/eval_jaxpr/rgw,wd->rgd/dot_general | solution.py:75
  211.3 0.2 and_and_fusion.2
  211.5 2.1 fusion.43
  213.6 1.0 fusion.44
  214.6 2.6 %fusion.45 = bf16[8,128,8,128]{3,1,2,0:T(8,128)(2,1)} fusion(bf16[8,128,8,128]{3,1,2,0:T(8,128)(2,1)} %get-tuple-element.200, s32[]{:T(128)S(6)} %copy.43, f32[128,8,1152]{2,0,1:T(8,128)S(1)} %get-tuple-element.186, f32[128,8]{0,1:T(8,128)S(1)} %get-tuple-element.187, bf16[8,1152,128]{1,2,0:T(8,128)(2,1)} %get-tuple-element.214, ...), kind=kOutput, calls=%fused_computation.11.clone.1 | convolution fusion | flops 304611328 | bytes 5284864 | tf_op jit(solution)/shard_map/while/body/eval_jaxpr/rgw,wd->rgd/dot_general | solution.py:75
  217.2 2.9 %copy.22 = bf16[128,8,8,128]{3,2,1,0:T(8,128)(2,1)S(1)} copy(bf16[128,8,8,128]{3,0,2,1:T(8,128)(2,1)} %bitcast.52) | data formatting | bytes 4194304 | tf_op jit(solution)/shard_map/transpose | solution.py:79
  220.1 2.3 %broadcast_in_dim_reshape.3 = bf16[1,128,8192]{2,1,0:T(8,128)(2,1)} reshape(bf16[128,8,8,128]{3,2,1,0:T(8,128)(2,1)S(1)} %copy.22) | data formatting | bytes 4194304 | tf_op jit(solution)/shard_map/broadcast_in_dim;reshape | solution.py:99
  (28 shorter events, 1.5 us)
Async XLA Ops:
  14.6 32.5 %collective-permute-start = (bf16[2,128,1024]{1,2,0:T(8,128)(2,1)S(1)}, bf16[2,128,1024]{1,2,0:T(8,128)(2,1)}, u32[]{:S(2)}, u32[]{:S(2)}) collective-permute-start(bf16[2,128,1024]{1,2,0:T(8,128)(2,1)S(1)} %all_gather.3), channel_id=1, source_target_pairs={{0,8},{1,9},{2,10},{3,11},{4,12},{5,13},{6,14},{7,15},{8,16},{9,17... | collective-permute-start | bytes 1572872 | tf_op jit(solution)/shard_map/ppermute | solution.py:20
  15.9 50.9 %collective-permute-start.1 = (bf16[2,128,1024]{1,2,0:T(8,128)(2,1)S(1)}, bf16[2,128,1024]{1,2,0:T(8,128)(2,1)S(1)}, u32[]{:S(2)}, u32[]{:S(2)}) collective-permute-start(bf16[2,128,1024]{1,2,0:T(8,128)(2,1)S(1)} %all_gather.3), channel_id=1, source_target_pairs={{0,7},{1,8},{2,9},{3,10},{4,11},{5,12},{6,13},{7,14},{8,15},{9,16}... | collective-permute-start | bytes 1572872 | tf_op jit(solution)/shard_map/ppermute | solution.py:20
  21.0 69.8 %collective-permute-start.2 = (bf16[2,128,1024]{1,2,0:T(8,128)(2,1)S(1)}, bf16[2,128,1024]{1,2,0:T(8,128)(2,1)S(1)}, u32[]{:S(2)}, u32[]{:S(2)}) collective-permute-start(bf16[2,128,1024]{1,2,0:T(8,128)(2,1)S(1)} %all_gather.3), channel_id=1, source_target_pairs={{0,6},{1,7},{2,8},{3,9},{4,10},{5,11},{6,12},{7,13},{8,14},{9,15},... | collective-permute-start | bytes 1572872 | tf_op jit(solution)/shard_map/ppermute | solution.py:20
  22.9 90.0 %collective-permute-start.3 = (bf16[2,128,1024]{1,2,0:T(8,128)(2,1)S(1)}, bf16[2,128,1024]{1,2,0:T(8,128)(2,1)S(1)}, u32[]{:S(2)}, u32[]{:S(2)}) collective-permute-start(bf16[2,128,1024]{1,2,0:T(8,128)(2,1)S(1)} %all_gather.3), channel_id=1, source_target_pairs={{0,5},{1,6},{2,7},{3,8},{4,9},{5,10},{6,11},{7,12},{8,13},{9,14},{... | collective-permute-start | bytes 1572872 | tf_op jit(solution)/shard_map/ppermute | solution.py:20
  24.9 88.2 %collective-permute-start.4 = (bf16[2,128,1024]{1,2,0:T(8,128)(2,1)S(1)}, bf16[2,128,1024]{1,2,0:T(8,128)(2,1)S(1)}, u32[]{:S(2)}, u32[]{:S(2)}) collective-permute-start(bf16[2,128,1024]{1,2,0:T(8,128)(2,1)S(1)} %all_gather.3), channel_id=1, source_target_pairs={{0,4},{1,5},{2,6},{3,7},{4,8},{5,9},{6,10},{7,11},{8,12},{9,13},{1... | collective-permute-start | bytes 1572872 | tf_op jit(solution)/shard_map/ppermute | solution.py:20
  29.5 4.6 %copy-start.1 = (f32[1,64]{1,0:T(1,128)S(1)}, f32[1,64]{1,0:T(1,128)}, u32[]{:S(2)}) copy-start(f32[1,64]{1,0:T(1,128)} %param.8) | copy-start | bytes 772
  29.6 4.6 %copy-start = (s32[16]{0:T(128)S(1)}, s32[16]{0:T(128)}, u32[]{:S(2)}) copy-start(s32[16]{0:T(128)} %param.9) | copy-start | bytes 196
  47.1 72.9 %collective-permute-start.5 = (bf16[2,128,1024]{1,2,0:T(8,128)(2,1)S(1)}, bf16[2,128,1024]{1,2,0:T(8,128)(2,1)S(1)}, u32[]{:S(2)}, u32[]{:S(2)}) collective-permute-start(bf16[2,128,1024]{1,2,0:T(8,128)(2,1)S(1)} %all_gather.3), channel_id=1, source_target_pairs={{0,3},{1,4},{2,5},{3,6},{4,7},{5,8},{6,9},{7,10},{8,11},{9,12},{10... | collective-permute-start | bytes 1572872 | tf_op jit(solution)/shard_map/ppermute | solution.py:20
  66.7 68.0 %collective-permute-start.6 = (bf16[2,128,1024]{1,2,0:T(8,128)(2,1)S(1)}, bf16[2,128,1024]{1,2,0:T(8,128)(2,1)S(1)}, u32[]{:S(2)}, u32[]{:S(2)}) collective-permute-start(bf16[2,128,1024]{1,2,0:T(8,128)(2,1)S(1)} %all_gather.3), channel_id=1, source_target_pairs={{0,2},{1,3},{2,4},{3,5},{4,6},{5,7},{6,8},{7,9},{8,10},{9,11},{10,... | collective-permute-start | bytes 1572872 | tf_op jit(solution)/shard_map/ppermute | solution.py:20
  90.8 75.9 %collective-permute-start.7 = (bf16[2,128,1024]{1,2,0:T(8,128)(2,1)S(1)}, bf16[2,128,1024]{1,2,0:T(8,128)(2,1)S(1)}, u32[]{:S(2)}, u32[]{:S(2)}) collective-permute-start(bf16[2,128,1024]{1,2,0:T(8,128)(2,1)S(1)} %all_gather.3), channel_id=1, source_target_pairs={{0,1},{1,2},{2,3},{3,4},{4,5},{5,6},{6,7},{7,8},{8,9},{9,10},{10,1... | collective-permute-start | bytes 1572872 | tf_op jit(solution)/shard_map/ppermute | solution.py:20
where the time goes:
time: 223 us; the launch traced here: 222 us
  waiting for transfers between devices  112 us (50%)
  matrix products  37.5 us (17%)
  other arithmetic  25.7 us (12%)
  starting transfers between devices  18.1 us (8%)
  local copies, waits for them, and re-layouts  15.5 us (7%)
  blocking collectives  13.6 us (6%)
    ppermute x8, waiting for transfers between devices, passed_along(): lax.ppermute(value, axis, [(source, source + steps) for source in range(f...  112 us
    dot_general x8, matrix products, per_group(): jnp.einsum('rgw,wd->rgd', weights, v_part, preferred_element_type=jnp.flo...  20.8 us
    ppermute x8, starting transfers between devices, passed_along(): lax.ppermute(value, axis, [(source, source + steps) for source in range(f...  18.1 us
    dot_general x8, matrix products, per_group(): jnp.einsum('rgd,wd->rgw', q_part, k_part, preferred_element_type=jnp.floa...  16.7 us
    all_gather x1, blocking collectives, on_device(): whole = lax.all_gather(keys_values, 'cand', axis=2, tiled=True)  13.6 us
    another operation x4, other arithmetic  9.14 us
    reduce_sum x8, other arithmetic, per_group(): total = jnp.sum(expw, axis=-1, keepdims=True)  8.08 us
    slice x1, local copies, waits for them, and re-layouts, rotate(): first_half = shaped[..., :half_dim]  4.58 us
  transfers between devices with their start and end apart: 8, of which 6 were waited for; matrix products, arithmetic and copies ran while one was open for 10% of the time, Pallas kernels for 0%

commit v1 on v0

v1 whole, which is shorter than its diff:
```python
import math

import jax
import jax.numpy as jnp
from jax import lax
from jax.sharding import PartitionSpec as P

H = 64
KVH = 8
HD = 128
SPAN = 8


ROPE_BASE = 500000.0


def passed_along(value, axis, steps):
    count = lax.axis_size(axis)
    first, last = (max(0, -steps), min(count, count - steps))
    return lax.ppermute(value, axis, [(source, source + steps) for source in range(first, last)])


def locate(index_rows, lengths):
    ends = jnp.cumsum(lengths)
    starts = ends - lengths
    docid = jnp.sum((index_rows[:, None] >= ends[None, :]).astype(jnp.int32), axis=1)
    onehot = docid[:, None] == jnp.arange(lengths.shape[0], dtype=jnp.int32)[None, :]
    first_row = jnp.sum(jnp.where(onehot, starts[None, :], 0), axis=1)
    valid = index_rows >= 0
    return (jnp.where(valid, docid, -1), jnp.where(valid, index_rows - first_row, 0))


def rotate(values, offsets, factor):
    row_count = values.shape[0]
    heads_here = values.shape[1] // HD
    half_dim = HD // 2
    shaped = values.reshape(row_count, heads_here, HD).astype(jnp.float32)
    inverse = jnp.power(ROPE_BASE, -2.0 * jnp.arange(half_dim, dtype=jnp.float32) / HD) / factor
    angles = offsets.astype(jnp.float32)[:, None] * inverse[None, :]
    cosine = jnp.cos(angles)[:, None, :]
    sine = jnp.sin(angles)[:, None, :]
    first_half = shaped[..., :half_dim]
    second_half = shaped[..., half_dim:]
    turned = jnp.concatenate(
        [first_half * cosine - second_half * sine, second_half * cosine + first_half * sine],
        axis=-1,
    )
    return turned.reshape(row_count, heads_here * HD).astype(jnp.bfloat16)


def attend_group(query_rot, key_rot, value_rows, allowed):
    row_count = query_rot.shape[0]
    group_size = H // KVH
    q_part = query_rot.reshape(row_count, group_size, HD)
    scale = 1.0 / math.sqrt(HD)
    scores = jnp.einsum("rgd,wd->rgw", q_part, key_rot, preferred_element_type=jnp.float32) * scale
    scores = jnp.where(allowed[:, None, :], scores, -1e30)
    largest = jnp.max(scores, axis=-1, keepdims=True)
    expw = jnp.exp(scores - largest)
    total = jnp.sum(expw, axis=-1, keepdims=True)
    weights = expw.astype(jnp.bfloat16)
    numer = jnp.einsum("rgw,wd->rgd", weights, value_rows, preferred_element_type=jnp.float32)
    return (numer / total).astype(jnp.bfloat16).reshape(row_count, group_size * HD)


def on_device(queries, keys_values, factors, lengths):
    row_count = queries.shape[0]
    group_width = queries.shape[1] // KVH
    device = lax.axis_index("doc")
    group = lax.axis_index("cand")
    query_index = device * row_count + jnp.arange(row_count, dtype=jnp.int32)
    key_index = (device - SPAN) * row_count + jnp.arange((SPAN + 1) * row_count, dtype=jnp.int32)
    every_factor = lax.all_gather(factors, "cand", axis=0, tiled=True)
    pieces = []
    for distance in range(SPAN, 0, -1):
        pieces.append(passed_along(keys_values, "doc", distance))
    pieces.append(keys_values)
    window = jnp.concatenate(pieces, axis=1)
    query_doc, query_offset = locate(query_index, lengths)
    key_doc, key_offset = locate(key_index, lengths)
    allowed = (
        (key_doc[None, :] == query_doc[:, None])
        & (key_index[None, :] <= query_index[:, None])
        & (key_doc[None, :] >= 0)
    )
    own_queries = lax.dynamic_slice_in_dim(queries, group * group_width, group_width, 1)

    def per_candidate(factor):
        query_rot = rotate(own_queries, query_offset, factor)
        key_rot = rotate(window[0], key_offset, factor)
        return attend_group(query_rot, key_rot, window[1], allowed)

    mixed = lax.map(per_candidate, every_factor)
    return lax.all_to_all(mixed, "cand", 0, 2, tiled=True)


def solution(mesh):
    placed = (P("doc", None), P(None, "doc", "cand"), P("cand", None), P())
    return jax.shard_map(
        on_device, mesh=mesh, in_specs=placed, out_specs=P("cand", "doc", None), check_vma=False
    )
```

time: 223 us -> 208 us (0.933)
  the two profiles are of different devices: /device:TPU:448 before, /device:TPU:32 now
where the time goes in v1:
time: 208 us; the launch traced here: 206 us
  other arithmetic  62.6 us (30%)
  blocking collectives  43.4 us (21%)
  starting transfers between devices  37.1 us (18%)
  local copies, waits for them, and re-layouts  29.7 us (14%)
  matrix products  26.4 us (13%)
  waiting for transfers between devices  6.2 us (3%)
    ppermute x8, starting transfers between devices, passed_along(): lax.ppermute(value, axis, [(source, source + steps) for source in range(f...  37.1 us
    all_to_all x1, blocking collectives, on_device(): return lax.all_to_all(mixed, 'cand', 0, 2, tiled=True)  31.8 us
    another operation x26, other arithmetic  28.7 us
    dot_general x8, matrix products, attend_group(): jnp.einsum('rgd,wd->rgw', q_part, key_rot, preferred_element_type=jnp.flo...  18.1 us
    all_gather x1, blocking collectives, on_device(): every_factor = lax.all_gather(factors, 'cand', axis=0, tiled=True)  11.5 us
    while x80, local copies, waits for them, and re-layouts  10.9 us
    dot_general x8, matrix products, attend_group(): jnp.einsum('rgw,wd->rgd', weights, value_rows, preferred_element_type=jnp...  8.29 us
    reduce_sum x8, other arithmetic, attend_group(): total = jnp.sum(expw, axis=-1, keepdims=True)  8.04 us
  transfers between devices with their start and end apart: 8, of which 2 were waited for; matrix products, arithmetic and copies ran while one was open for 2% of the time, Pallas kernels for 0%

profile of v1, /device:TPU:32, one launch (start us, length us, event | category | flops | bytes accessed | tf_op | source)
XLA Modules:
  0.0 206.3 jit_solution(13450548175812455790)
XLA Ops:
  0.0 1.1 copy.37
  1.1 5.2 %collective-permute-start = (bf16[2,128,128]{1,2,0:T(8,128)(2,1)S(1)}, bf16[2,128,128]{1,2,0:T(8,128)(2,1)S(1)}, u32[]{:S(2)}, u32[]{:S(2)}) collective-permute-start(bf16[2,128,128]{1,2,0:T(8,128)(2,1)S(1)} %copy.37), channel_id=1, source_target_pairs={{0,8},{1,9},{2,10},{3,11},{4,12},{5,13},{6,14},{7,15},{8,16},{9,17... | collective-permute-start | bytes 196616 | tf_op jit(solution)/shard_map/ppermute | solution.py:20
  6.3 7.2 %collective-permute-start.1 = (bf16[2,128,128]{1,2,0:T(8,128)(2,1)S(1)}, bf16[2,128,128]{1,2,0:T(8,128)(2,1)S(1)}, u32[]{:S(2)}, u32[]{:S(2)}) collective-permute-start(bf16[2,128,128]{1,2,0:T(8,128)(2,1)S(1)} %copy.37), channel_id=1, source_target_pairs={{0,7},{1,8},{2,9},{3,10},{4,11},{5,12},{6,13},{7,14},{8,15},{9,16}... | collective-permute-start | bytes 196616 | tf_op jit(solution)/shard_map/ppermute | solution.py:20
  13.5 5.4 %collective-permute-start.2 = (bf16[2,128,128]{1,2,0:T(8,128)(2,1)S(1)}, bf16[2,128,128]{1,2,0:T(8,128)(2,1)S(1)}, u32[]{:S(2)}, u32[]{:S(2)}) collective-permute-start(bf16[2,128,128]{1,2,0:T(8,128)(2,1)S(1)} %copy.37), channel_id=1, source_target_pairs={{0,6},{1,7},{2,8},{3,9},{4,10},{5,11},{6,12},{7,13},{8,14},{9,15},... | collective-permute-start | bytes 196616 | tf_op jit(solution)/shard_map/ppermute | solution.py:20
  19.0 4.1 %collective-permute-start.3 = (bf16[2,128,128]{1,2,0:T(8,128)(2,1)S(1)}, bf16[2,128,128]{1,2,0:T(8,128)(2,1)S(1)}, u32[]{:S(2)}, u32[]{:S(2)}) collective-permute-start(bf16[2,128,128]{1,2,0:T(8,128)(2,1)S(1)} %copy.37), channel_id=1, source_target_pairs={{0,5},{1,6},{2,7},{3,8},{4,9},{5,10},{6,11},{7,12},{8,13},{9,14},{... | collective-permute-start | bytes 196616 | tf_op jit(solution)/shard_map/ppermute | solution.py:20
  23.1 5.0 %collective-permute-start.4 = (bf16[2,128,128]{1,2,0:T(8,128)(2,1)S(1)}, bf16[2,128,128]{1,2,0:T(8,128)(2,1)S(1)}, u32[]{:S(2)}, u32[]{:S(2)}) collective-permute-start(bf16[2,128,128]{1,2,0:T(8,128)(2,1)S(1)} %copy.37), channel_id=1, source_target_pairs={{0,4},{1,5},{2,6},{3,7},{4,8},{5,9},{6,10},{7,11},{8,12},{9,13},{1... | collective-permute-start | bytes 196616 | tf_op jit(solution)/shard_map/ppermute | solution.py:20
  32.0 11.5 %all-gather = f32[8,1,64]{2,1,0:T(1,128)} all-gather(f32[1,1,64]{2,1,0:T(1,128)} %bitcast.51), channel_id=1, replica_groups=mesh['cand'=8,'doc'=64] {'cand'}, dimensions={0}, use_global_device_ids=true | all-gather | bytes 2304 | tf_op jit(solution)/shard_map/all_gather | solution.py:73
  43.6 4.7 %collective-permute-start.5 = (bf16[2,128,128]{1,2,0:T(8,128)(2,1)S(1)}, bf16[2,128,128]{1,2,0:T(8,128)(2,1)S(1)}, u32[]{:S(2)}, u32[]{:S(2)}) collective-permute-start(bf16[2,128,128]{1,2,0:T(8,128)(2,1)S(1)} %copy.37), channel_id=1, source_target_pairs={{0,3},{1,4},{2,5},{3,6},{4,7},{5,8},{6,9},{7,10},{8,11},{9,12},{10... | collective-permute-start | bytes 196616 | tf_op jit(solution)/shard_map/ppermute | solution.py:20
  48.3 3.4 %collective-permute-start.6 = (bf16[2,128,128]{1,2,0:T(8,128)(2,1)S(1)}, bf16[2,128,128]{1,2,0:T(8,128)(2,1)S(1)}, u32[]{:S(2)}, u32[]{:S(2)}) collective-permute-start(bf16[2,128,128]{1,2,0:T(8,128)(2,1)S(1)} %copy.37), channel_id=1, source_target_pairs={{0,2},{1,3},{2,4},{3,5},{4,6},{5,7},{6,8},{7,9},{8,10},{9,11},{10,... | collective-permute-start | bytes 196616 | tf_op jit(solution)/shard_map/ppermute | solution.py:20
  51.8 1.9 collective-permute-start.7
  53.9 3.0 %collective-permute-done.6 = bf16[2,128,128]{1,2,0:T(8,128)(2,1)S(1)} collective-permute-done((bf16[2,128,128]{1,2,0:T(8,128)(2,1)S(1)}, bf16[2,128,128]{1,2,0:T(8,128)(2,1)S(1)}, u32[]{:S(2)}, u32[]{:S(2)}) %collective-permute-start.6) | collective-permute-done | bytes 65568 | tf_op jit(solution)/shard_map/ppermute | solution.py:20
  56.9 3.1 %collective-permute-done.7 = bf16[2,128,128]{1,2,0:T(8,128)(2,1)S(1)} collective-permute-done((bf16[2,128,128]{1,2,0:T(8,128)(2,1)S(1)}, bf16[2,128,128]{1,2,0:T(8,128)(2,1)S(1)}, u32[]{:S(2)}, u32[]{:S(2)}) %collective-permute-start.7) | collective-permute-done | bytes 65568 | tf_op jit(solution)/shard_map/ppermute | solution.py:20
  60.9 109.5 %while.13 = (s32[]{:T(128)}, bf16[8,128,1024]{1,2,0:T(8,128)(2,1)}, bf16[128,1024]{0,1:T(8,128)(2,1)S(1)}, f32[128,1]{0,1:T(1,128)S(1)}, f32[8,64]{1,0:T(8,128)}...) while((s32[]{:T(128)}, bf16[8,128,1024]{1,2,0:T(8,128)(2,1)}, ...), condition=%wide.region_8.9_spmd.clone, body=%wide.region_5.8_spmd.clone.sunk | while | flops 615544960 | bytes 23285628 | solution.py:93
  62.9 1.1 copy.56
  64.1 0.9 subtract_convert_fusion.2
  65.0 1.0 bitcast_convert_fusion.2
  66.7 1.9 fusion.47
  69.5 2.3 %fusion.49 = (f32[128,8]{0,1:T(8,128)S(1)}, f32[128,8,1152]{2,0,1:T(8,128)S(1)}) fusion(bf16[1152,1,64]{0,2,1:T(8,128)(2,1)S(1)} %get-tuple-element.261, bf16[1152,1,64]{0,2,1:T(8,128)(2,1)S(1)} %get-tuple-element.262, bf16[128,8,64]{2,0,1:T(8,128)(2,1)} %get-tuple-element.267, bf16[128,8,64]{2,0,1:T(8,128)(2,1)} %get-tuple-element.268, ...), kind=kOutput, calls=%fused_computation.66.clone.1 | convolution fusion | flops 306641920 | bytes 5427200 | tf_op jit(solution)/shard_map/while/body/eval_jaxpr/rgd,wd->rgw/dot_general | solution.py:56
  71.8 1.0 fusion.50
  72.8 1.0 fusion.51
  76.6 1.1 copy.56
  78.7 1.0 bitcast_convert_fusion.2
  80.4 1.9 fusion.47
  83.2 2.3 %fusion.49 = (f32[128,8]{0,1:T(8,128)S(1)}, f32[128,8,1152]{2,0,1:T(8,128)S(1)}) fusion(bf16[1152,1,64]{0,2,1:T(8,128)(2,1)S(1)} %get-tuple-element.261, bf16[1152,1,64]{0,2,1:T(8,128)(2,1)S(1)} %get-tuple-element.262, bf16[128,8,64]{2,0,1:T(8,128)(2,1)} %get-tuple-element.267, bf16[128,8,64]{2,0,1:T(8,128)(2,1)} %get-tuple-element.268, ...), kind=kOutput, calls=%fused_computation.66.clone.1 | convolution fusion | flops 306641920 | bytes 5427200 | tf_op jit(solution)/shard_map/while/body/eval_jaxpr/rgd,wd->rgw/dot_general | solution.py:56
  85.5 1.0 fusion.50
  86.5 1.0 fusion.51
  90.3 1.1 copy.56
  92.4 1.0 bitcast_convert_fusion.2
  94.1 1.9 fusion.47
  96.9 2.3 %fusion.49 = (f32[128,8]{0,1:T(8,128)S(1)}, f32[128,8,1152]{2,0,1:T(8,128)S(1)}) fusion(bf16[1152,1,64]{0,2,1:T(8,128)(2,1)S(1)} %get-tuple-element.261, bf16[1152,1,64]{0,2,1:T(8,128)(2,1)S(1)} %get-tuple-element.262, bf16[128,8,64]{2,0,1:T(8,128)(2,1)} %get-tuple-element.267, bf16[128,8,64]{2,0,1:T(8,128)(2,1)} %get-tuple-element.268, ...), kind=kOutput, calls=%fused_computation.66.clone.1 | convolution fusion | flops 306641920 | bytes 5427200 | tf_op jit(solution)/shard_map/while/body/eval_jaxpr/rgd,wd->rgw/dot_general | solution.py:56
  99.2 1.0 fusion.50
  100.2 1.0 fusion.51
  104.0 1.1 copy.56
  106.0 1.0 bitcast_convert_fusion.2
  107.8 1.9 fusion.47
  110.6 2.3 %fusion.49 = (f32[128,8]{0,1:T(8,128)S(1)}, f32[128,8,1152]{2,0,1:T(8,128)S(1)}) fusion(bf16[1152,1,64]{0,2,1:T(8,128)(2,1)S(1)} %get-tuple-element.261, bf16[1152,1,64]{0,2,1:T(8,128)(2,1)S(1)} %get-tuple-element.262, bf16[128,8,64]{2,0,1:T(8,128)(2,1)} %get-tuple-element.267, bf16[128,8,64]{2,0,1:T(8,128)(2,1)} %get-tuple-element.268, ...), kind=kOutput, calls=%fused_computation.66.clone.1 | convolution fusion | flops 306641920 | bytes 5427200 | tf_op jit(solution)/shard_map/while/body/eval_jaxpr/rgd,wd->rgw/dot_general | solution.py:56
  112.9 1.0 fusion.50
  113.9 1.0 fusion.51
  117.6 1.1 copy.56
  119.7 1.0 bitcast_convert_fusion.2
  121.4 1.9 fusion.47
  124.3 2.3 %fusion.49 = (f32[128,8]{0,1:T(8,128)S(1)}, f32[128,8,1152]{2,0,1:T(8,128)S(1)}) fusion(bf16[1152,1,64]{0,2,1:T(8,128)(2,1)S(1)} %get-tuple-element.261, bf16[1152,1,64]{0,2,1:T(8,128)(2,1)S(1)} %get-tuple-element.262, bf16[128,8,64]{2,0,1:T(8,128)(2,1)} %get-tuple-element.267, bf16[128,8,64]{2,0,1:T(8,128)(2,1)} %get-tuple-element.268, ...), kind=kOutput, calls=%fused_computation.66.clone.1 | convolution fusion | flops 306641920 | bytes 5427200 | tf_op jit(solution)/shard_map/while/body/eval_jaxpr/rgd,wd->rgw/dot_general | solution.py:56
  126.6 1.0 fusion.50
  127.6 1.0 fusion.51
  131.3 1.1 copy.56
  133.4 1.0 bitcast_convert_fusion.2
  135.1 1.9 fusion.47
  138.0 2.3 %fusion.49 = (f32[128,8]{0,1:T(8,128)S(1)}, f32[128,8,1152]{2,0,1:T(8,128)S(1)}) fusion(bf16[1152,1,64]{0,2,1:T(8,128)(2,1)S(1)} %get-tuple-element.261, bf16[1152,1,64]{0,2,1:T(8,128)(2,1)S(1)} %get-tuple-element.262, bf16[128,8,64]{2,0,1:T(8,128)(2,1)} %get-tuple-element.267, bf16[128,8,64]{2,0,1:T(8,128)(2,1)} %get-tuple-element.268, ...), kind=kOutput, calls=%fused_computation.66.clone.1 | convolution fusion | flops 306641920 | bytes 5427200 | tf_op jit(solution)/shard_map/while/body/eval_jaxpr/rgd,wd->rgw/dot_general | solution.py:56
  140.2 1.0 fusion.50
  141.3 1.0 fusion.51
  145.0 1.1 copy.56
  147.1 1.0 bitcast_convert_fusion.2
  148.8 1.9 fusion.47
  151.6 2.3 %fusion.49 = (f32[128,8]{0,1:T(8,128)S(1)}, f32[128,8,1152]{2,0,1:T(8,128)S(1)}) fusion(bf16[1152,1,64]{0,2,1:T(8,128)(2,1)S(1)} %get-tuple-element.261, bf16[1152,1,64]{0,2,1:T(8,128)(2,1)S(1)} %get-tuple-element.262, bf16[128,8,64]{2,0,1:T(8,128)(2,1)} %get-tuple-element.267, bf16[128,8,64]{2,0,1:T(8,128)(2,1)} %get-tuple-element.268, ...), kind=kOutput, calls=%fused_computation.66.clone.1 | convolution fusion | flops 306641920 | bytes 5427200 | tf_op jit(solution)/shard_map/while/body/eval_jaxpr/rgd,wd->rgw/dot_general | solution.py:56
  153.9 1.0 fusion.50
  154.9 1.0 fusion.51
  158.7 1.1 copy.56
  160.8 1.0 bitcast_convert_fusion.2
  162.5 1.9 fusion.47
  165.3 2.3 %fusion.49 = (f32[128,8]{0,1:T(8,128)S(1)}, f32[128,8,1152]{2,0,1:T(8,128)S(1)}) fusion(bf16[1152,1,64]{0,2,1:T(8,128)(2,1)S(1)} %get-tuple-element.261, bf16[1152,1,64]{0,2,1:T(8,128)(2,1)S(1)} %get-tuple-element.262, bf16[128,8,64]{2,0,1:T(8,128)(2,1)} %get-tuple-element.267, bf16[128,8,64]{2,0,1:T(8,128)(2,1)} %get-tuple-element.268, ...), kind=kOutput, calls=%fused_computation.66.clone.1 | convolution fusion | flops 306641920 | bytes 5427200 | tf_op jit(solution)/shard_map/while/body/eval_jaxpr/rgd,wd->rgw/dot_general | solution.py:56
  167.6 1.0 fusion.50
  168.6 1.0 fusion.51
  170.4 31.8 %all_to_all.18 = bf16[8,128,1024]{1,2,0:T(8,128)(2,1)} all-to-all(bf16[8,128,1024]{1,2,0:T(8,128)(2,1)} %get-tuple-element.110), channel_id=1, replica_groups=mesh['cand'=8,'doc'=64] {'cand'}, dimensions={0} | all-to-all | bytes 4194304 | tf_op jit(solution)/shard_map/all_to_all | solution.py:94
  202.2 4.1 %copy.48 = bf16[1,128,8192]{2,1,0:T(8,128)(2,1)} copy(bf16[1,128,8192]{1,2,0:T(8,128)(2,1)} %bitcast.47) | data formatting | bytes 4194304 | tf_op jit(solution)/shard_map/all_to_all | solution.py:94
  (165 shorter events, 45.5 us)
Async XLA Ops:
  0.0 31.8 %copy-start = (bf16[128,8192]{1,0:T(8,128)(2,1)S(1)}, bf16[128,8192]{1,0:T(8,128)(2,1)}, u32[]{:S(2)}) copy-start(bf16[128,8192]{1,0:T(8,128)(2,1)} %param.6) | copy-start | bytes 6291460
  1.1 42.5 %collective-permute-start = (bf16[2,128,128]{1,2,0:T(8,128)(2,1)S(1)}, bf16[2,128,128]{1,2,0:T(8,128)(2,1)S(1)}, u32[]{:S(2)}, u32[]{:S(2)}) collective-permute-start(bf16[2,128,128]{1,2,0:T(8,128)(2,1)S(1)} %copy.37), channel_id=1, source_target_pairs={{0,8},{1,9},{2,10},{3,11},{4,12},{5,13},{6,14},{7,15},{8,16},{9,17... | collective-permute-start | bytes 196616 | tf_op jit(solution)/shard_map/ppermute | solution.py:20
  6.3 42.0 %collective-permute-start.1 = (bf16[2,128,128]{1,2,0:T(8,128)(2,1)S(1)}, bf16[2,128,128]{1,2,0:T(8,128)(2,1)S(1)}, u32[]{:S(2)}, u32[]{:S(2)}) collective-permute-start(bf16[2,128,128]{1,2,0:T(8,128)(2,1)S(1)} %copy.37), channel_id=1, source_target_pairs={{0,7},{1,8},{2,9},{3,10},{4,11},{5,12},{6,13},{7,14},{8,15},{9,16}... | collective-permute-start | bytes 196616 | tf_op jit(solution)/shard_map/ppermute | solution.py:20
  13.5 38.3 %collective-permute-start.2 = (bf16[2,128,128]{1,2,0:T(8,128)(2,1)S(1)}, bf16[2,128,128]{1,2,0:T(8,128)(2,1)S(1)}, u32[]{:S(2)}, u32[]{:S(2)}) collective-permute-start(bf16[2,128,128]{1,2,0:T(8,128)(2,1)S(1)} %copy.37), channel_id=1, source_target_pairs={{0,6},{1,7},{2,8},{3,9},{4,10},{5,11},{6,12},{7,13},{8,14},{9,15},... | collective-permute-start | bytes 196616 | tf_op jit(solution)/shard_map/ppermute | solution.py:20
  19.0 34.8 %collective-permute-start.3 = (bf16[2,128,128]{1,2,0:T(8,128)(2,1)S(1)}, bf16[2,128,128]{1,2,0:T(8,128)(2,1)S(1)}, u32[]{:S(2)}, u32[]{:S(2)}) collective-permute-start(bf16[2,128,128]{1,2,0:T(8,128)(2,1)S(1)} %copy.37), channel_id=1, source_target_pairs={{0,5},{1,6},{2,7},{3,8},{4,9},{5,10},{6,11},{7,12},{8,13},{9,14},{... | collective-permute-start | bytes 196616 | tf_op jit(solution)/shard_map/ppermute | solution.py:20
  23.1 30.7 %collective-permute-start.4 = (bf16[2,128,128]{1,2,0:T(8,128)(2,1)S(1)}, bf16[2,128,128]{1,2,0:T(8,128)(2,1)S(1)}, u32[]{:S(2)}, u32[]{:S(2)}) collective-permute-start(bf16[2,128,128]{1,2,0:T(8,128)(2,1)S(1)} %copy.37), channel_id=1, source_target_pairs={{0,4},{1,5},{2,6},{3,7},{4,8},{5,9},{6,10},{7,11},{8,12},{9,13},{1... | collective-permute-start | bytes 196616 | tf_op jit(solution)/shard_map/ppermute | solution.py:20
  30.5 1.3 copy-start.4
  43.6 10.2 %collective-permute-start.5 = (bf16[2,128,128]{1,2,0:T(8,128)(2,1)S(1)}, bf16[2,128,128]{1,2,0:T(8,128)(2,1)S(1)}, u32[]{:S(2)}, u32[]{:S(2)}) collective-permute-start(bf16[2,128,128]{1,2,0:T(8,128)(2,1)S(1)} %copy.37), channel_id=1, source_target_pairs={{0,3},{1,4},{2,5},{3,6},{4,7},{5,8},{6,9},{7,10},{8,11},{9,12},{10... | collective-permute-start | bytes 196616 | tf_op jit(solution)/shard_map/ppermute | solution.py:20
  48.3 8.6 %collective-permute-start.6 = (bf16[2,128,128]{1,2,0:T(8,128)(2,1)S(1)}, bf16[2,128,128]{1,2,0:T(8,128)(2,1)S(1)}, u32[]{:S(2)}, u32[]{:S(2)}) collective-permute-start(bf16[2,128,128]{1,2,0:T(8,128)(2,1)S(1)} %copy.37), channel_id=1, source_target_pairs={{0,2},{1,3},{2,4},{3,5},{4,6},{5,7},{6,8},{7,9},{8,10},{9,11},{10,... | collective-permute-start | bytes 196616 | tf_op jit(solution)/shard_map/ppermute | solution.py:20
  51.8 8.3 %collective-permute-start.7 = (bf16[2,128,128]{1,2,0:T(8,128)(2,1)S(1)}, bf16[2,128,128]{1,2,0:T(8,128)(2,1)S(1)}, u32[]{:S(2)}, u32[]{:S(2)}) collective-permute-start(bf16[2,128,128]{1,2,0:T(8,128)(2,1)S(1)} %copy.37), channel_id=1, source_target_pairs={{0,1},{1,2},{2,3},{3,4},{4,5},{5,6},{6,7},{7,8},{8,9},{9,10},{10,1... | collective-permute-start | bytes 196616 | tf_op jit(solution)/shard_map/ppermute | solution.py:20
  60.1 0.8 copy-start.1
  60.9 1.0 copy-start.5
  61.6 1.1 copy-start.3
  69.5 3.3 %copy-start.2 = (bf16[2,1152,128]{1,2,0:T(8,128)(2,1)S(1)}, bf16[2,1152,128]{1,2,0:T(8,128)(2,1)}, u32[]{:S(2)}) copy-start(bf16[2,1152,128]{1,2,0:T(8,128)(2,1)} %get-tuple-element.304) | copy-start | bytes 1769476 | tf_op jit(solution)/shard_map/while
  71.8 2.8 %copy-start.6 = (f32[128,1]{0,1:T(1,128)S(1)}, f32[128,1]{0,1:T(1,128)}, u32[]{:S(2)}) copy-start(f32[128,1]{0,1:T(1,128)} %copy-done.5) | copy-start | bytes 1540 | tf_op jit(solution)/shard_map/while
  74.6 1.0 copy-start.5
  75.3 1.1 copy-start.3
  83.2 3.3 %copy-start.2 = (bf16[2,1152,128]{1,2,0:T(8,128)(2,1)S(1)}, bf16[2,1152,128]{1,2,0:T(8,128)(2,1)}, u32[]{:S(2)}) copy-start(bf16[2,1152,128]{1,2,0:T(8,128)(2,1)} %get-tuple-element.304) | copy-start | bytes 1769476 | tf_op jit(solution)/shard_map/while
  85.5 2.8 %copy-start.6 = (f32[128,1]{0,1:T(1,128)S(1)}, f32[128,1]{0,1:T(1,128)}, u32[]{:S(2)}) copy-start(f32[128,1]{0,1:T(1,128)} %copy-done.5) | copy-start | bytes 1540 | tf_op jit(solution)/shard_map/while
  88.3 1.0 copy-start.5
  89.0 1.1 copy-start.3
  96.9 3.3 %copy-start.2 = (bf16[2,1152,128]{1,2,0:T(8,128)(2,1)S(1)}, bf16[2,1152,128]{1,2,0:T(8,128)(2,1)}, u32[]{:S(2)}) copy-start(bf16[2,1152,128]{1,2,0:T(8,128)(2,1)} %get-tuple-element.304) | copy-start | bytes 1769476 | tf_op jit(solution)/shard_map/while
  99.2 2.8 %copy-start.6 = (f32[128,1]{0,1:T(1,128)S(1)}, f32[128,1]{0,1:T(1,128)}, u32[]{:S(2)}) copy-start(f32[128,1]{0,1:T(1,128)} %copy-done.5) | copy-start | bytes 1540 | tf_op jit(solution)/shard_map/while
  102.0 1.0 copy-start.5
  102.7 1.1 copy-start.3
  110.6 3.3 %copy-start.2 = (bf16[2,1152,128]{1,2,0:T(8,128)(2,1)S(1)}, bf16[2,1152,128]{1,2,0:T(8,128)(2,1)}, u32[]{:S(2)}) copy-start(bf16[2,1152,128]{1,2,0:T(8,128)(2,1)} %get-tuple-element.304) | copy-start | bytes 1769476 | tf_op jit(solution)/shard_map/while
  112.9 2.8 %copy-start.6 = (f32[128,1]{0,1:T(1,128)S(1)}, f32[128,1]{0,1:T(1,128)}, u32[]{:S(2)}) copy-start(f32[128,1]{0,1:T(1,128)} %copy-done.5) | copy-start | bytes 1540 | tf_op jit(solution)/shard_map/while
  115.7 1.0 copy-start.5
  116.4 1.1 copy-start.3
  124.3 3.3 %copy-start.2 = (bf16[2,1152,128]{1,2,0:T(8,128)(2,1)S(1)}, bf16[2,1152,128]{1,2,0:T(8,128)(2,1)}, u32[]{:S(2)}) copy-start(bf16[2,1152,128]{1,2,0:T(8,128)(2,1)} %get-tuple-element.304) | copy-start | bytes 1769476 | tf_op jit(solution)/shard_map/while
  126.5 2.8 %copy-start.6 = (f32[128,1]{0,1:T(1,128)S(1)}, f32[128,1]{0,1:T(1,128)}, u32[]{:S(2)}) copy-start(f32[128,1]{0,1:T(1,128)} %copy-done.5) | copy-start | bytes 1540 | tf_op jit(solution)/shard_map/while
  129.3 1.0 copy-start.5
  130.0 1.1 copy-start.3
  138.0 3.3 %copy-start.2 = (bf16[2,1152,128]{1,2,0:T(8,128)(2,1)S(1)}, bf16[2,1152,128]{1,2,0:T(8,128)(2,1)}, u32[]{:S(2)}) copy-start(bf16[2,1152,128]{1,2,0:T(8,128)(2,1)} %get-tuple-element.304) | copy-start | bytes 1769476 | tf_op jit(solution)/shard_map/while
  140.2 2.8 %copy-start.6 = (f32[128,1]{0,1:T(1,128)S(1)}, f32[128,1]{0,1:T(1,128)}, u32[]{:S(2)}) copy-start(f32[128,1]{0,1:T(1,128)} %copy-done.5) | copy-start | bytes 1540 | tf_op jit(solution)/shard_map/while
  143.0 1.0 copy-start.5
  143.7 1.1 copy-start.3
  151.6 3.3 %copy-start.2 = (bf16[2,1152,128]{1,2,0:T(8,128)(2,1)S(1)}, bf16[2,1152,128]{1,2,0:T(8,128)(2,1)}, u32[]{:S(2)}) copy-start(bf16[2,1152,128]{1,2,0:T(8,128)(2,1)} %get-tuple-element.304) | copy-start | bytes 1769476 | tf_op jit(solution)/shard_map/while
  153.9 2.8 %copy-start.6 = (f32[128,1]{0,1:T(1,128)S(1)}, f32[128,1]{0,1:T(1,128)}, u32[]{:S(2)}) copy-start(f32[128,1]{0,1:T(1,128)} %copy-done.5) | copy-start | bytes 1540 | tf_op jit(solution)/shard_map/while
  156.7 1.0 copy-start.5
  157.4 1.1 copy-start.3
  165.3 3.3 %copy-start.2 = (bf16[2,1152,128]{1,2,0:T(8,128)(2,1)S(1)}, bf16[2,1152,128]{1,2,0:T(8,128)(2,1)}, u32[]{:S(2)}) copy-start(bf16[2,1152,128]{1,2,0:T(8,128)(2,1)} %get-tuple-element.304) | copy-start | bytes 1769476 | tf_op jit(solution)/shard_map/while
  167.6 2.8 %copy-start.6 = (f32[128,1]{0,1:T(1,128)S(1)}, f32[128,1]{0,1:T(1,128)}, u32[]{:S(2)}) copy-start(f32[128,1]{0,1:T(1,128)} %copy-done.5) | copy-start | bytes 1540 | tf_op jit(solution)/shard_map/while

commit v2 on v1

v2 whole, which is shorter than its diff:
```python
import math

import jax
import jax.numpy as jnp
from jax import lax
from jax.experimental import pallas as pl
from jax.experimental.pallas import tpu as pltpu
from jax.sharding import PartitionSpec as P

H = 64
KVH = 8
HD = 128
SPAN = 8


ROPE_BASE = 500000.0


def passed_along(value, axis, steps):
    count = lax.axis_size(axis)
    first, last = (max(0, -steps), min(count, count - steps))
    return lax.ppermute(value, axis, [(source, source + steps) for source in range(first, last)])


def locate(index_rows, lengths):
    ends = jnp.cumsum(lengths)
    starts = ends - lengths
    docid = jnp.sum((index_rows[:, None] >= ends[None, :]).astype(jnp.int32), axis=1)
    onehot = docid[:, None] == jnp.arange(lengths.shape[0], dtype=jnp.int32)[None, :]
    first_row = jnp.sum(jnp.where(onehot, starts[None, :], 0), axis=1)
    valid = index_rows >= 0
    return (jnp.where(valid, docid, -1), jnp.where(valid, index_rows - first_row, 0))


def rotation_table(offsets, factors):
    half_dim = HD // 2
    inverse = jnp.power(ROPE_BASE, -2.0 * jnp.arange(half_dim, dtype=jnp.float32) / HD) / factors
    angles = offsets.astype(jnp.float32)[None, :, None] * inverse[:, None, :]
    return jnp.concatenate([jnp.cos(angles), jnp.sin(angles)], axis=-1)


def attention_kernel(q_ref, kv_ref, table_ref, bias_ref, out_ref):
    half_dim = HD // 2
    group_size = H // KVH
    query_rows = q_ref.shape[0]
    table = table_ref[0]
    swapped = pltpu.roll(table, half_dim, 1)
    low = lax.broadcasted_iota(jnp.int32, table.shape, 1) < half_dim
    cosine = jnp.where(low, table, swapped)
    sine = jnp.where(low, -swapped, table)
    keys = kv_ref[0].astype(jnp.float32)
    key_rot = (keys * cosine + pltpu.roll(keys, half_dim, 1) * sine).astype(jnp.bfloat16)
    values = kv_ref[1]
    first_query = table.shape[0] - query_rows
    q_cos = cosine[first_query:]
    q_sin = sine[first_query:]
    bias = bias_ref[...]
    scale = 1.0 / math.sqrt(HD)
    for head in range(group_size):
        cols = slice(head * HD, (head + 1) * HD)
        x = q_ref[:, cols].astype(jnp.float32)
        q_rot = (x * q_cos + pltpu.roll(x, half_dim, 1) * q_sin).astype(jnp.bfloat16)
        scores = lax.dot_general(
            q_rot, key_rot, (((1,), (1,)), ((), ())), preferred_element_type=jnp.float32
        )
        scores = scores * scale + bias
        largest = jnp.max(scores, axis=-1, keepdims=True)
        expw = jnp.exp(scores - largest)
        total = jnp.sum(expw, axis=-1, keepdims=True)
        numer = jnp.dot(expw.astype(jnp.bfloat16), values, preferred_element_type=jnp.float32)
        out_ref[0, :, cols] = (numer / total).astype(jnp.bfloat16)


def attend_all(own_queries, window, table, bias):
    cands, key_rows, _ = table.shape
    query_rows, width = own_queries.shape
    heads = width // HD
    flops = cands * heads * 4 * query_rows * key_rows * HD
    return pl.pallas_call(
        attention_kernel,
        out_shape=jax.ShapeDtypeStruct((cands, query_rows, width), jnp.bfloat16),
        grid=(cands,),
        in_specs=[
            pl.BlockSpec((query_rows, width), lambda c: (0, 0)),
            pl.BlockSpec(window.shape, lambda c: (0, 0, 0)),
            pl.BlockSpec((1, key_rows, HD), lambda c: (c, 0, 0)),
            pl.BlockSpec(bias.shape, lambda c: (0, 0)),
        ],
        out_specs=pl.BlockSpec((1, query_rows, width), lambda c: (c, 0, 0)),
        cost_estimate=pl.CostEstimate(
            flops=flops,
            transcendentals=cands * heads * query_rows * key_rows,
            bytes_accessed=table.size * 4 + window.size * 2 + cands * query_rows * width * 2,
        ),
    )(own_queries, window, table, bias)


def on_device(queries, keys_values, factors, lengths):
    row_count = queries.shape[0]
    group_width = queries.shape[1] // KVH
    device = lax.axis_index("doc")
    group = lax.axis_index("cand")
    query_index = device * row_count + jnp.arange(row_count, dtype=jnp.int32)
    key_index = (device - SPAN) * row_count + jnp.arange((SPAN + 1) * row_count, dtype=jnp.int32)
    every_factor = lax.all_gather(factors, "cand", axis=0, tiled=True)
    pieces = []
    for distance in range(SPAN, 0, -1):
        pieces.append(passed_along(keys_values, "doc", distance))
    pieces.append(keys_values)
    window = jnp.concatenate(pieces, axis=1)
    query_doc, _ = locate(query_index, lengths)
    key_doc, key_offset = locate(key_index, lengths)
    allowed = (
        (key_doc[None, :] == query_doc[:, None])
        & (key_index[None, :] <= query_index[:, None])
        & (key_doc[None, :] >= 0)
    )
    bias = jnp.where(allowed, 0.0, -1e30).astype(jnp.float32)
    table = rotation_table(key_offset, every_factor)
    own_queries = lax.dynamic_slice_in_dim(queries, group * group_width, group_width, 1)
    mixed = attend_all(own_queries, window, table, bias)
    return lax.all_to_all(mixed, "cand", 0, 2, tiled=True)


def solution(mesh):
    placed = (P("doc", None), P(None, "doc", "cand"), P("cand", None), P())
    return jax.shard_map(
        on_device, mesh=mesh, in_specs=placed, out_specs=P("cand", "doc", None), check_vma=False
    )
```

time: 208 us -> 150 us (0.72)
  other arithmetic: 62.6 us -> 22.2 us
  Pallas kernels: 0 us -> 30.9 us
  matrix products: 26.4 us -> 0 us
  local copies, waits for them, and re-layouts: 29.7 us -> 10.4 us
    pallas_call x0 -> x1, Pallas kernels: none -> 30.9 us  [attend_all(): pl.pallas_call(attention_kernel, out_shape=jax.ShapeDtypeStruct((cands, q...]
    another operation x26 -> x2, other arithmetic: 28.7 us -> 0.15 us
    dot_general x16 -> x0, matrix products: 26.4 us -> none  [the longest x8 18.1 us: attend_group(): jnp.einsum('rgd,wd->rgw', q_part, key_rot, preferred_element_type=jnp.flo...]
    cos x8 -> x1, other arithmetic: 2.45 us -> 16.6 us  [rotation_table(): return jnp.concatenate([jnp.cos(angles), jnp.sin(angles)], axis=-1)]
    while x80 -> x0, local copies, waits for them, and re-layouts: 10.9 us -> none
    convert_element_type x10 -> x1, other arithmetic: 8.61 us -> 0.01 us  [rotation_table(): angles = offsets.astype(jnp.float32)[None, :, None] * inverse[:, None, :]]
    reduce_sum x8 -> x0, other arithmetic: 8.04 us -> none  [attend_group(): total = jnp.sum(expw, axis=-1, keepdims=True)]
    and x8 -> x0, other arithmetic: 7 us -> none  [on_device(): (key_doc[None, :] == query_doc[:, None]) & (key_index[None, :] <= query_i...]
  transfers between devices with their start and end apart: 8 -> 8, of which waited for: 2 -> 2; matrix products, arithmetic and copies ran while one was open for 2% -> 16% of each run, Pallas kernels for 0% -> 0%
where the time goes in v2:
time: 150 us
  blocking collectives  42.8 us (29%)
  starting transfers between devices  37.4 us (25%)
  Pallas kernels  30.9 us (21%)
  other arithmetic  22.2 us (15%)
  local copies, waits for them, and re-layouts  10.4 us (7%)
  waiting for transfers between devices  6.05 us (4%)
    ppermute x8, starting transfers between devices, passed_along(): lax.ppermute(value, axis, [(source, source + steps) for source in range(f...  37.4 us
    all_to_all x1, blocking collectives, on_device(): return lax.all_to_all(mixed, 'cand', 0, 2, tiled=True)  31.8 us
    pallas_call x1, Pallas kernels, attend_all(): pl.pallas_call(attention_kernel, out_shape=jax.ShapeDtypeStruct((cands, q...  30.9 us
    cos x1, other arithmetic, rotation_table(): return jnp.concatenate([jnp.cos(angles), jnp.sin(angles)], axis=-1)  16.6 us
    all_gather x1, blocking collectives, on_device(): every_factor = lax.all_gather(factors, 'cand', axis=0, tiled=True)  10.9 us
    all_to_all x2, local copies, waits for them, and re-layouts, on_device(): return lax.all_to_all(mixed, 'cand', 0, 2, tiled=True)  7.99 us
    ppermute x8, waiting for transfers between devices, passed_along(): lax.ppermute(value, axis, [(source, source + steps) for source in range(f...  6.05 us
    concatenate x1, other arithmetic, rotation_table(): return jnp.concatenate([jnp.cos(angles), jnp.sin(angles)], axis=-1)  3.41 us
  transfers between devices with their start and end apart: 8, of which 2 were waited for; matrix products, arithmetic and copies ran while one was open for 16% of the time, Pallas kernels for 0%

profile of v2, /device:TPU:32, one launch (start us, length us, event | category | flops | bytes accessed | tf_op | source)
XLA Modules:
  0.0 149.9 jit_solution(17619031420701379824)
XLA Ops:
  0.0 0.0 copy-start
  0.0 5.3 %collective-permute-start = (bf16[2,128,128]{2,1,0:T(8,128)(2,1)}, bf16[2,128,128]{2,1,0:T(8,128)(2,1)S(1)}, u32[]{:S(2)}, u32[]{:S(2)}) collective-permute-start(bf16[2,128,128]{2,1,0:T(8,128)(2,1)} %param.5), channel_id=1, source_target_pairs={{0,8},{1,9},{2,10},{3,11},{4,12},{5,13},{6,14},{7,15},{8,16},{9,17... | collective-permute-start | bytes 196616 | tf_op jit(solution)/shard_map/ppermute | solution.py:22
  5.3 7.2 %collective-permute-start.1 = (bf16[2,128,128]{2,1,0:T(8,128)(2,1)}, bf16[2,128,128]{2,1,0:T(8,128)(2,1)S(1)}, u32[]{:S(2)}, u32[]{:S(2)}) collective-permute-start(bf16[2,128,128]{2,1,0:T(8,128)(2,1)} %param.5), channel_id=1, source_target_pairs={{0,7},{1,8},{2,9},{3,10},{4,11},{5,12},{6,13},{7,14},{8,15},{9,16}... | collective-permute-start | bytes 196616 | tf_op jit(solution)/shard_map/ppermute | solution.py:22
  12.6 5.4 %collective-permute-start.2 = (bf16[2,128,128]{2,1,0:T(8,128)(2,1)}, bf16[2,128,128]{2,1,0:T(8,128)(2,1)S(1)}, u32[]{:S(2)}, u32[]{:S(2)}) collective-permute-start(bf16[2,128,128]{2,1,0:T(8,128)(2,1)} %param.5), channel_id=1, source_target_pairs={{0,6},{1,7},{2,8},{3,9},{4,10},{5,11},{6,12},{7,13},{8,14},{9,15},... | collective-permute-start | bytes 196616 | tf_op jit(solution)/shard_map/ppermute | solution.py:22
  18.0 4.2 %collective-permute-start.3 = (bf16[2,128,128]{2,1,0:T(8,128)(2,1)}, bf16[2,128,128]{2,1,0:T(8,128)(2,1)S(1)}, u32[]{:S(2)}, u32[]{:S(2)}) collective-permute-start(bf16[2,128,128]{2,1,0:T(8,128)(2,1)} %param.5), channel_id=1, source_target_pairs={{0,5},{1,6},{2,7},{3,8},{4,9},{5,10},{6,11},{7,12},{8,13},{9,14},{... | collective-permute-start | bytes 196616 | tf_op jit(solution)/shard_map/ppermute | solution.py:22
  22.1 5.0 %collective-permute-start.4 = (bf16[2,128,128]{2,1,0:T(8,128)(2,1)}, bf16[2,128,128]{2,1,0:T(8,128)(2,1)S(1)}, u32[]{:S(2)}, u32[]{:S(2)}) collective-permute-start(bf16[2,128,128]{2,1,0:T(8,128)(2,1)} %param.5), channel_id=1, source_target_pairs={{0,4},{1,5},{2,6},{3,7},{4,8},{5,9},{6,10},{7,11},{8,12},{9,13},{1... | collective-permute-start | bytes 196616 | tf_op jit(solution)/shard_map/ppermute | solution.py:22
  27.2 0.7 copy.12
  28.0 0.1 reduce
  28.1 0.7 sub.14
  28.8 0.1 convert_reduce_fusion
  28.9 0.1 convert_reduce_fusion.1
  29.0 0.1 select_reduce_fusion
  29.1 10.9 %all-gather = f32[8,1,64]{2,1,0:T(1,128)S(1)} all-gather(f32[1,1,64]{2,1,0:T(1,128)} %bitcast.11), channel_id=1, replica_groups=mesh['cand'=8,'doc'=64] {'cand'}, dimensions={0}, use_global_device_ids=true | all-gather | bytes 2304 | tf_op jit(solution)/shard_map/all_gather | solution.py:105
  40.0 16.6 %multiply_cosine_fusion = (f32[8,1152,64]{2,1,0:T(8,128)S(1)}, f32[8,1152,64]{2,1,0:T(8,128)S(1)}) fusion(f32[8,64]{1,0:T(8,128)S(1)} %broadcast_divide_fusion, f32[1152]{0:T(1024)S(1)} %select_convert_fusion), kind=kLoop, calls=%fused_computation.1 | loop fusion | flops 589824 | bytes 4725248 | tf_op jit(solution)/shard_map/cos | solution.py:39
  56.6 0.0 copy-start.1
  56.6 3.4 %pad_maximum_fusion.table_ref = f32[8,1152,128]{2,1,0:T(8,128)} fusion(f32[8,1152,64]{2,1,0:T(8,128)S(1)} %get-tuple-element.8, f32[8,1152,64]{2,1,0:T(8,128)S(1)} %get-tuple-element.7), kind=kLoop, calls=%fused_computation.2 | loop fusion | flops 1179648 | bytes 9437184 | tf_op jit(solution)/shard_map/concatenate | solution.py:39
  60.0 1.0 and_select_fusion.bias_ref
  61.1 0.0 copy-done
  61.1 0.7 constant_dynamic-slice_fusion.q_ref
  61.8 0.0 collective-permute-done
  61.8 0.0 copy-done.1
  61.8 4.7 %collective-permute-start.5 = (bf16[2,128,128]{2,1,0:T(8,128)(2,1)S(1)}, bf16[2,128,128]{2,1,0:T(8,128)(2,1)S(1)}, u32[]{:S(2)}, u32[]{:S(2)}) collective-permute-start(bf16[2,128,128]{2,1,0:T(8,128)(2,1)S(1)} %copy-done.1), channel_id=1, source_target_pairs={{0,3},{1,4},{2,5},{3,6},{4,7},{5,8},{6,9},{7,10},{8,11},{9,12},{10... | collective-permute-start | bytes 196616 | tf_op jit(solution)/shard_map/ppermute | solution.py:22
  66.5 0.0 collective-permute-done.1
  66.5 3.4 %collective-permute-start.6 = (bf16[2,128,128]{2,1,0:T(8,128)(2,1)S(1)}, bf16[2,128,128]{2,1,0:T(8,128)(2,1)S(1)}, u32[]{:S(2)}, u32[]{:S(2)}) collective-permute-start(bf16[2,128,128]{2,1,0:T(8,128)(2,1)S(1)} %copy-done.1), channel_id=1, source_target_pairs={{0,2},{1,3},{2,4},{3,5},{4,6},{5,7},{6,8},{7,9},{8,10},{9,11},{10,... | collective-permute-start | bytes 196616 | tf_op jit(solution)/shard_map/ppermute | solution.py:22
  70.0 0.0 collective-permute-done.2
  70.0 2.1 %collective-permute-start.7 = (bf16[2,128,128]{2,1,0:T(8,128)(2,1)S(1)}, bf16[2,128,128]{2,1,0:T(8,128)(2,1)S(1)}, u32[]{:S(2)}, u32[]{:S(2)}) collective-permute-start(bf16[2,128,128]{2,1,0:T(8,128)(2,1)S(1)} %copy-done.1), channel_id=1, source_target_pairs={{0,1},{1,2},{2,3},{3,4},{4,5},{5,6},{6,7},{7,8},{8,9},{9,10},{10,1... | collective-permute-start | bytes 196616 | tf_op jit(solution)/shard_map/ppermute | solution.py:22
  72.1 0.0 collective-permute-done.3
  72.2 0.0 collective-permute-done.4
  72.2 0.0 collective-permute-done.5
  72.2 2.9 %collective-permute-done.6 = bf16[2,128,128]{2,1,0:T(8,128)(2,1)S(1)} collective-permute-done((bf16[2,128,128]{2,1,0:T(8,128)(2,1)S(1)}, bf16[2,128,128]{2,1,0:T(8,128)(2,1)S(1)}, u32[]{:S(2)}, u32[]{:S(2)}) %collective-permute-start.6) | collective-permute-done | bytes 65568 | tf_op jit(solution)/shard_map/ppermute | solution.py:22
  75.1 3.1 %collective-permute-done.7 = bf16[2,128,128]{2,1,0:T(8,128)(2,1)S(1)} collective-permute-done((bf16[2,128,128]{2,1,0:T(8,128)(2,1)S(1)}, bf16[2,128,128]{2,1,0:T(8,128)(2,1)S(1)}, u32[]{:S(2)}, u32[]{:S(2)}) %collective-permute-start.7) | collective-permute-done | bytes 65568 | tf_op jit(solution)/shard_map/ppermute | solution.py:22
  78.3 0.0 copy-start.2
  78.3 0.8 copy-done.2
  79.2 30.9 %shard_map.46 = bf16[8,128,1024]{2,1,0:T(8,128)(2,1)} custom-call(bf16[128,1024]{1,0:T(8,128)(2,1)} %constant_dynamic-slice_fusion.q_ref, bf16[2,1152,128]{2,1,0:T(8,128)(2,1)} %copy-done.2, f32[8,1152,128]{2,1,0:T(8,128)} %pad_maximum_fusion.table_ref, f32[128,1152]{1,0:T(8,128)} %and_select_fusion.bias_ref), custom_call_target="tpu_custom_call" | custom-call | flops 4831838208 | bytes 7405568 | tf_op jit(solution)/shard_map/pallas_call | solution.py:79
  110.0 31.8 %all_to_all.18 = bf16[8,128,1024]{2,1,0:T(8,128)(2,1)} all-to-all(bf16[8,128,1024]{2,1,0:T(8,128)(2,1)} %shard_map.46), channel_id=1, replica_groups=mesh['cand'=8,'doc'=64] {'cand'}, dimensions={0} | all-to-all | bytes 4194304 | tf_op jit(solution)/shard_map/all_to_all | solution.py:122
  141.9 3.9 %copy.13 = bf16[1,128,8,1024]{1,3,2,0:T(8,128)(2,1)} copy(bf16[1,128,8,1024]{3,1,2,0:T(8,128)(2,1)} %bitcast.7) | data formatting | bytes 4194304 | tf_op jit(solution)/shard_map/all_to_all | solution.py:122
  145.8 4.1 %copy.14 = bf16[1,128,8192]{2,1,0:T(8,128)(2,1)} copy(bf16[1,128,8192]{1,2,0:T(8,128)(2,1)} %bitcast.8) | data formatting | bytes 4194304 | tf_op jit(solution)/shard_map/all_to_all | solution.py:122
  (17 shorter events, 0.2 us)
Async XLA Ops:
  0.0 61.1 %copy-start = (bf16[128,8192]{1,0:T(8,128)(2,1)S(1)}, bf16[128,8192]{1,0:T(8,128)(2,1)}, u32[]{:S(2)}) copy-start(bf16[128,8192]{1,0:T(8,128)(2,1)} %param.4) | copy-start | bytes 6291460
  0.0 61.8 %collective-permute-start = (bf16[2,128,128]{2,1,0:T(8,128)(2,1)}, bf16[2,128,128]{2,1,0:T(8,128)(2,1)S(1)}, u32[]{:S(2)}, u32[]{:S(2)}) collective-permute-start(bf16[2,128,128]{2,1,0:T(8,128)(2,1)} %param.5), channel_id=1, source_target_pairs={{0,8},{1,9},{2,10},{3,11},{4,12},{5,13},{6,14},{7,15},{8,16},{9,17... | collective-permute-start | bytes 196616 | tf_op jit(solution)/shard_map/ppermute | solution.py:22
  5.3 61.2 %collective-permute-start.1 = (bf16[2,128,128]{2,1,0:T(8,128)(2,1)}, bf16[2,128,128]{2,1,0:T(8,128)(2,1)S(1)}, u32[]{:S(2)}, u32[]{:S(2)}) collective-permute-start(bf16[2,128,128]{2,1,0:T(8,128)(2,1)} %param.5), channel_id=1, source_target_pairs={{0,7},{1,8},{2,9},{3,10},{4,11},{5,12},{6,13},{7,14},{8,15},{9,16}... | collective-permute-start | bytes 196616 | tf_op jit(solution)/shard_map/ppermute | solution.py:22
  12.6 57.5 %collective-permute-start.2 = (bf16[2,128,128]{2,1,0:T(8,128)(2,1)}, bf16[2,128,128]{2,1,0:T(8,128)(2,1)S(1)}, u32[]{:S(2)}, u32[]{:S(2)}) collective-permute-start(bf16[2,128,128]{2,1,0:T(8,128)(2,1)} %param.5), channel_id=1, source_target_pairs={{0,6},{1,7},{2,8},{3,9},{4,10},{5,11},{6,12},{7,13},{8,14},{9,15},... | collective-permute-start | bytes 196616 | tf_op jit(solution)/shard_map/ppermute | solution.py:22
  18.0 54.2 %collective-permute-start.3 = (bf16[2,128,128]{2,1,0:T(8,128)(2,1)}, bf16[2,128,128]{2,1,0:T(8,128)(2,1)S(1)}, u32[]{:S(2)}, u32[]{:S(2)}) collective-permute-start(bf16[2,128,128]{2,1,0:T(8,128)(2,1)} %param.5), channel_id=1, source_target_pairs={{0,5},{1,6},{2,7},{3,8},{4,9},{5,10},{6,11},{7,12},{8,13},{9,14},{... | collective-permute-start | bytes 196616 | tf_op jit(solution)/shard_map/ppermute | solution.py:22
  22.1 50.0 %collective-permute-start.4 = (bf16[2,128,128]{2,1,0:T(8,128)(2,1)}, bf16[2,128,128]{2,1,0:T(8,128)(2,1)S(1)}, u32[]{:S(2)}, u32[]{:S(2)}) collective-permute-start(bf16[2,128,128]{2,1,0:T(8,128)(2,1)} %param.5), channel_id=1, source_target_pairs={{0,4},{1,5},{2,6},{3,7},{4,8},{5,9},{6,10},{7,11},{8,12},{9,13},{1... | collective-permute-start | bytes 196616 | tf_op jit(solution)/shard_map/ppermute | solution.py:22
  56.6 5.2 %copy-start.1 = (bf16[2,128,128]{2,1,0:T(8,128)(2,1)S(1)}, bf16[2,128,128]{2,1,0:T(8,128)(2,1)}, u32[]{:S(2)}) copy-start(bf16[2,128,128]{2,1,0:T(8,128)(2,1)} %param.5) | copy-start | bytes 196612
  61.8 10.4 %collective-permute-start.5 = (bf16[2,128,128]{2,1,0:T(8,128)(2,1)S(1)}, bf16[2,128,128]{2,1,0:T(8,128)(2,1)S(1)}, u32[]{:S(2)}, u32[]{:S(2)}) collective-permute-start(bf16[2,128,128]{2,1,0:T(8,128)(2,1)S(1)} %copy-done.1), channel_id=1, source_target_pairs={{0,3},{1,4},{2,5},{3,6},{4,7},{5,8},{6,9},{7,10},{8,11},{9,12},{10... | collective-permute-start | bytes 196616 | tf_op jit(solution)/shard_map/ppermute | solution.py:22
  66.5 8.6 %collective-permute-start.6 = (bf16[2,128,128]{2,1,0:T(8,128)(2,1)S(1)}, bf16[2,128,128]{2,1,0:T(8,128)(2,1)S(1)}, u32[]{:S(2)}, u32[]{:S(2)}) collective-permute-start(bf16[2,128,128]{2,1,0:T(8,128)(2,1)S(1)} %copy-done.1), channel_id=1, source_target_pairs={{0,2},{1,3},{2,4},{3,5},{4,6},{5,7},{6,8},{7,9},{8,10},{9,11},{10,... | collective-permute-start | bytes 196616 | tf_op jit(solution)/shard_map/ppermute | solution.py:22
  70.0 8.3 %collective-permute-start.7 = (bf16[2,128,128]{2,1,0:T(8,128)(2,1)S(1)}, bf16[2,128,128]{2,1,0:T(8,128)(2,1)S(1)}, u32[]{:S(2)}, u32[]{:S(2)}) collective-permute-start(bf16[2,128,128]{2,1,0:T(8,128)(2,1)S(1)} %copy-done.1), channel_id=1, source_target_pairs={{0,1},{1,2},{2,3},{3,4},{4,5},{5,6},{6,7},{7,8},{8,9},{9,10},{10,1... | collective-permute-start | bytes 196616 | tf_op jit(solution)/shard_map/ppermute | solution.py:22
  78.3 0.8 copy-start.2

commit v3 on v2

--- a/solution.py
+++ b/solution.py
@@ -32,26 +32,39 @@
     return (jnp.where(valid, docid, -1), jnp.where(valid, index_rows - first_row, 0))
 
 
-def rotation_table(offsets, factors):
+def inverse_rows(factors):
     half_dim = HD // 2
     inverse = jnp.power(ROPE_BASE, -2.0 * jnp.arange(half_dim, dtype=jnp.float32) / HD) / factors
-    angles = offsets.astype(jnp.float32)[None, :, None] * inverse[:, None, :]
-    return jnp.concatenate([jnp.cos(angles), jnp.sin(angles)], axis=-1)
+    return jnp.concatenate([inverse, inverse], axis=-1)[:, None, :]
 
 
-def attention_kernel(q_ref, kv_ref, table_ref, bias_ref, out_ref):
+def cos_and_sin(angle, low):
+    turns = jnp.floor(angle * 0.636619772367581343 + 0.5)
+    rest = ((angle - turns * 1.5703125) - turns * 4.837512969970703125e-4) - turns * 7.54978995489188216e-8
+    square = rest * rest
+    sine = rest + rest * square * (-1.6666654611e-1 + square * (8.3321608736e-3 + square * -1.9515295891e-4))
+    cosine = 1.0 - 0.5 * square + square * square * (
+        4.166664568298827e-2 + square * (-1.388731625493765e-3 + square * 2.443315711809948e-5)
+    )
+    quadrant = turns.astype(jnp.int32) + jnp.where(low, 0, 3)
+    base = jnp.where((quadrant & 1) == 1, sine, cosine)
+    return jnp.where(((quadrant + 1) & 2) != 0, -base, base)
+
+
+def attention_kernel(q_ref, kv_ref, offset_ref, inverse_ref, bias_ref, out_ref):
     half_dim = HD // 2
     group_size = H // KVH
     query_rows = q_ref.shape[0]
-    table = table_ref[0]
+    angle = offset_ref[...] * inverse_ref[0]
+    low = lax.broadcasted_iota(jnp.int32, angle.shape, 1) < half_dim
+    table = cos_and_sin(angle, low)
     swapped = pltpu.roll(table, half_dim, 1)
-    low = lax.broadcasted_iota(jnp.int32, table.shape, 1) < half_dim
     cosine = jnp.where(low, table, swapped)
     sine = jnp.where(low, -swapped, table)
     keys = kv_ref[0].astype(jnp.float32)
     key_rot = (keys * cosine + pltpu.roll(keys, half_dim, 1) * sine).astype(jnp.bfloat16)
     values = kv_ref[1]
-    first_query = table.shape[0] - query_rows
+    first_query = angle.shape[0] - query_rows
     q_cos = cosine[first_query:]
     q_sin = sine[first_query:]
     bias = bias_ref[...]
@@ -71,8 +84,9 @@
         out_ref[0, :, cols] = (numer / total).astype(jnp.bfloat16)
 
 
-def attend_all(own_queries, window, table, bias):
-    cands, key_rows, _ = table.shape
+def attend_all(own_queries, window, offsets, inverse, bias):
+    cands = inverse.shape[0]
+    key_rows = window.shape[1]
     query_rows, width = own_queries.shape
     heads = width // HD
     flops = cands * heads * 4 * query_rows * key_rows * HD
@@ -83,16 +97,22 @@
         in_specs=[
             pl.BlockSpec((query_rows, width), lambda c: (0, 0)),
             pl.BlockSpec(window.shape, lambda c: (0, 0, 0)),
-            pl.BlockSpec((1, key_rows, HD), lambda c: (c, 0, 0)),
+            pl.BlockSpec(offsets.shape, lambda c: (0, 0)),
+            pl.BlockSpec((1, 1, HD), lambda c: (c, 0, 0)),
             pl.BlockSpec(bias.shape, lambda c: (0, 0)),
         ],
         out_specs=pl.BlockSpec((1, query_rows, width), lambda c: (c, 0, 0)),
         cost_estimate=pl.CostEstimate(
             flops=flops,
             transcendentals=cands * heads * query_rows * key_rows,
-            bytes_accessed=table.size * 4 + window.size * 2 + cands * query_rows * width * 2,
+            bytes_accessed=window.size * 2 + own_queries.size * 2 + cands * query_rows * width * 2,
         ),
-    )(own_queries, window, table, bias)
+    )(own_queries, window, offsets, inverse, bias)
+
+
+def cyclic_shift(value, axis, steps):
+    count = lax.axis_size(axis)
+    return lax.ppermute(value, axis, [(source, (source + steps) % count) for source in range(count)])
 
 
 def on_device(queries, keys_values, factors, lengths):
@@ -102,12 +122,20 @@
     group = lax.axis_index("cand")
     query_index = device * row_count + jnp.arange(row_count, dtype=jnp.int32)
     key_index = (device - SPAN) * row_count + jnp.arange((SPAN + 1) * row_count, dtype=jnp.int32)
-    every_factor = lax.all_gather(factors, "cand", axis=0, tiled=True)
-    pieces = []
-    for distance in range(SPAN, 0, -1):
-        pieces.append(passed_along(keys_values, "doc", distance))
-    pieces.append(keys_values)
-    window = jnp.concatenate(pieces, axis=1)
+    cands = lax.axis_size("cand")
+    behind = factors
+    reach = 1
+    while reach < cands:
+        behind = jnp.concatenate([behind, cyclic_shift(behind, "cand", reach)], axis=0)
+        reach *= 2
+    every_factor = jnp.take(behind, (group - jnp.arange(cands, dtype=jnp.int32)) % cands, axis=0)
+    far = passed_along(keys_values, "doc", SPAN)
+    window = keys_values
+    reach = 1
+    while reach < SPAN:
+        window = jnp.concatenate([passed_along(window, "doc", reach), window], axis=1)
+        reach *= 2
+    window = jnp.concatenate([far, window], axis=1)
     query_doc, _ = locate(query_index, lengths)
     key_doc, key_offset = locate(key_index, lengths)
     allowed = (
@@ -116,9 +144,9 @@
         & (key_doc[None, :] >= 0)
     )
     bias = jnp.where(allowed, 0.0, -1e30).astype(jnp.float32)
-    table = rotation_table(key_offset, every_factor)
+    offsets = jnp.broadcast_to(key_offset.astype(jnp.float32)[:, None], (key_offset.shape[0], HD))
     own_queries = lax.dynamic_slice_in_dim(queries, group * group_width, group_width, 1)
-    mixed = attend_all(own_queries, window, table, bias)
+    mixed = attend_all(own_queries, window, offsets, inverse_rows(every_factor), bias)
     return lax.all_to_all(mixed, "cand", 0, 2, tiled=True)
 
 

time: 150 us -> 125 us (0.83)
  the two profiles are of different devices: /device:TPU:32 before, /device:TPU:128 now
where the time goes in v3:
time: 125 us; the launch traced here: 124 us
  Pallas kernels  35.9 us (29%)
  blocking collectives  31.8 us (25%)
  starting transfers between devices  22.2 us (18%)
  waiting for transfers between devices  16.3 us (13%)
  local copies, waits for them, and re-layouts  11.1 us (9%)
  other arithmetic  6.67 us (5%)
    pallas_call x1, Pallas kernels, attend_all(): pl.pallas_call(attention_kernel, out_shape=jax.ShapeDtypeStruct((cands, q...  35.9 us
    all_to_all x1, blocking collectives, on_device(): return lax.all_to_all(mixed, 'cand', 0, 2, tiled=True)  31.8 us
    ppermute x4, starting transfers between devices, passed_along(): lax.ppermute(value, axis, [(source, source + steps) for source in range(f...  16 us
    ppermute x4, waiting for transfers between devices, passed_along(): lax.ppermute(value, axis, [(source, source + steps) for source in range(f...  12 us
    all_to_all x2, local copies, waits for them, and re-layouts, on_device(): return lax.all_to_all(mixed, 'cand', 0, 2, tiled=True)  7.99 us
    ppermute x3, starting transfers between devices, cyclic_shift(): lax.ppermute(value, axis, [(source, (source + steps) % count) for source...  6.22 us
    ppermute x3, waiting for transfers between devices, cyclic_shift(): lax.ppermute(value, axis, [(source, (source + steps) % count) for source...  4.33 us
  transfers between devices with their start and end apart: 7, of which 4 were waited for; matrix products, arithmetic and copies ran while one was open for 7% of the time, Pallas kernels for 0%

profile of v3, /device:TPU:128, one launch (start us, length us, event | category | flops | bytes accessed | tf_op | source)
XLA Modules:
  0.0 124.2 jit_solution(17257892843200245695)
XLA Ops:
  0.0 0.0 copy-start
  0.0 0.0 copy-start.1
  0.0 3.5 %collective-permute-start.1 = (bf16[2,128,128]{2,1,0:T(8,128)(2,1)}, bf16[2,128,128]{2,1,0:T(8,128)(2,1)S(1)}, u32[]{:S(2)}, u32[]{:S(2)}) collective-permute-start(bf16[2,128,128]{2,1,0:T(8,128)(2,1)} %param.5), channel_id=1, source_target_pairs={{0,1},{1,2},{2,3},{3,4},{4,5},{5,6},{6,7},{7,8},{8,9},{9,10},{10,1... | collective-permute-start | bytes 196616 | tf_op jit(solution)/shard_map/ppermute | solution.py:22
  3.5 5.2 %collective-permute-start = (bf16[2,128,128]{2,1,0:T(8,128)(2,1)}, bf16[2,128,128]{2,1,0:T(8,128)(2,1)S(1)}, u32[]{:S(2)}, u32[]{:S(2)}) collective-permute-start(bf16[2,128,128]{2,1,0:T(8,128)(2,1)} %param.5), channel_id=1, source_target_pairs={{0,8},{1,9},{2,10},{3,11},{4,12},{5,13},{6,14},{7,15},{8,16},{9,17... | collective-permute-start | bytes 196616 | tf_op jit(solution)/shard_map/ppermute | solution.py:22
  8.7 0.0 collective-permute-start.4
  8.8 0.7 copy.9
  9.6 0.1 reduce
  9.7 0.7 sub.33
  10.4 0.1 convert_reduce_fusion.1
  10.4 0.1 convert_reduce_fusion
  10.6 0.1 select_reduce_fusion
  10.7 0.0 copy-done
  10.7 0.7 constant_dynamic-slice_fusion.q_ref
  11.4 1.1 and_select_fusion.bias_ref
  12.5 0.6 collective-permute-done.4
  13.0 0.7 pad_maximum_fusion.5
  13.7 2.9 %collective-permute-start.5 = (f32[2,64]{1,0:T(2,128)S(1)}, f32[2,64]{1,0:T(2,128)S(1)}, u32[]{:S(2)}, u32[]{:S(2)}) collective-permute-start(f32[2,64]{1,0:T(2,128)S(1)} %pad_maximum_fusion.5), channel_id=1, source_target_pairs={{0,128},{64,192},{128,256},{192,320},{256,384},{320,448},{384,0},{... | collective-permute-start | bytes 1544 | tf_op jit(solution)/shard_map/ppermute | solution.py:115
  16.6 3.7 %collective-permute-done.5 = f32[2,64]{1,0:T(2,128)S(1)} collective-permute-done((f32[2,64]{1,0:T(2,128)S(1)}, f32[2,64]{1,0:T(2,128)S(1)}, u32[]{:S(2)}, u32[]{:S(2)}) %collective-permute-start.5) | collective-permute-done | bytes 544 | tf_op jit(solution)/shard_map/ppermute | solution.py:115
  20.4 0.7 pad_maximum_fusion.4
  21.0 3.3 %collective-permute-start.6 = (f32[4,64]{1,0:T(4,128)S(1)}, f32[4,64]{1,0:T(4,128)S(1)}, u32[]{:S(2)}, u32[]{:S(2)}) collective-permute-start(f32[4,64]{1,0:T(4,128)S(1)} %pad_maximum_fusion.4), channel_id=1, source_target_pairs={{0,256},{64,320},{128,384},{192,448},{256,0},{320,64},{384,128},{4... | collective-permute-start | bytes 3080 | tf_op jit(solution)/shard_map/ppermute | solution.py:115
  24.3 0.0 collective-permute-done.1
  24.4 0.9 pad_maximum_fusion.1
  25.2 4.6 %collective-permute-start.2 = (bf16[2,256,128]{2,1,0:T(8,128)(2,1)S(1)}, bf16[2,256,128]{2,1,0:T(8,128)(2,1)S(1)}, u32[]{:S(2)}, u32[]{:S(2)}) collective-permute-start(bf16[2,256,128]{2,1,0:T(8,128)(2,1)S(1)} %pad_maximum_fusion.1), channel_id=1, source_target_pairs={{0,2},{1,3},{2,4},{3,5},{4,6},{5,7},{6,8},{7,9},{8,10},{9,11},{10,... | collective-permute-start | bytes 393224 | tf_op jit(solution)/shard_map/ppermute | solution.py:22
  29.9 0.0 collective-permute-done.6
  29.9 0.7 pad_maximum_fusion.2
  30.6 0.6 gather_fusion
  31.1 5.0 %collective-permute-done.2 = bf16[2,256,128]{2,1,0:T(8,128)(2,1)S(1)} collective-permute-done((bf16[2,256,128]{2,1,0:T(8,128)(2,1)S(1)}, bf16[2,256,128]{2,1,0:T(8,128)(2,1)S(1)}, u32[]{:S(2)}, u32[]{:S(2)}) %collective-permute-start.2) | collective-permute-done | bytes 131104 | tf_op jit(solution)/shard_map/ppermute | solution.py:22
  36.1 0.9 pad_maximum_fusion
  36.9 2.6 %collective-permute-start.3 = (bf16[2,512,128]{2,1,0:T(8,128)(2,1)S(1)}, bf16[2,512,128]{2,1,0:T(8,128)(2,1)S(1)}, u32[]{:S(2)}, u32[]{:S(2)}) collective-permute-start(bf16[2,512,128]{2,1,0:T(8,128)(2,1)S(1)} %pad_maximum_fusion), channel_id=1, source_target_pairs={{0,4},{1,5},{2,6},{3,7},{4,8},{5,9},{6,10},{7,11},{8,12},{9,13},{1... | collective-permute-start | bytes 786440 | tf_op jit(solution)/shard_map/ppermute | solution.py:22
  39.5 0.1 select_divide_fusion
  39.6 0.7 pad_maximum_fusion.3
  40.3 0.0 collective-permute-done
  40.3 7.0 %collective-permute-done.3 = bf16[2,512,128]{2,1,0:T(8,128)(2,1)S(1)} collective-permute-done((bf16[2,512,128]{2,1,0:T(8,128)(2,1)S(1)}, bf16[2,512,128]{2,1,0:T(8,128)(2,1)S(1)}, u32[]{:S(2)}, u32[]{:S(2)}) %collective-permute-start.3) | collective-permute-done | bytes 262176 | tf_op jit(solution)/shard_map/ppermute | solution.py:22
  47.4 0.0 copy-done.1
  47.4 0.0 copy-start.2
  47.5 1.0 broadcast_in_dim.63.offset_ref
  48.5 0.0 copy-done.2
  48.5 35.9 %shard_map.46 = bf16[8,128,1024]{2,1,0:T(8,128)(2,1)} custom-call(bf16[128,1024]{1,0:T(8,128)(2,1)} %constant_dynamic-slice_fusion.q_ref, bf16[2,1152,128]{2,1,0:T(8,128)(2,1)} %copy-done.2, f32[1152,128]{1,0:T(8,128)} %broadcast_in_dim.63.offset_ref, f32[8,1,128]{2,1,0:T(1,128)} %bitcast.10, f32[128,1152]{1,0:T(8,128)} %and_select_fusion.bias_ref), custom_call_target="tpu_custom_call" | custom-call | flops 4831838208 | bytes 2949120 | tf_op jit(solution)/shard_map/pallas_call | solution.py:93
  84.4 31.8 %all_to_all.18 = bf16[8,128,1024]{2,1,0:T(8,128)(2,1)} all-to-all(bf16[8,128,1024]{2,1,0:T(8,128)(2,1)} %shard_map.46), channel_id=1, replica_groups=mesh['cand'=8,'doc'=64] {'cand'}, dimensions={0} | all-to-all | bytes 4194304 | tf_op jit(solution)/shard_map/all_to_all | solution.py:150
  116.2 3.9 %copy.10 = bf16[1,128,8,1024]{1,3,2,0:T(8,128)(2,1)} copy(bf16[1,128,8,1024]{3,1,2,0:T(8,128)(2,1)} %bitcast.8) | data formatting | bytes 4194304 | tf_op jit(solution)/shard_map/all_to_all | solution.py:150
  120.1 4.1 %copy.11 = bf16[1,128,8192]{2,1,0:T(8,128)(2,1)} copy(bf16[1,128,8192]{1,2,0:T(8,128)(2,1)} %bitcast.9) | data formatting | bytes 4194304 | tf_op jit(solution)/shard_map/all_to_all | solution.py:150
  (15 shorter events, 0.2 us)
Async XLA Ops:
  0.0 10.7 %copy-start = (bf16[128,8192]{1,0:T(8,128)(2,1)S(1)}, bf16[128,8192]{1,0:T(8,128)(2,1)}, u32[]{:S(2)}) copy-start(bf16[128,8192]{1,0:T(8,128)(2,1)} %param.4) | copy-start | bytes 6291460
  0.0 47.4 %copy-start.1 = (bf16[2,128,128]{2,1,0:T(8,128)(2,1)S(1)}, bf16[2,128,128]{2,1,0:T(8,128)(2,1)}, u32[]{:S(2)}) copy-start(bf16[2,128,128]{2,1,0:T(8,128)(2,1)} %param.5) | copy-start | bytes 196612
  0.0 24.3 %collective-permute-start.1 = (bf16[2,128,128]{2,1,0:T(8,128)(2,1)}, bf16[2,128,128]{2,1,0:T(8,128)(2,1)S(1)}, u32[]{:S(2)}, u32[]{:S(2)}) collective-permute-start(bf16[2,128,128]{2,1,0:T(8,128)(2,1)} %param.5), channel_id=1, source_target_pairs={{0,1},{1,2},{2,3},{3,4},{4,5},{5,6},{6,7},{7,8},{8,9},{9,10},{10,1... | collective-permute-start | bytes 196616 | tf_op jit(solution)/shard_map/ppermute | solution.py:22
  3.5 36.8 %collective-permute-start = (bf16[2,128,128]{2,1,0:T(8,128)(2,1)}, bf16[2,128,128]{2,1,0:T(8,128)(2,1)S(1)}, u32[]{:S(2)}, u32[]{:S(2)}) collective-permute-start(bf16[2,128,128]{2,1,0:T(8,128)(2,1)} %param.5), channel_id=1, source_target_pairs={{0,8},{1,9},{2,10},{3,11},{4,12},{5,13},{6,14},{7,15},{8,16},{9,17... | collective-permute-start | bytes 196616 | tf_op jit(solution)/shard_map/ppermute | solution.py:22
  8.7 4.3 %collective-permute-start.4 = (f32[1,64]{1,0:T(1,128)}, f32[1,64]{1,0:T(1,128)S(1)}, u32[]{:S(2)}, u32[]{:S(2)}) collective-permute-start(f32[1,64]{1,0:T(1,128)} %param.6), channel_id=1, source_target_pairs={{0,64},{64,128},{128,192},{192,256},{256,320},{320,384},{384,448},... | collective-permute-start | bytes 776 | tf_op jit(solution)/shard_map/ppermute | solution.py:115
  13.7 6.7 %collective-permute-start.5 = (f32[2,64]{1,0:T(2,128)S(1)}, f32[2,64]{1,0:T(2,128)S(1)}, u32[]{:S(2)}, u32[]{:S(2)}) collective-permute-start(f32[2,64]{1,0:T(2,128)S(1)} %pad_maximum_fusion.5), channel_id=1, source_target_pairs={{0,128},{64,192},{128,256},{192,320},{256,384},{320,448},{384,0},{... | collective-permute-start | bytes 1544 | tf_op jit(solution)/shard_map/ppermute | solution.py:115
  21.0 8.8 %collective-permute-start.6 = (f32[4,64]{1,0:T(4,128)S(1)}, f32[4,64]{1,0:T(4,128)S(1)}, u32[]{:S(2)}, u32[]{:S(2)}) collective-permute-start(f32[4,64]{1,0:T(4,128)S(1)} %pad_maximum_fusion.4), channel_id=1, source_target_pairs={{0,256},{64,320},{128,384},{192,448},{256,0},{320,64},{384,128},{4... | collective-permute-start | bytes 3080 | tf_op jit(solution)/shard_map/ppermute | solution.py:115
  25.2 10.8 %collective-permute-start.2 = (bf16[2,256,128]{2,1,0:T(8,128)(2,1)S(1)}, bf16[2,256,128]{2,1,0:T(8,128)(2,1)S(1)}, u32[]{:S(2)}, u32[]{:S(2)}) collective-permute-start(bf16[2,256,128]{2,1,0:T(8,128)(2,1)S(1)} %pad_maximum_fusion.1), channel_id=1, source_target_pairs={{0,2},{1,3},{2,4},{3,5},{4,6},{5,7},{6,8},{7,9},{8,10},{9,11},{10,... | collective-permute-start | bytes 393224 | tf_op jit(solution)/shard_map/ppermute | solution.py:22
  36.9 10.4 %collective-permute-start.3 = (bf16[2,512,128]{2,1,0:T(8,128)(2,1)S(1)}, bf16[2,512,128]{2,1,0:T(8,128)(2,1)S(1)}, u32[]{:S(2)}, u32[]{:S(2)}) collective-permute-start(bf16[2,512,128]{2,1,0:T(8,128)(2,1)S(1)} %pad_maximum_fusion), channel_id=1, source_target_pairs={{0,4},{1,5},{2,6},{3,7},{4,8},{5,9},{6,10},{7,11},{8,12},{9,13},{1... | collective-permute-start | bytes 786440 | tf_op jit(solution)/shard_map/ppermute | solution.py:22
  47.4 1.0 copy-start.2

commit v4 on v3

--- a/solution.py
+++ b/solution.py
@@ -128,7 +128,6 @@
     while reach < cands:
         behind = jnp.concatenate([behind, cyclic_shift(behind, "cand", reach)], axis=0)
         reach *= 2
-    every_factor = jnp.take(behind, (group - jnp.arange(cands, dtype=jnp.int32)) % cands, axis=0)
     far = passed_along(keys_values, "doc", SPAN)
     window = keys_values
     reach = 1
@@ -146,8 +145,25 @@
     bias = jnp.where(allowed, 0.0, -1e30).astype(jnp.float32)
     offsets = jnp.broadcast_to(key_offset.astype(jnp.float32)[:, None], (key_offset.shape[0], HD))
     own_queries = lax.dynamic_slice_in_dim(queries, group * group_width, group_width, 1)
-    mixed = attend_all(own_queries, window, offsets, inverse_rows(every_factor), bias)
-    return lax.all_to_all(mixed, "cand", 0, 2, tiled=True)
+    placed = jnp.zeros((row_count, queries.shape[1]), jnp.bfloat16)
+    order = list(range(1, cands)) + [0]
+    chunk = 2
+    for first in range(0, cands, chunk):
+        steps = order[first : first + chunk]
+        rows = jnp.concatenate([inverse_for(behind, step) for step in steps], axis=0)
+        mixed = attend_all(own_queries, window, offsets, rows, bias)
+        for slot, step in enumerate(steps):
+            block = mixed[slot]
+            if step:
+                block = cyclic_shift(block, "cand", step)
+            source = (group - step) % cands
+            placed = lax.dynamic_update_slice_in_dim(placed, block, source * group_width, 1)
+    return placed[None]
+
+
+def inverse_for(behind, step):
+    count = behind.shape[0]
+    return inverse_rows(behind[(count - step) % count :][:1])
 
 
 def solution(mesh):

time: 125 us -> 132 us (1.056)
  blocking collectives: 31.8 us -> 0 us
  starting transfers between devices: 22.2 us -> 39.9 us
  waiting for transfers between devices: 16.3 us -> 29 us
  Pallas kernels: 35.9 us -> 42.5 us
  other arithmetic: 6.67 us -> 8.5 us
    all_to_all x1 -> x0, blocking collectives: 31.8 us -> none  [on_device(): return lax.all_to_all(mixed, 'cand', 0, 2, tiled=True)]
    ppermute x3 -> x10, starting transfers between devices: 6.22 us -> 24 us  [cyclic_shift(): lax.ppermute(value, axis, [(source, (source + steps) % count) for source...]
    ppermute x3 -> x10, waiting for transfers between devices: 4.33 us -> 17.5 us  [cyclic_shift(): lax.ppermute(value, axis, [(source, (source + steps) % count) for source...]
    all_to_all x2 -> x0, local copies, waits for them, and re-layouts: 7.99 us -> none  [on_device(): return lax.all_to_all(mixed, 'cand', 0, 2, tiled=True)]
    pallas_call x1 -> x4, Pallas kernels: 35.9 us -> 42.5 us  [attend_all(): pl.pallas_call(attention_kernel, out_shape=jax.ShapeDtypeStruct((cands, q...]
    squeeze x0 -> x4, local copies, waits for them, and re-layouts: none -> 5.76 us  [on_device(): block = mixed[slot]]
    concatenate x1 -> x4, other arithmetic: 0.67 us -> 2.24 us  [on_device(): jnp.concatenate([inverse_for(behind, step) for step in steps], axis=0)]
  transfers between devices with their start and end apart: 7 -> 14, of which waited for: 4 -> 7; matrix products, arithmetic and copies ran while one was open for 7% -> 12% of each run, Pallas kernels for 0% -> 24%
where the time goes in v4:
time: 132 us; the launch traced here: 131 us
  Pallas kernels  42.5 us (32%)
  starting transfers between devices  39.9 us (30%)
  waiting for transfers between devices  29 us (22%)
  local copies, waits for them, and re-layouts  10.8 us (8%)
  other arithmetic  8.5 us (6%)
    pallas_call x4, Pallas kernels, attend_all(): pl.pallas_call(attention_kernel, out_shape=jax.ShapeDtypeStruct((cands, q...  42.5 us
    ppermute x10, starting transfers between devices, cyclic_shift(): lax.ppermute(value, axis, [(source, (source + steps) % count) for source...  24 us
    ppermute x10, waiting for transfers between devices, cyclic_shift(): lax.ppermute(value, axis, [(source, (source + steps) % count) for source...  17.5 us
    ppermute x4, starting transfers between devices, passed_along(): lax.ppermute(value, axis, [(source, source + steps) for source in range(f...  16 us
    ppermute x4, waiting for transfers between devices, passed_along(): lax.ppermute(value, axis, [(source, source + steps) for source in range(f...  11.4 us
    squeeze x4, local copies, waits for them, and re-layouts, on_device(): block = mixed[slot]  5.76 us
  transfers between devices with their start and end apart: 14, of which 7 were waited for; matrix products, arithmetic and copies ran while one was open for 12% of the time, Pallas kernels for 24%

profile of v4, /device:TPU:128, one launch (start us, length us, event | category | flops | bytes accessed | tf_op | source)
XLA Modules:
  0.0 131.2 jit_solution(10312305020301689496)
XLA Ops:
  0.0 3.5 %collective-permute-start.1 = (bf16[2,128,128]{2,1,0:T(8,128)(2,1)}, bf16[2,128,128]{2,1,0:T(8,128)(2,1)S(1)}, u32[]{:S(2)}, u32[]{:S(2)}) collective-permute-start(bf16[2,128,128]{2,1,0:T(8,128)(2,1)} %param.5), channel_id=1, source_target_pairs={{0,1},{1,2},{2,3},{3,4},{4,5},{5,6},{6,7},{7,8},{8,9},{9,10},{10,1... | collective-permute-start | bytes 196616 | tf_op jit(solution)/shard_map/ppermute | solution.py:22
  3.5 5.2 %collective-permute-start = (bf16[2,128,128]{2,1,0:T(8,128)(2,1)}, bf16[2,128,128]{2,1,0:T(8,128)(2,1)S(1)}, u32[]{:S(2)}, u32[]{:S(2)}) collective-permute-start(bf16[2,128,128]{2,1,0:T(8,128)(2,1)} %param.5), channel_id=1, source_target_pairs={{0,8},{1,9},{2,10},{3,11},{4,12},{5,13},{6,14},{7,15},{8,16},{9,17... | collective-permute-start | bytes 196616 | tf_op jit(solution)/shard_map/ppermute | solution.py:22
  8.7 0.0 collective-permute-start.4
  8.9 0.7 fusion.2
  9.6 0.1 maximum_bitcast_fusion.7
  9.7 0.7 copy.7
  10.4 0.1 reduce
  10.6 0.7 sub.35
  11.2 0.1 convert_reduce_fusion.1
  11.3 0.1 convert_reduce_fusion
  11.4 0.1 select_reduce_fusion
  11.6 0.7 constant_dynamic-slice_fusion.q_ref
  12.3 1.0 and_select_fusion.bias_ref
  13.3 0.0 collective-permute-done.4
  13.3 0.1 maximum_bitcast_fusion.6
  13.4 0.7 pad_maximum_fusion.3
  14.1 3.5 %collective-permute-start.5 = (f32[2,64]{1,0:T(2,128)S(1)}, f32[2,64]{1,0:T(2,128)S(1)}, u32[]{:S(2)}, u32[]{:S(2)}) collective-permute-start(f32[2,64]{1,0:T(2,128)S(1)} %pad_maximum_fusion.3), channel_id=1, source_target_pairs={{0,128},{64,192},{128,256},{192,320},{256,384},{320,448},{384,0},{... | collective-permute-start | bytes 1544 | tf_op jit(solution)/shard_map/ppermute | solution.py:115
  17.6 0.5 pad_maximum_fusion.7.inverse_ref
  18.1 2.6 %collective-permute-done.5 = f32[2,64]{1,0:T(2,128)S(1)} collective-permute-done((f32[2,64]{1,0:T(2,128)S(1)}, f32[2,64]{1,0:T(2,128)S(1)}, u32[]{:S(2)}, u32[]{:S(2)}) %collective-permute-start.5) | collective-permute-done | bytes 544 | tf_op jit(solution)/shard_map/ppermute | solution.py:115
  20.7 0.7 pad_maximum_fusion.2
  21.4 3.9 %collective-permute-start.6 = (f32[4,64]{1,0:T(4,128)S(1)}, f32[4,64]{1,0:T(4,128)S(1)}, u32[]{:S(2)}, u32[]{:S(2)}) collective-permute-start(f32[4,64]{1,0:T(4,128)S(1)} %pad_maximum_fusion.2), channel_id=1, source_target_pairs={{0,256},{64,320},{128,384},{192,448},{256,0},{320,64},{384,128},{4... | collective-permute-start | bytes 3080 | tf_op jit(solution)/shard_map/ppermute | solution.py:115
  25.3 0.1 maximum_bitcast_fusion.4
  25.4 0.6 pad_maximum_fusion.6.inverse_ref
  26.0 2.4 %collective-permute-done.6 = f32[4,64]{1,0:T(4,128)S(1)} collective-permute-done((f32[4,64]{1,0:T(4,128)S(1)}, f32[4,64]{1,0:T(4,128)S(1)}, u32[]{:S(2)}, u32[]{:S(2)}) %collective-permute-start.6) | collective-permute-done | bytes 1056 | tf_op jit(solution)/shard_map/ppermute | solution.py:115
  28.4 0.0 collective-permute-done.1
  28.4 0.9 pad_maximum_fusion.1
  29.3 4.6 %collective-permute-start.2 = (bf16[2,256,128]{2,1,0:T(8,128)(2,1)S(1)}, bf16[2,256,128]{2,1,0:T(8,128)(2,1)S(1)}, u32[]{:S(2)}, u32[]{:S(2)}) collective-permute-start(bf16[2,256,128]{2,1,0:T(8,128)(2,1)S(1)} %pad_maximum_fusion.1), channel_id=1, source_target_pairs={{0,2},{1,3},{2,4},{3,5},{4,6},{5,7},{6,8},{7,9},{8,10},{9,11},{10,... | collective-permute-start | bytes 393224 | tf_op jit(solution)/shard_map/ppermute | solution.py:22
  33.9 0.1 maximum_bitcast_fusion.2
  34.0 0.5 pad_maximum_fusion.5.inverse_ref
  34.5 5.2 %collective-permute-done.2 = bf16[2,256,128]{2,1,0:T(8,128)(2,1)S(1)} collective-permute-done((bf16[2,256,128]{2,1,0:T(8,128)(2,1)S(1)}, bf16[2,256,128]{2,1,0:T(8,128)(2,1)S(1)}, u32[]{:S(2)}, u32[]{:S(2)}) %collective-permute-start.2) | collective-permute-done | bytes 131104 | tf_op jit(solution)/shard_map/ppermute | solution.py:22
  39.8 0.9 pad_maximum_fusion
  40.6 2.6 %collective-permute-start.3 = (bf16[2,512,128]{2,1,0:T(8,128)(2,1)S(1)}, bf16[2,512,128]{2,1,0:T(8,128)(2,1)S(1)}, u32[]{:S(2)}, u32[]{:S(2)}) collective-permute-start(bf16[2,512,128]{2,1,0:T(8,128)(2,1)S(1)} %pad_maximum_fusion), channel_id=1, source_target_pairs={{0,4},{1,5},{2,6},{3,7},{4,8},{5,9},{6,10},{7,11},{8,12},{9,13},{1... | collective-permute-start | bytes 786440 | tf_op jit(solution)/shard_map/ppermute | solution.py:22
  43.2 0.1 maximum_bitcast_fusion
  43.3 0.6 pad_maximum_fusion.4.inverse_ref
  43.9 0.0 collective-permute-done
  43.9 6.2 %collective-permute-done.3 = bf16[2,512,128]{2,1,0:T(8,128)(2,1)S(1)} collective-permute-done((bf16[2,512,128]{2,1,0:T(8,128)(2,1)S(1)}, bf16[2,512,128]{2,1,0:T(8,128)(2,1)S(1)}, u32[]{:S(2)}, u32[]{:S(2)}) %collective-permute-start.3) | collective-permute-done | bytes 262176 | tf_op jit(solution)/shard_map/ppermute | solution.py:22
  50.2 0.0 copy-start.4
  50.2 1.1 broadcast_in_dim.100.offset_ref
  51.3 10.6 %shard_map.49 = bf16[2,128,1024]{2,1,0:T(8,128)(2,1)} custom-call(bf16[128,1024]{1,0:T(8,128)(2,1)} %constant_dynamic-slice_fusion.q_ref, bf16[2,1152,128]{2,1,0:T(8,128)(2,1)} %copy-done.4, f32[1152,128]{1,0:T(8,128)} %broadcast_in_dim.100.offset_ref, f32[2,1,128]{2,1,0:T(1,128)} %pad_maximum_fusion.7.inverse_ref, f32[128,1152]{1,0:T(8,128)} %and_select_fusion.bias_ref), custom_call_target="tpu_custom_call" | custom-call | flops 1207959552 | bytes 1376256 | tf_op jit(solution)/shard_map/pallas_call | solution.py:93
  61.9 1.0 slice_bitcast_fusion
  62.9 0.0 collective-permute-start.13
  62.9 10.7 %shard_map.48 = bf16[2,128,1024]{2,1,0:T(8,128)(2,1)} custom-call(bf16[128,1024]{1,0:T(8,128)(2,1)} %constant_dynamic-slice_fusion.q_ref, bf16[2,1152,128]{2,1,0:T(8,128)(2,1)} %copy-done.4, f32[1152,128]{1,0:T(8,128)} %broadcast_in_dim.100.offset_ref, f32[2,1,128]{2,1,0:T(1,128)} %pad_maximum_fusion.6.inverse_ref, f32[128,1152]{1,0:T(8,128)} %and_select_fusion.bias_ref), custom_call_target="tpu_custom_call" | custom-call | flops 1207959552 | bytes 1376256 | tf_op jit(solution)/shard_map/pallas_call | solution.py:93
  73.5 1.9 %slice_bitcast_fusion.1 = (bf16[128,1024]{1,0:T(8,128)(2,1)}, bf16[128,1024]{1,0:T(8,128)(2,1)}) fusion(bf16[2,128,1024]{2,1,0:T(8,128)(2,1)} %shard_map.48), kind=kLoop, calls=%fused_computation.3 | loop fusion | bytes 1048576 | tf_op jit(solution)/shard_map/squeeze | solution.py:156
  75.4 3.7 %collective-permute-start.12 = (bf16[128,1024]{1,0:T(8,128)(2,1)}, bf16[128,1024]{1,0:T(8,128)(2,1)S(1)}, u32[]{:S(2)}, u32[]{:S(2)}) collective-permute-start(bf16[128,1024]{1,0:T(8,128)(2,1)} %get-tuple-element.7), channel_id=1, source_target_pairs={{0,384},{64,448},{128,0},{192,64},{256,128},{320,192},{384,256},{4... | collective-permute-start | bytes 786440 | tf_op jit(solution)/shard_map/ppermute | solution.py:115
  79.1 2.5 %collective-permute-start.11 = (bf16[128,1024]{1,0:T(8,128)(2,1)}, bf16[128,1024]{1,0:T(8,128)(2,1)S(1)}, u32[]{:S(2)}, u32[]{:S(2)}) collective-permute-start(bf16[128,1024]{1,0:T(8,128)(2,1)} %get-tuple-element.8), channel_id=1, source_target_pairs={{0,320},{64,384},{128,448},{192,0},{256,64},{320,128},{384,192},{4... | collective-permute-start | bytes 786440 | tf_op jit(solution)/shard_map/ppermute | solution.py:115
  81.6 10.6 %shard_map.46 = bf16[2,128,1024]{2,1,0:T(8,128)(2,1)} custom-call(bf16[128,1024]{1,0:T(8,128)(2,1)} %constant_dynamic-slice_fusion.q_ref, bf16[2,1152,128]{2,1,0:T(8,128)(2,1)} %copy-done.4, f32[1152,128]{1,0:T(8,128)} %broadcast_in_dim.100.offset_ref, f32[2,1,128]{2,1,0:T(1,128)} %pad_maximum_fusion.4.inverse_ref, f32[128,1152]{1,0:T(8,128)} %and_select_fusion.bias_ref), custom_call_target="tpu_custom_call" | custom-call | flops 1207959552 | bytes 1376256 | tf_op jit(solution)/shard_map/pallas_call | solution.py:93
  92.3 1.9 %slice_bitcast_fusion.5 = (bf16[128,1024]{1,0:T(8,128)(2,1)}, bf16[128,1024]{1,0:T(8,128)(2,1)}) fusion(bf16[2,128,1024]{2,1,0:T(8,128)(2,1)} %shard_map.46), kind=kLoop, calls=%fused_computation.7 | loop fusion | bytes 1048576 | tf_op jit(solution)/shard_map/squeeze | solution.py:156
  94.1 0.4 collective-permute-start.7
  94.5 10.6 %shard_map.47 = bf16[2,128,1024]{2,1,0:T(8,128)(2,1)} custom-call(bf16[128,1024]{1,0:T(8,128)(2,1)} %constant_dynamic-slice_fusion.q_ref, bf16[2,1152,128]{2,1,0:T(8,128)(2,1)} %copy-done.4, f32[1152,128]{1,0:T(8,128)} %broadcast_in_dim.100.offset_ref, f32[2,1,128]{2,1,0:T(1,128)} %pad_maximum_fusion.5.inverse_ref, f32[128,1152]{1,0:T(8,128)} %and_select_fusion.bias_ref), custom_call_target="tpu_custom_call" | custom-call | flops 1207959552 | bytes 1376256 | tf_op jit(solution)/shard_map/pallas_call | solution.py:93
  105.1 3.2 %collective-permute-start.8 = (bf16[128,1024]{1,0:T(8,128)(2,1)}, bf16[128,1024]{1,0:T(8,128)(2,1)S(1)}, u32[]{:S(2)}, u32[]{:S(2)}) collective-permute-start(bf16[128,1024]{1,0:T(8,128)(2,1)} %get-tuple-element.11), channel_id=1, source_target_pairs={{0,128},{64,192},{128,256},{192,320},{256,384},{320,448},{384,0},{... | collective-permute-start | bytes 786440 | tf_op jit(solution)/shard_map/ppermute | solution.py:115
  108.3 1.1 slice_bitcast_fusion.3
  109.4 0.0 collective-permute-done.7
  109.4 3.3 %collective-permute-start.9 = (bf16[128,1024]{1,0:T(8,128)(2,1)S(1)}, bf16[128,1024]{1,0:T(8,128)(2,1)S(1)}, u32[]{:S(2)}, u32[]{:S(2)}) collective-permute-start(bf16[128,1024]{1,0:T(8,128)(2,1)S(1)} %get-tuple-element.10), channel_id=1, source_target_pairs={{0,192},{64,256},{128,320},{192,384},{256,448},{320,0},{384,64},{4... | collective-permute-start | bytes 786440 | tf_op jit(solution)/shard_map/ppermute | solution.py:115
  112.8 0.2 broadcast_in_dim.97
  113.0 4.3 %collective-permute-done.8 = bf16[128,1024]{1,0:T(8,128)(2,1)S(1)} collective-permute-done((bf16[128,1024]{1,0:T(8,128)(2,1)}, bf16[128,1024]{1,0:T(8,128)(2,1)S(1)}, u32[]{:S(2)}, u32[]{:S(2)}) %collective-permute-start.8) | collective-permute-done | bytes 262176 | tf_op jit(solution)/shard_map/ppermute | solution.py:115
  117.3 3.5 %collective-permute-start.10 = (bf16[128,1024]{1,0:T(8,128)(2,1)S(1)}, bf16[128,1024]{1,0:T(8,128)(2,1)S(1)}, u32[]{:S(2)}, u32[]{:S(2)}) collective-permute-start(bf16[128,1024]{1,0:T(8,128)(2,1)S(1)} %get-tuple-element.9), channel_id=1, source_target_pairs={{0,256},{64,320},{128,384},{192,448},{256,0},{320,64},{384,128},{4... | collective-permute-start | bytes 786440 | tf_op jit(solution)/shard_map/ppermute | solution.py:115
  120.8 2.6 %collective-permute-done.9 = bf16[128,1024]{1,0:T(8,128)(2,1)S(1)} collective-permute-done((bf16[128,1024]{1,0:T(8,128)(2,1)S(1)}, bf16[128,1024]{1,0:T(8,128)(2,1)S(1)}, u32[]{:S(2)}, u32[]{:S(2)}) %collective-permute-start.9) | collective-permute-done | bytes 262176 | tf_op jit(solution)/shard_map/ppermute | solution.py:115
  123.4 5.6 %collective-permute-done.10 = bf16[128,1024]{1,0:T(8,128)(2,1)S(1)} collective-permute-done((bf16[128,1024]{1,0:T(8,128)(2,1)S(1)}, bf16[128,1024]{1,0:T(8,128)(2,1)S(1)}, u32[]{:S(2)}, u32[]{:S(2)}) %collective-permute-start.10) | collective-permute-done | bytes 262176 | tf_op jit(solution)/shard_map/ppermute | solution.py:115
  129.0 0.0 collective-permute-done.11
  129.0 0.0 collective-permute-done.12
  129.1 0.0 collective-permute-done.13
  129.1 0.0 copy-start.1
  129.1 1.3 copy-done.1
  130.5 0.7 slice_dynamic-update-slice_fusion
  (28 shorter events, 0.4 us)
Async XLA Ops:
  0.0 11.5 %copy-start = (bf16[128,8192]{1,0:T(8,128)(2,1)S(1)}, bf16[128,8192]{1,0:T(8,128)(2,1)}, u32[]{:S(2)}) copy-start(bf16[128,8192]{1,0:T(8,128)(2,1)} %param.4) | copy-start | bytes 6291460
  0.0 50.2 %copy-start.2 = (bf16[2,128,128]{2,1,0:T(8,128)(2,1)S(1)}, bf16[2,128,128]{2,1,0:T(8,128)(2,1)}, u32[]{:S(2)}) copy-start(bf16[2,128,128]{2,1,0:T(8,128)(2,1)} %param.5) | copy-start | bytes 196612
  0.0 28.4 %collective-permute-start.1 = (bf16[2,128,128]{2,1,0:T(8,128)(2,1)}, bf16[2,128,128]{2,1,0:T(8,128)(2,1)S(1)}, u32[]{:S(2)}, u32[]{:S(2)}) collective-permute-start(bf16[2,128,128]{2,1,0:T(8,128)(2,1)} %param.5), channel_id=1, source_target_pairs={{0,1},{1,2},{2,3},{3,4},{4,5},{5,6},{6,7},{7,8},{8,9},{9,10},{10,1... | collective-permute-start | bytes 196616 | tf_op jit(solution)/shard_map/ppermute | solution.py:22
  3.5 40.4 %collective-permute-start = (bf16[2,128,128]{2,1,0:T(8,128)(2,1)}, bf16[2,128,128]{2,1,0:T(8,128)(2,1)S(1)}, u32[]{:S(2)}, u32[]{:S(2)}) collective-permute-start(bf16[2,128,128]{2,1,0:T(8,128)(2,1)} %param.5), channel_id=1, source_target_pairs={{0,8},{1,9},{2,10},{3,11},{4,12},{5,13},{6,14},{7,15},{8,16},{9,17... | collective-permute-start | bytes 196616 | tf_op jit(solution)/shard_map/ppermute | solution.py:22
  8.7 4.6 %collective-permute-start.4 = (f32[1,64]{1,0:T(1,128)}, f32[1,64]{1,0:T(1,128)S(1)}, u32[]{:S(2)}, u32[]{:S(2)}) collective-permute-start(f32[1,64]{1,0:T(1,128)} %param.6), channel_id=1, source_target_pairs={{0,64},{64,128},{128,192},{192,256},{256,320},{320,384},{384,448},... | collective-permute-start | bytes 776 | tf_op jit(solution)/shard_map/ppermute | solution.py:115
  14.1 6.7 %collective-permute-start.5 = (f32[2,64]{1,0:T(2,128)S(1)}, f32[2,64]{1,0:T(2,128)S(1)}, u32[]{:S(2)}, u32[]{:S(2)}) collective-permute-start(f32[2,64]{1,0:T(2,128)S(1)} %pad_maximum_fusion.3), channel_id=1, source_target_pairs={{0,128},{64,192},{128,256},{192,320},{256,384},{320,448},{384,0},{... | collective-permute-start | bytes 1544 | tf_op jit(solution)/shard_map/ppermute | solution.py:115
  21.4 7.0 %collective-permute-start.6 = (f32[4,64]{1,0:T(4,128)S(1)}, f32[4,64]{1,0:T(4,128)S(1)}, u32[]{:S(2)}, u32[]{:S(2)}) collective-permute-start(f32[4,64]{1,0:T(4,128)S(1)} %pad_maximum_fusion.2), channel_id=1, source_target_pairs={{0,256},{64,320},{128,384},{192,448},{256,0},{320,64},{384,128},{4... | collective-permute-start | bytes 3080 | tf_op jit(solution)/shard_map/ppermute | solution.py:115
  29.3 10.5 %collective-permute-start.2 = (bf16[2,256,128]{2,1,0:T(8,128)(2,1)S(1)}, bf16[2,256,128]{2,1,0:T(8,128)(2,1)S(1)}, u32[]{:S(2)}, u32[]{:S(2)}) collective-permute-start(bf16[2,256,128]{2,1,0:T(8,128)(2,1)S(1)} %pad_maximum_fusion.1), channel_id=1, source_target_pairs={{0,2},{1,3},{2,4},{3,5},{4,6},{5,7},{6,8},{7,9},{8,10},{9,11},{10,... | collective-permute-start | bytes 393224 | tf_op jit(solution)/shard_map/ppermute | solution.py:22
  40.6 9.5 %collective-permute-start.3 = (bf16[2,512,128]{2,1,0:T(8,128)(2,1)S(1)}, bf16[2,512,128]{2,1,0:T(8,128)(2,1)S(1)}, u32[]{:S(2)}, u32[]{:S(2)}) collective-permute-start(bf16[2,512,128]{2,1,0:T(8,128)(2,1)S(1)} %pad_maximum_fusion), channel_id=1, source_target_pairs={{0,4},{1,5},{2,6},{3,7},{4,8},{5,9},{6,10},{7,11},{8,12},{9,13},{1... | collective-permute-start | bytes 786440 | tf_op jit(solution)/shard_map/ppermute | solution.py:22
  50.2 1.1 copy-start.4
  62.9 66.2 %collective-permute-start.13 = (bf16[128,1024]{1,0:T(8,128)(2,1)S(1)}, bf16[128,1024]{1,0:T(8,128)(2,1)S(1)}, u32[]{:S(2)}, u32[]{:S(2)}) collective-permute-start(bf16[128,1024]{1,0:T(8,128)(2,1)S(1)} %slice_bitcast_fusion), channel_id=1, source_target_pairs={{0,448},{64,0},{128,64},{192,128},{256,192},{320,256},{384,320},{4... | collective-permute-start | bytes 786440 | tf_op jit(solution)/shard_map/ppermute | solution.py:115
  75.4 53.7 %collective-permute-start.12 = (bf16[128,1024]{1,0:T(8,128)(2,1)}, bf16[128,1024]{1,0:T(8,128)(2,1)S(1)}, u32[]{:S(2)}, u32[]{:S(2)}) collective-permute-start(bf16[128,1024]{1,0:T(8,128)(2,1)} %get-tuple-element.7), channel_id=1, source_target_pairs={{0,384},{64,448},{128,0},{192,64},{256,128},{320,192},{384,256},{4... | collective-permute-start | bytes 786440 | tf_op jit(solution)/shard_map/ppermute | solution.py:115
  79.1 49.9 %collective-permute-start.11 = (bf16[128,1024]{1,0:T(8,128)(2,1)}, bf16[128,1024]{1,0:T(8,128)(2,1)S(1)}, u32[]{:S(2)}, u32[]{:S(2)}) collective-permute-start(bf16[128,1024]{1,0:T(8,128)(2,1)} %get-tuple-element.8), channel_id=1, source_target_pairs={{0,320},{64,384},{128,448},{192,0},{256,64},{320,128},{384,192},{4... | collective-permute-start | bytes 786440 | tf_op jit(solution)/shard_map/ppermute | solution.py:115
  94.1 15.3 %collective-permute-start.7 = (bf16[128,1024]{1,0:T(8,128)(2,1)}, bf16[128,1024]{1,0:T(8,128)(2,1)S(1)}, u32[]{:S(2)}, u32[]{:S(2)}) collective-permute-start(bf16[128,1024]{1,0:T(8,128)(2,1)} %get-tuple-element.12), channel_id=1, source_target_pairs={{0,64},{64,128},{128,192},{192,256},{256,320},{320,384},{384,448},... | collective-permute-start | bytes 786440 | tf_op jit(solution)/shard_map/ppermute | solution.py:115
  105.1 12.2 %collective-permute-start.8 = (bf16[128,1024]{1,0:T(8,128)(2,1)}, bf16[128,1024]{1,0:T(8,128)(2,1)S(1)}, u32[]{:S(2)}, u32[]{:S(2)}) collective-permute-start(bf16[128,1024]{1,0:T(8,128)(2,1)} %get-tuple-element.11), channel_id=1, source_target_pairs={{0,128},{64,192},{128,256},{192,320},{256,384},{320,448},{384,0},{... | collective-permute-start | bytes 786440 | tf_op jit(solution)/shard_map/ppermute | solution.py:115
  109.4 13.9 %collective-permute-start.9 = (bf16[128,1024]{1,0:T(8,128)(2,1)S(1)}, bf16[128,1024]{1,0:T(8,128)(2,1)S(1)}, u32[]{:S(2)}, u32[]{:S(2)}) collective-permute-start(bf16[128,1024]{1,0:T(8,128)(2,1)S(1)} %get-tuple-element.10), channel_id=1, source_target_pairs={{0,192},{64,256},{128,320},{192,384},{256,448},{320,0},{384,64},{4... | collective-permute-start | bytes 786440 | tf_op jit(solution)/shard_map/ppermute | solution.py:115
  113.0 17.5 %copy-start.3 = (bf16[2,128,1024]{2,1,0:T(8,128)(2,1)S(1)}, bf16[2,128,1024]{2,1,0:T(8,128)(2,1)}, u32[]{:S(2)}) copy-start(bf16[2,128,1024]{2,1,0:T(8,128)(2,1)} %shard_map.49) | copy-start | bytes 1572868
  117.3 11.7 %collective-permute-start.10 = (bf16[128,1024]{1,0:T(8,128)(2,1)S(1)}, bf16[128,1024]{1,0:T(8,128)(2,1)S(1)}, u32[]{:S(2)}, u32[]{:S(2)}) collective-permute-start(bf16[128,1024]{1,0:T(8,128)(2,1)S(1)} %get-tuple-element.9), channel_id=1, source_target_pairs={{0,256},{64,320},{128,384},{192,448},{256,0},{320,64},{384,128},{4... | collective-permute-start | bytes 786440 | tf_op jit(solution)/shard_map/ppermute | solution.py:115
  129.1 1.3 %copy-start.1 = (bf16[1,128,8192]{2,1,0:T(8,128)(2,1)}, bf16[1,128,8192]{2,1,0:T(8,128)(2,1)S(1)}, u32[]{:S(2)}) copy-start(bf16[1,128,8192]{2,1,0:T(8,128)(2,1)S(1)} %bitcast_dynamic-update-slice_fusion) | copy-start | bytes 6291460

commit v5 on v3

--- a/solution.py
+++ b/solution.py
@@ -110,6 +110,21 @@
     )(own_queries, window, offsets, inverse, bias)
 
 
+def place_kernel(in_ref, out_ref):
+    out_ref[...] = in_ref[0]
+
+
+def side_by_side(blocks):
+    count, rows, width = blocks.shape
+    return pl.pallas_call(
+        place_kernel,
+        out_shape=jax.ShapeDtypeStruct((rows, count * width), blocks.dtype),
+        grid=(count,),
+        in_specs=[pl.BlockSpec((1, rows, width), lambda g: (g, 0, 0))],
+        out_specs=pl.BlockSpec((rows, width), lambda g: (0, g)),
+    )(blocks)
+
+
 def cyclic_shift(value, axis, steps):
     count = lax.axis_size(axis)
     return lax.ppermute(value, axis, [(source, (source + steps) % count) for source in range(count)])
@@ -123,12 +138,9 @@
     query_index = device * row_count + jnp.arange(row_count, dtype=jnp.int32)
     key_index = (device - SPAN) * row_count + jnp.arange((SPAN + 1) * row_count, dtype=jnp.int32)
     cands = lax.axis_size("cand")
-    behind = factors
-    reach = 1
-    while reach < cands:
-        behind = jnp.concatenate([behind, cyclic_shift(behind, "cand", reach)], axis=0)
-        reach *= 2
-    every_factor = jnp.take(behind, (group - jnp.arange(cands, dtype=jnp.int32)) % cands, axis=0)
+    every_factor = lax.all_to_all(
+        jnp.broadcast_to(factors, (cands, factors.shape[1])), "cand", 0, 0, tiled=True
+    )
     far = passed_along(keys_values, "doc", SPAN)
     window = keys_values
     reach = 1
@@ -147,7 +159,8 @@
     offsets = jnp.broadcast_to(key_offset.astype(jnp.float32)[:, None], (key_offset.shape[0], HD))
     own_queries = lax.dynamic_slice_in_dim(queries, group * group_width, group_width, 1)
     mixed = attend_all(own_queries, window, offsets, inverse_rows(every_factor), bias)
-    return lax.all_to_all(mixed, "cand", 0, 2, tiled=True)
+    gathered = lax.all_to_all(mixed, "cand", 0, 0, tiled=True)
+    return side_by_side(gathered)[None]
 
 
 def solution(mesh):

time: 125 us -> 117 us (0.936)
  local copies, waits for them, and re-layouts: 11.1 us -> 3.85 us
  Pallas kernels: 35.9 us -> 41.5 us
  waiting for transfers between devices: 16.3 us -> 13.7 us
  other arithmetic: 6.67 us -> 4.56 us
  starting transfers between devices: 22.2 us -> 20.4 us
    all_to_all x2 -> x0, local copies, waits for them, and re-layouts: 7.99 us -> none  [on_device(): return lax.all_to_all(mixed, 'cand', 0, 2, tiled=True)]
    ppermute x3 -> x0, starting transfers between devices: 6.22 us -> none  [cyclic_shift(): lax.ppermute(value, axis, [(source, (source + steps) % count) for source...]
    pallas_call x0 -> x1, Pallas kernels: none -> 5.63 us  [side_by_side(): pl.pallas_call(place_kernel, out_shape=jax.ShapeDtypeStruct((rows, count...]
    all_to_all x0 -> x1, starting transfers between devices: none -> 4.47 us  [on_device(): lax.all_to_all(jnp.broadcast_to(factors, (cands, factors.shape[1])), 'can...]
    ppermute x3 -> x0, waiting for transfers between devices: 4.33 us -> none  [cyclic_shift(): lax.ppermute(value, axis, [(source, (source + steps) % count) for source...]
    concatenate x3 -> x0, other arithmetic: 2 us -> none  [on_device(): jnp.concatenate([behind, cyclic_shift(behind, 'cand', reach)], axis=0)]
    ppermute x4, waiting for transfers between devices: 12 us -> 13.7 us  [passed_along(): lax.ppermute(value, axis, [(source, source + steps) for source in range(f...]
    broadcast_in_dim x0 -> x1, local copies, waits for them, and re-layouts: none -> 1.25 us  [on_device(): jnp.broadcast_to(factors, (cands, factors.shape[1]))]
  transfers between devices with their start and end apart: 7 -> 5, of which waited for: 4 -> 2; matrix products, arithmetic and copies ran while one was open for 7% -> 6% of each run, Pallas kernels for 0% -> 0%
where the time goes in v5:
time: 117 us; the launch traced here: 116 us
  Pallas kernels  41.5 us (35%)
  blocking collectives  31.8 us (27%)
  starting transfers between devices  20.4 us (17%)
  waiting for transfers between devices  13.7 us (12%)
  other arithmetic  4.56 us (4%)
  local copies, waits for them, and re-layouts  3.85 us (3%)
    pallas_call x1, Pallas kernels, attend_all(): pl.pallas_call(attention_kernel, out_shape=jax.ShapeDtypeStruct((cands, q...  35.9 us
    all_to_all x1, blocking collectives, on_device(): gathered = lax.all_to_all(mixed, 'cand', 0, 0, tiled=True)  31.8 us
    ppermute x4, starting transfers between devices, passed_along(): lax.ppermute(value, axis, [(source, source + steps) for source in range(f...  16 us
    ppermute x4, waiting for transfers between devices, passed_along(): lax.ppermute(value, axis, [(source, source + steps) for source in range(f...  13.7 us
    pallas_call x1, Pallas kernels, side_by_side(): pl.pallas_call(place_kernel, out_shape=jax.ShapeDtypeStruct((rows, count...  5.63 us
    all_to_all x1, starting transfers between devices, on_device(): lax.all_to_all(jnp.broadcast_to(factors, (cands, factors.shape[1])), 'can...  4.47 us
  transfers between devices with their start and end apart: 5, of which 2 were waited for; matrix products, arithmetic and copies ran while one was open for 6% of the time, Pallas kernels for 0%

profile of v5, /device:TPU:128, one launch (start us, length us, event | category | flops | bytes accessed | tf_op | source)
XLA Modules:
  0.0 116.0 jit_solution(15182710533711614882)
XLA Ops:
  0.0 0.0 copy-start
  0.0 0.0 copy-start.1
  0.0 3.5 %collective-permute-start.1 = (bf16[2,128,128]{2,1,0:T(8,128)(2,1)}, bf16[2,128,128]{2,1,0:T(8,128)(2,1)S(1)}, u32[]{:S(2)}, u32[]{:S(2)}) collective-permute-start(bf16[2,128,128]{2,1,0:T(8,128)(2,1)} %param.5), channel_id=1, source_target_pairs={{0,1},{1,2},{2,3},{3,4},{4,5},{5,6},{6,7},{7,8},{8,9},{9,10},{10,1... | collective-permute-start | bytes 196616 | tf_op jit(solution)/shard_map/ppermute | solution.py:22
  3.5 5.2 %collective-permute-start = (bf16[2,128,128]{2,1,0:T(8,128)(2,1)}, bf16[2,128,128]{2,1,0:T(8,128)(2,1)S(1)}, u32[]{:S(2)}, u32[]{:S(2)}) collective-permute-start(bf16[2,128,128]{2,1,0:T(8,128)(2,1)} %param.5), channel_id=1, source_target_pairs={{0,8},{1,9},{2,10},{3,11},{4,12},{5,13},{6,14},{7,15},{8,16},{9,17... | collective-permute-start | bytes 196616 | tf_op jit(solution)/shard_map/ppermute | solution.py:22
  8.7 1.3 %broadcast_in_dim.62 = f32[8,1,64]{2,1,0:T(1,128)} broadcast(f32[64]{0:T(128)} %bitcast.7), dimensions={2} | broadcast | bytes 2304 | tf_op jit(solution)/shard_map/broadcast_in_dim | solution.py:142
  10.0 4.5 %all-to-all-start = ((f32[8,1,64]{2,1,0:T(1,128)}), f32[8,1,64]{2,1,0:T(1,128)S(1)}, u32[]{:S(2)}, u32[]{:S(2)}) async-start(f32[8,1,64]{2,1,0:T(1,128)} %broadcast_in_dim.62), calls=%async_computation | async-start | bytes 8192 | tf_op jit(solution)/shard_map/all_to_all | solution.py:141
  14.5 0.7 copy.8
  15.2 0.1 reduce
  15.4 0.7 sub.14
  16.0 0.1 convert_reduce_fusion.1
  16.1 0.1 convert_reduce_fusion
  16.2 0.1 select_reduce_fusion
  16.3 1.1 and_select_fusion.bias_ref
  17.4 0.0 collective-permute-done.1
  17.4 0.9 pad_maximum_fusion.1
  18.2 4.6 %collective-permute-start.2 = (bf16[2,256,128]{2,1,0:T(8,128)(2,1)S(1)}, bf16[2,256,128]{2,1,0:T(8,128)(2,1)S(1)}, u32[]{:S(2)}, u32[]{:S(2)}) collective-permute-start(bf16[2,256,128]{2,1,0:T(8,128)(2,1)S(1)} %pad_maximum_fusion.1), channel_id=1, source_target_pairs={{0,2},{1,3},{2,4},{3,5},{4,6},{5,7},{6,8},{7,9},{8,10},{9,11},{10,... | collective-permute-start | bytes 393224 | tf_op jit(solution)/shard_map/ppermute | solution.py:22
  22.9 0.0 copy-done
  22.9 0.7 constant_dynamic-slice_fusion.q_ref
  23.6 6.0 %collective-permute-done.2 = bf16[2,256,128]{2,1,0:T(8,128)(2,1)S(1)} collective-permute-done((bf16[2,256,128]{2,1,0:T(8,128)(2,1)S(1)}, bf16[2,256,128]{2,1,0:T(8,128)(2,1)S(1)}, u32[]{:S(2)}, u32[]{:S(2)}) %collective-permute-start.2) | collective-permute-done | bytes 131104 | tf_op jit(solution)/shard_map/ppermute | solution.py:22
  29.6 0.9 pad_maximum_fusion
  30.5 2.6 %collective-permute-start.3 = (bf16[2,512,128]{2,1,0:T(8,128)(2,1)S(1)}, bf16[2,512,128]{2,1,0:T(8,128)(2,1)S(1)}, u32[]{:S(2)}, u32[]{:S(2)}) collective-permute-start(bf16[2,512,128]{2,1,0:T(8,128)(2,1)S(1)} %pad_maximum_fusion), channel_id=1, source_target_pairs={{0,4},{1,5},{2,6},{3,7},{4,8},{5,9},{6,10},{7,11},{8,12},{9,13},{1... | collective-permute-start | bytes 786440 | tf_op jit(solution)/shard_map/ppermute | solution.py:22
  33.1 0.0 all-to-all-done
  33.1 0.7 pad_maximum_fusion.2
  33.8 0.0 collective-permute-done
  33.8 7.7 %collective-permute-done.3 = bf16[2,512,128]{2,1,0:T(8,128)(2,1)S(1)} collective-permute-done((bf16[2,512,128]{2,1,0:T(8,128)(2,1)S(1)}, bf16[2,512,128]{2,1,0:T(8,128)(2,1)S(1)}, u32[]{:S(2)}, u32[]{:S(2)}) %collective-permute-start.3) | collective-permute-done | bytes 262176 | tf_op jit(solution)/shard_map/ppermute | solution.py:22
  41.6 0.0 copy-done.1
  41.6 0.0 copy-start.2
  41.7 1.0 broadcast_in_dim.61.offset_ref
  42.7 0.0 copy-done.2
  42.7 35.9 %shard_map.49 = bf16[8,128,1024]{2,1,0:T(8,128)(2,1)} custom-call(bf16[128,1024]{1,0:T(8,128)(2,1)} %constant_dynamic-slice_fusion.q_ref, bf16[2,1152,128]{2,1,0:T(8,128)(2,1)} %copy-done.2, f32[1152,128]{1,0:T(8,128)} %broadcast_in_dim.61.offset_ref, f32[8,1,128]{2,1,0:T(1,128)} %bitcast.6, f32[128,1152]{1,0:T(8,128)} %and_select_fusion.bias_ref), custom_call_target="tpu_custom_call" | custom-call | flops 4831838208 | bytes 2949120 | tf_op jit(solution)/shard_map/pallas_call | solution.py:93
  78.6 31.8 %all_to_all.14.in_ref = bf16[8,128,1024]{2,1,0:T(8,128)(2,1)} all-to-all(bf16[8,128,1024]{2,1,0:T(8,128)(2,1)} %shard_map.49), channel_id=1, replica_groups=mesh['cand'=8,'doc'=64] {'cand'}, dimensions={0} | all-to-all | bytes 4194304 | tf_op jit(solution)/shard_map/all_to_all | solution.py:162
  110.4 5.6 %shard_map.50 = bf16[128,8192]{1,0:T(8,128)(2,1)} custom-call(bf16[8,128,1024]{2,1,0:T(8,128)(2,1)} %all_to_all.14.in_ref), custom_call_target="tpu_custom_call" | custom-call | tf_op jit(solution)/shard_map/pallas_call | solution.py:119
  (13 shorter events, 0.2 us)
Async XLA Ops:
  0.0 22.9 %copy-start = (bf16[128,8192]{1,0:T(8,128)(2,1)S(1)}, bf16[128,8192]{1,0:T(8,128)(2,1)}, u32[]{:S(2)}) copy-start(bf16[128,8192]{1,0:T(8,128)(2,1)} %param.4) | copy-start | bytes 6291460
  0.0 41.6 %copy-start.1 = (bf16[2,128,128]{2,1,0:T(8,128)(2,1)S(1)}, bf16[2,128,128]{2,1,0:T(8,128)(2,1)}, u32[]{:S(2)}) copy-start(bf16[2,128,128]{2,1,0:T(8,128)(2,1)} %param.5) | copy-start | bytes 196612
  0.0 17.4 %collective-permute-start.1 = (bf16[2,128,128]{2,1,0:T(8,128)(2,1)}, bf16[2,128,128]{2,1,0:T(8,128)(2,1)S(1)}, u32[]{:S(2)}, u32[]{:S(2)}) collective-permute-start(bf16[2,128,128]{2,1,0:T(8,128)(2,1)} %param.5), channel_id=1, source_target_pairs={{0,1},{1,2},{2,3},{3,4},{4,5},{5,6},{6,7},{7,8},{8,9},{9,10},{10,1... | collective-permute-start | bytes 196616 | tf_op jit(solution)/shard_map/ppermute | solution.py:22
  3.5 30.3 %collective-permute-start = (bf16[2,128,128]{2,1,0:T(8,128)(2,1)}, bf16[2,128,128]{2,1,0:T(8,128)(2,1)S(1)}, u32[]{:S(2)}, u32[]{:S(2)}) collective-permute-start(bf16[2,128,128]{2,1,0:T(8,128)(2,1)} %param.5), channel_id=1, source_target_pairs={{0,8},{1,9},{2,10},{3,11},{4,12},{5,13},{6,14},{7,15},{8,16},{9,17... | collective-permute-start | bytes 196616 | tf_op jit(solution)/shard_map/ppermute | solution.py:22
  10.0 23.1 %all-to-all-start = ((f32[8,1,64]{2,1,0:T(1,128)}), f32[8,1,64]{2,1,0:T(1,128)S(1)}, u32[]{:S(2)}, u32[]{:S(2)}) async-start(f32[8,1,64]{2,1,0:T(1,128)} %broadcast_in_dim.62), calls=%async_computation | async-start | bytes 8192 | tf_op jit(solution)/shard_map/all_to_all | solution.py:141
  18.2 11.4 %collective-permute-start.2 = (bf16[2,256,128]{2,1,0:T(8,128)(2,1)S(1)}, bf16[2,256,128]{2,1,0:T(8,128)(2,1)S(1)}, u32[]{:S(2)}, u32[]{:S(2)}) collective-permute-start(bf16[2,256,128]{2,1,0:T(8,128)(2,1)S(1)} %pad_maximum_fusion.1), channel_id=1, source_target_pairs={{0,2},{1,3},{2,4},{3,5},{4,6},{5,7},{6,8},{7,9},{8,10},{9,11},{10,... | collective-permute-start | bytes 393224 | tf_op jit(solution)/shard_map/ppermute | solution.py:22
  30.5 11.0 %collective-permute-start.3 = (bf16[2,512,128]{2,1,0:T(8,128)(2,1)S(1)}, bf16[2,512,128]{2,1,0:T(8,128)(2,1)S(1)}, u32[]{:S(2)}, u32[]{:S(2)}) collective-permute-start(bf16[2,512,128]{2,1,0:T(8,128)(2,1)S(1)} %pad_maximum_fusion), channel_id=1, source_target_pairs={{0,4},{1,5},{2,6},{3,7},{4,8},{5,9},{6,10},{7,11},{8,12},{9,13},{1... | collective-permute-start | bytes 786440 | tf_op jit(solution)/shard_map/ppermute | solution.py:22
  41.6 1.0 copy-start.2

commit v6 on v5

--- a/solution.py
+++ b/solution.py
@@ -51,28 +51,24 @@
     return jnp.where(((quadrant + 1) & 2) != 0, -base, base)
 
 
-def attention_kernel(q_ref, kv_ref, offset_ref, inverse_ref, bias_ref, out_ref):
+def rotation(angle):
     half_dim = HD // 2
-    group_size = H // KVH
-    query_rows = q_ref.shape[0]
-    angle = offset_ref[...] * inverse_ref[0]
     low = lax.broadcasted_iota(jnp.int32, angle.shape, 1) < half_dim
     table = cos_and_sin(angle, low)
     swapped = pltpu.roll(table, half_dim, 1)
-    cosine = jnp.where(low, table, swapped)
-    sine = jnp.where(low, -swapped, table)
-    keys = kv_ref[0].astype(jnp.float32)
-    key_rot = (keys * cosine + pltpu.roll(keys, half_dim, 1) * sine).astype(jnp.bfloat16)
-    values = kv_ref[1]
-    first_query = angle.shape[0] - query_rows
-    q_cos = cosine[first_query:]
-    q_sin = sine[first_query:]
-    bias = bias_ref[...]
+    return jnp.where(low, table, swapped), jnp.where(low, -swapped, table)
+
+
+def turned(values, cosine, sine):
+    return (values * cosine + pltpu.roll(values, HD // 2, 1) * sine).astype(jnp.bfloat16)
+
+
+def attend_rows(q_ref, key_rot, values, q_cos, q_sin, bias, out_ref):
+    group_size = H // KVH
     scale = 1.0 / math.sqrt(HD)
     for head in range(group_size):
         cols = slice(head * HD, (head + 1) * HD)
-        x = q_ref[:, cols].astype(jnp.float32)
-        q_rot = (x * q_cos + pltpu.roll(x, half_dim, 1) * q_sin).astype(jnp.bfloat16)
+        q_rot = turned(q_ref[:, cols].astype(jnp.float32), q_cos, q_sin)
         scores = lax.dot_general(
             q_rot, key_rot, (((1,), (1,)), ((), ())), preferred_element_type=jnp.float32
         )
@@ -84,45 +80,84 @@
         out_ref[0, :, cols] = (numer / total).astype(jnp.bfloat16)
 
 
+def first_kernel(q_ref, kv_ref, offset_ref, inverse_ref, bias_ref, out_ref, keys_out_ref):
+    query_rows = q_ref.shape[0]
+    cosine, sine = rotation(offset_ref[...] * inverse_ref[0])
+    key_rot = turned(kv_ref[0].astype(jnp.float32), cosine, sine)
+    keys_out_ref[0] = key_rot
+    first_query = offset_ref.shape[0] - 2 * query_rows
+    q_cos = cosine[first_query : first_query + query_rows]
+    q_sin = sine[first_query : first_query + query_rows]
+    attend_rows(q_ref, key_rot, kv_ref[1], q_cos, q_sin, bias_ref[...], out_ref)
+
+
+def second_kernel(q_ref, kv_ref, offset_ref, inverse_ref, bias_ref, keys_ref, out_ref):
+    query_rows = q_ref.shape[0]
+    first_query = offset_ref.shape[0] - query_rows
+    q_cos, q_sin = rotation(offset_ref[first_query:, :] * inverse_ref[0])
+    attend_rows(q_ref, keys_ref[0], kv_ref[1], q_cos, q_sin, bias_ref[...], out_ref)
+
+
 def attend_all(own_queries, window, offsets, inverse, bias):
     cands = inverse.shape[0]
     key_rows = window.shape[1]
     query_rows, width = own_queries.shape
-    heads = width // HD
-    flops = cands * heads * 4 * query_rows * key_rows * HD
-    return pl.pallas_call(
-        attention_kernel,
-        out_shape=jax.ShapeDtypeStruct((cands, query_rows, width), jnp.bfloat16),
+    half = query_rows // 2
+    flops = cands * (width // HD) * 4 * half * key_rows * HD
+    common = [
+        pl.BlockSpec(window.shape, lambda c: (0, 0, 0)),
+        pl.BlockSpec(offsets.shape, lambda c: (0, 0)),
+        pl.BlockSpec((1, 1, HD), lambda c: (c, 0, 0)),
+    ]
+    out_spec = pl.BlockSpec((1, half, width), lambda c: (c, 0, 0))
+    keys_spec = pl.BlockSpec((1, key_rows, HD), lambda c: (c, 0, 0))
+    cost = pl.CostEstimate(
+        flops=flops,
+        transcendentals=cands * (width // HD) * half * key_rows,
+        bytes_accessed=window.size * 2 + own_queries.size + cands * half * width * 2,
+    )
+    first, rotated = pl.pallas_call(
+        first_kernel,
+        out_shape=(
+            jax.ShapeDtypeStruct((cands, half, width), jnp.bfloat16),
+            jax.ShapeDtypeStruct((cands, key_rows, HD), jnp.bfloat16),
+        ),
         grid=(cands,),
-        in_specs=[
-            pl.BlockSpec((query_rows, width), lambda c: (0, 0)),
-            pl.BlockSpec(window.shape, lambda c: (0, 0, 0)),
-            pl.BlockSpec(offsets.shape, lambda c: (0, 0)),
-            pl.BlockSpec((1, 1, HD), lambda c: (c, 0, 0)),
-            pl.BlockSpec(bias.shape, lambda c: (0, 0)),
-        ],
-        out_specs=pl.BlockSpec((1, query_rows, width), lambda c: (c, 0, 0)),
-        cost_estimate=pl.CostEstimate(
-            flops=flops,
-            transcendentals=cands * heads * query_rows * key_rows,
-            bytes_accessed=window.size * 2 + own_queries.size * 2 + cands * query_rows * width * 2,
-        ),
+        in_specs=[pl.BlockSpec((half, width), lambda c: (0, 0))]
+        + common
+        + [pl.BlockSpec((half, key_rows), lambda c: (0, 0))],
+        out_specs=(out_spec, keys_spec),
+        cost_estimate=cost,
     )(own_queries, window, offsets, inverse, bias)
+    first = lax.all_to_all(first, "cand", 0, 0, tiled=True)
+    second = pl.pallas_call(
+        second_kernel,
+        out_shape=jax.ShapeDtypeStruct((cands, half, width), jnp.bfloat16),
+        grid=(cands,),
+        in_specs=[pl.BlockSpec((half, width), lambda c: (1, 0))]
+        + common
+        + [pl.BlockSpec((half, key_rows), lambda c: (1, 0)), keys_spec],
+        out_specs=out_spec,
+        cost_estimate=cost,
+    )(own_queries, window, offsets, inverse, bias, rotated)
+    second = lax.all_to_all(second, "cand", 0, 0, tiled=True)
+    return first, second
 
 
 def place_kernel(in_ref, out_ref):
-    out_ref[...] = in_ref[0]
-
-
-def side_by_side(blocks):
-    count, rows, width = blocks.shape
+    out_ref[...] = in_ref[0, 0]
+
+
+def side_by_side(first, second):
+    count, rows, width = first.shape
+    both = jnp.stack([first, second])
     return pl.pallas_call(
         place_kernel,
-        out_shape=jax.ShapeDtypeStruct((rows, count * width), blocks.dtype),
-        grid=(count,),
-        in_specs=[pl.BlockSpec((1, rows, width), lambda g: (g, 0, 0))],
-        out_specs=pl.BlockSpec((rows, width), lambda g: (0, g)),
-    )(blocks)
+        out_shape=jax.ShapeDtypeStruct((2 * rows, count * width), first.dtype),
+        grid=(2, count),
+        in_specs=[pl.BlockSpec((1, 1, rows, width), lambda h, g: (h, g, 0, 0))],
+        out_specs=pl.BlockSpec((rows, width), lambda h, g: (h, g)),
+    )(both)
 
 
 def cyclic_shift(value, axis, steps):
@@ -158,9 +193,8 @@
     bias = jnp.where(allowed, 0.0, -1e30).astype(jnp.float32)
     offsets = jnp.broadcast_to(key_offset.astype(jnp.float32)[:, None], (key_offset.shape[0], HD))
     own_queries = lax.dynamic_slice_in_dim(queries, group * group_width, group_width, 1)
-    mixed = attend_all(own_queries, window, offsets, inverse_rows(every_factor), bias)
-    gathered = lax.all_to_all(mixed, "cand", 0, 0, tiled=True)
-    return side_by_side(gathered)[None]
+    first, second = attend_all(own_queries, window, offsets, inverse_rows(every_factor), bias)
+    return side_by_side(first, second)[None]
 
 
 def solution(mesh):

time: 117 us -> 141 us (1.21)
  Pallas kernels: 41.5 us -> 70.8 us
  blocking collectives: 31.8 us -> 20.9 us
  starting transfers between devices: 20.4 us -> 24.5 us
  other arithmetic: 4.56 us -> 6.07 us
    pallas_call x2 -> x3, Pallas kernels: 41.5 us -> 70.8 us  [the longest x1 33.6 us: attend_all(): pl.pallas_call(first_kernel, out_shape=(jax.ShapeDtypeStruct((cands, half...]
    all_to_all x1, blocking collectives: 31.8 us -> 20.9 us  [attend_all(): second = lax.all_to_all(second, 'cand', 0, 0, tiled=True)]
    all_to_all x0 -> x1, starting transfers between devices: none -> 4.06 us  [attend_all(): first = lax.all_to_all(first, 'cand', 0, 0, tiled=True)]
    another operation x2 -> x3, other arithmetic: 0.15 us -> 1.69 us  [the longest x1 1.53 us: side_by_side(): both = jnp.stack([first, second])]
  transfers between devices with their start and end apart: 5 -> 6, of which waited for: 2 -> 2; matrix products, arithmetic and copies ran while one was open for 6% -> 5% of each run, Pallas kernels for 0% -> 20%
where the time goes in v6:
time: 141 us; the launch traced here: 140 us
  Pallas kernels  70.8 us (50%)
  starting transfers between devices  24.5 us (17%)
  blocking collectives  20.9 us (15%)
  waiting for transfers between devices  13.7 us (10%)
  other arithmetic  6.07 us (4%)
  local copies, waits for them, and re-layouts  3.85 us (3%)
    pallas_call x1, Pallas kernels, attend_all(): pl.pallas_call(first_kernel, out_shape=(jax.ShapeDtypeStruct((cands, half...  33.6 us
    pallas_call x1, Pallas kernels, attend_all(): pl.pallas_call(second_kernel, out_shape=jax.ShapeDtypeStruct((cands, half...  27.7 us
    all_to_all x1, blocking collectives, attend_all(): second = lax.all_to_all(second, 'cand', 0, 0, tiled=True)  20.9 us
    ppermute x4, starting transfers between devices, passed_along(): lax.ppermute(value, axis, [(source, source + steps) for source in range(f...  16 us
    ppermute x4, waiting for transfers between devices, passed_along(): lax.ppermute(value, axis, [(source, source + steps) for source in range(f...  13.7 us
    pallas_call x1, Pallas kernels, side_by_side(): pl.pallas_call(place_kernel, out_shape=jax.ShapeDtypeStruct((2 * rows, co...  9.47 us
    all_to_all x1, starting transfers between devices, on_device(): lax.all_to_all(jnp.broadcast_to(factors, (cands, factors.shape[1])), 'can...  4.47 us
    all_to_all x1, starting transfers between devices, attend_all(): first = lax.all_to_all(first, 'cand', 0, 0, tiled=True)  4.06 us
  transfers between devices with their start and end apart: 6, of which 2 were waited for; matrix products, arithmetic and copies ran while one was open for 5% of the time, Pallas kernels for 20%

profile of v6, /device:TPU:128, one launch (start us, length us, event | category | flops | bytes accessed | tf_op | source)
XLA Modules:
  0.0 140.0 jit_solution(15043564756388540043)
XLA Ops:
  0.0 0.0 copy-start
  0.0 0.0 copy-start.1
  0.0 3.5 %collective-permute-start.1 = (bf16[2,128,128]{2,1,0:T(8,128)(2,1)}, bf16[2,128,128]{2,1,0:T(8,128)(2,1)S(1)}, u32[]{:S(2)}, u32[]{:S(2)}) collective-permute-start(bf16[2,128,128]{2,1,0:T(8,128)(2,1)} %param.5), channel_id=1, source_target_pairs={{0,1},{1,2},{2,3},{3,4},{4,5},{5,6},{6,7},{7,8},{8,9},{9,10},{10,1... | collective-permute-start | bytes 196616 | tf_op jit(solution)/shard_map/ppermute | solution.py:22
  3.5 5.2 %collective-permute-start = (bf16[2,128,128]{2,1,0:T(8,128)(2,1)}, bf16[2,128,128]{2,1,0:T(8,128)(2,1)S(1)}, u32[]{:S(2)}, u32[]{:S(2)}) collective-permute-start(bf16[2,128,128]{2,1,0:T(8,128)(2,1)} %param.5), channel_id=1, source_target_pairs={{0,8},{1,9},{2,10},{3,11},{4,12},{5,13},{6,14},{7,15},{8,16},{9,17... | collective-permute-start | bytes 196616 | tf_op jit(solution)/shard_map/ppermute | solution.py:22
  8.7 1.3 broadcast_in_dim.62
  10.0 4.5 %all-to-all-start = ((f32[8,1,64]{2,1,0:T(1,128)}), f32[8,1,64]{2,1,0:T(1,128)S(1)}, u32[]{:S(2)}, u32[]{:S(2)}) async-start(f32[8,1,64]{2,1,0:T(1,128)} %broadcast_in_dim.62), calls=%async_computation | async-start | bytes 8192 | tf_op jit(solution)/shard_map/all_to_all | solution.py:176
  14.5 0.7 copy.8
  15.2 0.1 reduce
  15.4 0.7 sub.14
  16.0 0.1 convert_reduce_fusion.1
  16.1 0.1 convert_reduce_fusion
  16.2 0.1 select_reduce_fusion
  16.3 1.0 and_select_fusion.bias_ref
  17.3 0.0 collective-permute-done.1
  17.3 0.9 pad_maximum_fusion.2
  18.2 4.6 %collective-permute-start.2 = (bf16[2,256,128]{2,1,0:T(8,128)(2,1)S(1)}, bf16[2,256,128]{2,1,0:T(8,128)(2,1)S(1)}, u32[]{:S(2)}, u32[]{:S(2)}) collective-permute-start(bf16[2,256,128]{2,1,0:T(8,128)(2,1)S(1)} %pad_maximum_fusion.2), channel_id=1, source_target_pairs={{0,2},{1,3},{2,4},{3,5},{4,6},{5,7},{6,8},{7,9},{8,10},{9,11},{10,... | collective-permute-start | bytes 393224 | tf_op jit(solution)/shard_map/ppermute | solution.py:22
  22.9 0.0 copy-done
  22.9 0.7 constant_dynamic-slice_fusion.q_ref
  23.6 6.0 %collective-permute-done.2 = bf16[2,256,128]{2,1,0:T(8,128)(2,1)S(1)} collective-permute-done((bf16[2,256,128]{2,1,0:T(8,128)(2,1)S(1)}, bf16[2,256,128]{2,1,0:T(8,128)(2,1)S(1)}, u32[]{:S(2)}, u32[]{:S(2)}) %collective-permute-start.2) | collective-permute-done | bytes 131104 | tf_op jit(solution)/shard_map/ppermute | solution.py:22
  29.6 0.9 pad_maximum_fusion.1
  30.5 2.6 %collective-permute-start.3 = (bf16[2,512,128]{2,1,0:T(8,128)(2,1)S(1)}, bf16[2,512,128]{2,1,0:T(8,128)(2,1)S(1)}, u32[]{:S(2)}, u32[]{:S(2)}) collective-permute-start(bf16[2,512,128]{2,1,0:T(8,128)(2,1)S(1)} %pad_maximum_fusion.1), channel_id=1, source_target_pairs={{0,4},{1,5},{2,6},{3,7},{4,8},{5,9},{6,10},{7,11},{8,12},{9,13},{1... | collective-permute-start | bytes 786440 | tf_op jit(solution)/shard_map/ppermute | solution.py:22
  33.1 0.0 all-to-all-done
  33.1 0.7 pad_maximum_fusion.3
  33.8 0.0 collective-permute-done
  33.8 7.7 %collective-permute-done.3 = bf16[2,512,128]{2,1,0:T(8,128)(2,1)S(1)} collective-permute-done((bf16[2,512,128]{2,1,0:T(8,128)(2,1)S(1)}, bf16[2,512,128]{2,1,0:T(8,128)(2,1)S(1)}, u32[]{:S(2)}, u32[]{:S(2)}) %collective-permute-start.3) | collective-permute-done | bytes 262176 | tf_op jit(solution)/shard_map/ppermute | solution.py:22
  41.6 0.0 copy-done.1
  41.6 0.0 copy-start.2
  41.6 1.0 broadcast_in_dim.61.offset_ref
  42.7 0.0 copy-done.2
  42.7 33.6 %shard_map.49 = (bf16[8,64,1024]{2,1,0:T(8,128)(2,1)}, bf16[8,1152,128]{2,1,0:T(8,128)(2,1)}) custom-call(bf16[128,1024]{1,0:T(8,128)(2,1)} %constant_dynamic-slice_fusion.q_ref, bf16[2,1152,128]{2,1,0:T(8,128)(2,1)} %copy-done.2, f32[1152,128]{1,0:T(8,128)} %broadcast_in_dim.61.offset_ref, f32[8,1,128]{2,1,0:T(1,128)} %bitcast.10, ...), custom_call_target="tpu_custom_call" | custom-call | flops 2415919104 | bytes 1769472 | tf_op jit(solution)/shard_map/pallas_call | solution.py:119
  76.3 4.1 %all-to-all-start.1 = ((bf16[8,64,1024]{2,1,0:T(8,128)(2,1)}), bf16[8,64,1024]{2,1,0:T(8,128)(2,1)S(1)}, u32[]{:S(2)}, u32[]{:S(2)}) async-start(bf16[8,64,1024]{2,1,0:T(8,128)(2,1)} %get-tuple-element.7), calls=%async_computation.1 | async-start | bytes 2097152 | tf_op jit(solution)/shard_map/all_to_all | solution.py:132
  80.3 27.7 %shard_map.50 = bf16[8,64,1024]{2,1,0:T(8,128)(2,1)} custom-call(bf16[128,1024]{1,0:T(8,128)(2,1)} %constant_dynamic-slice_fusion.q_ref, bf16[2,1152,128]{2,1,0:T(8,128)(2,1)} %copy-done.2, f32[1152,128]{1,0:T(8,128)} %broadcast_in_dim.61.offset_ref, f32[8,1,128]{2,1,0:T(1,128)} %bitcast.11, f32[128,1152]{1,0:T(8,128)} %and_select_fusion.bias_ref, ...), custom_call_target="tpu_custom_call" | custom-call | flops 2415919104 | bytes 1769472 | tf_op jit(solution)/shard_map/pallas_call | solution.py:133
  108.1 0.0 all-to-all-done.1
  108.1 20.9 %all_to_all.19 = bf16[8,64,1024]{2,1,0:T(8,128)(2,1)S(1)} all-to-all(bf16[8,64,1024]{2,1,0:T(8,128)(2,1)} %shard_map.50), channel_id=1, replica_groups=mesh['cand'=8,'doc'=64] {'cand'}, dimensions={0} | all-to-all | bytes 2097152 | tf_op jit(solution)/shard_map/all_to_all | solution.py:143
  129.0 1.5 %pad_maximum_fusion.in_ref = bf16[2,8,64,1024]{3,2,1,0:T(8,128)(2,1)} fusion(bf16[1,8,64,1024]{3,2,1,0:T(8,128)(2,1)S(1)} %bitcast.8, bf16[1,8,64,1024]{3,2,1,0:T(8,128)(2,1)S(1)} %bitcast.7), kind=kLoop, calls=%fused_computation | loop fusion | flops 1048576 | bytes 4194304 | tf_op jit(solution)/shard_map/stack | solution.py:153
  130.5 9.5 %shard_map.51 = bf16[128,8192]{1,0:T(8,128)(2,1)} custom-call(bf16[2,8,64,1024]{3,2,1,0:T(8,128)(2,1)} %pad_maximum_fusion.in_ref), custom_call_target="tpu_custom_call" | custom-call | tf_op jit(solution)/shard_map/pallas_call | solution.py:154
  (13 shorter events, 0.2 us)
Async XLA Ops:
  0.0 22.9 %copy-start = (bf16[128,8192]{1,0:T(8,128)(2,1)S(1)}, bf16[128,8192]{1,0:T(8,128)(2,1)}, u32[]{:S(2)}) copy-start(bf16[128,8192]{1,0:T(8,128)(2,1)} %param.4) | copy-start | bytes 6291460
  0.0 41.6 %copy-start.1 = (bf16[2,128,128]{2,1,0:T(8,128)(2,1)S(1)}, bf16[2,128,128]{2,1,0:T(8,128)(2,1)}, u32[]{:S(2)}) copy-start(bf16[2,128,128]{2,1,0:T(8,128)(2,1)} %param.5) | copy-start | bytes 196612
  0.0 17.3 %collective-permute-start.1 = (bf16[2,128,128]{2,1,0:T(8,128)(2,1)}, bf16[2,128,128]{2,1,0:T(8,128)(2,1)S(1)}, u32[]{:S(2)}, u32[]{:S(2)}) collective-permute-start(bf16[2,128,128]{2,1,0:T(8,128)(2,1)} %param.5), channel_id=1, source_target_pairs={{0,1},{1,2},{2,3},{3,4},{4,5},{5,6},{6,7},{7,8},{8,9},{9,10},{10,1... | collective-permute-start | bytes 196616 | tf_op jit(solution)/shard_map/ppermute | solution.py:22
  3.5 30.3 %collective-permute-start = (bf16[2,128,128]{2,1,0:T(8,128)(2,1)}, bf16[2,128,128]{2,1,0:T(8,128)(2,1)S(1)}, u32[]{:S(2)}, u32[]{:S(2)}) collective-permute-start(bf16[2,128,128]{2,1,0:T(8,128)(2,1)} %param.5), channel_id=1, source_target_pairs={{0,8},{1,9},{2,10},{3,11},{4,12},{5,13},{6,14},{7,15},{8,16},{9,17... | collective-permute-start | bytes 196616 | tf_op jit(solution)/shard_map/ppermute | solution.py:22
  10.0 23.1 %all-to-all-start = ((f32[8,1,64]{2,1,0:T(1,128)}), f32[8,1,64]{2,1,0:T(1,128)S(1)}, u32[]{:S(2)}, u32[]{:S(2)}) async-start(f32[8,1,64]{2,1,0:T(1,128)} %broadcast_in_dim.62), calls=%async_computation | async-start | bytes 8192 | tf_op jit(solution)/shard_map/all_to_all | solution.py:176
  18.2 11.4 %collective-permute-start.2 = (bf16[2,256,128]{2,1,0:T(8,128)(2,1)S(1)}, bf16[2,256,128]{2,1,0:T(8,128)(2,1)S(1)}, u32[]{:S(2)}, u32[]{:S(2)}) collective-permute-start(bf16[2,256,128]{2,1,0:T(8,128)(2,1)S(1)} %pad_maximum_fusion.2), channel_id=1, source_target_pairs={{0,2},{1,3},{2,4},{3,5},{4,6},{5,7},{6,8},{7,9},{8,10},{9,11},{10,... | collective-permute-start | bytes 393224 | tf_op jit(solution)/shard_map/ppermute | solution.py:22
  30.5 11.0 %collective-permute-start.3 = (bf16[2,512,128]{2,1,0:T(8,128)(2,1)S(1)}, bf16[2,512,128]{2,1,0:T(8,128)(2,1)S(1)}, u32[]{:S(2)}, u32[]{:S(2)}) collective-permute-start(bf16[2,512,128]{2,1,0:T(8,128)(2,1)S(1)} %pad_maximum_fusion.1), channel_id=1, source_target_pairs={{0,4},{1,5},{2,6},{3,7},{4,8},{5,9},{6,10},{7,11},{8,12},{9,13},{1... | collective-permute-start | bytes 786440 | tf_op jit(solution)/shard_map/ppermute | solution.py:22
  41.6 1.0 copy-start.2
  76.3 31.8 %all-to-all-start.1 = ((bf16[8,64,1024]{2,1,0:T(8,128)(2,1)}), bf16[8,64,1024]{2,1,0:T(8,128)(2,1)S(1)}, u32[]{:S(2)}, u32[]{:S(2)}) async-start(bf16[8,64,1024]{2,1,0:T(8,128)(2,1)} %get-tuple-element.7), calls=%async_computation.1 | async-start | bytes 2097152 | tf_op jit(solution)/shard_map/all_to_all | solution.py:132

commit v7 on v5

--- a/solution.py
+++ b/solution.py
@@ -69,19 +69,31 @@
     q_sin = sine[first_query:]
     bias = bias_ref[...]
     scale = 1.0 / math.sqrt(HD)
+    stacked = jnp.concatenate(
+        [
+            (
+                q_ref[:, head * HD : (head + 1) * HD].astype(jnp.float32) * q_cos
+                + pltpu.roll(q_ref[:, head * HD : (head + 1) * HD].astype(jnp.float32), half_dim, 1) * q_sin
+            ).astype(jnp.bfloat16)
+            for head in range(group_size)
+        ],
+        axis=0,
+    )
+    scores = lax.dot_general(
+        stacked, key_rot, (((1,), (1,)), ((), ())), preferred_element_type=jnp.float32
+    )
+    weights = []
+    totals = []
     for head in range(group_size):
-        cols = slice(head * HD, (head + 1) * HD)
-        x = q_ref[:, cols].astype(jnp.float32)
-        q_rot = (x * q_cos + pltpu.roll(x, half_dim, 1) * q_sin).astype(jnp.bfloat16)
-        scores = lax.dot_general(
-            q_rot, key_rot, (((1,), (1,)), ((), ())), preferred_element_type=jnp.float32
-        )
-        scores = scores * scale + bias
-        largest = jnp.max(scores, axis=-1, keepdims=True)
-        expw = jnp.exp(scores - largest)
-        total = jnp.sum(expw, axis=-1, keepdims=True)
-        numer = jnp.dot(expw.astype(jnp.bfloat16), values, preferred_element_type=jnp.float32)
-        out_ref[0, :, cols] = (numer / total).astype(jnp.bfloat16)
+        part = scores[head * query_rows : (head + 1) * query_rows] * scale + bias
+        largest = jnp.max(part, axis=-1, keepdims=True)
+        expw = jnp.exp(part - largest)
+        totals.append(jnp.sum(expw, axis=-1, keepdims=True))
+        weights.append(expw.astype(jnp.bfloat16))
+    numer = jnp.dot(jnp.concatenate(weights, axis=0), values, preferred_element_type=jnp.float32)
+    for head in range(group_size):
+        rows = numer[head * query_rows : (head + 1) * query_rows]
+        out_ref[0, :, head * HD : (head + 1) * HD] = (rows / totals[head]).astype(jnp.bfloat16)
 
 
 def attend_all(own_queries, window, offsets, inverse, bias):

time: 117 us -> 113 us (0.966)
  Pallas kernels: 41.5 us -> 38.3 us
    pallas_call x1, Pallas kernels: 35.9 us -> 32.6 us  [attend_all(): pl.pallas_call(attention_kernel, out_shape=jax.ShapeDtypeStruct((cands, q...]
where the time goes in v7:
time: 113 us
  Pallas kernels  38.3 us (34%)
  blocking collectives  31.8 us (28%)
  starting transfers between devices  20.4 us (18%)
  waiting for transfers between devices  13.7 us (12%)
  other arithmetic  4.56 us (4%)
  local copies, waits for them, and re-layouts  3.85 us (3%)
    pallas_call x1, Pallas kernels, attend_all(): pl.pallas_call(attention_kernel, out_shape=jax.ShapeDtypeStruct((cands, q...  32.6 us
    all_to_all x1, blocking collectives, on_device(): gathered = lax.all_to_all(mixed, 'cand', 0, 0, tiled=True)  31.8 us
    ppermute x4, starting transfers between devices, passed_along(): lax.ppermute(value, axis, [(source, source + steps) for source in range(f...  16 us
    ppermute x4, waiting for transfers between devices, passed_along(): lax.ppermute(value, axis, [(source, source + steps) for source in range(f...  13.7 us
    pallas_call x1, Pallas kernels, side_by_side(): pl.pallas_call(place_kernel, out_shape=jax.ShapeDtypeStruct((rows, count...  5.63 us
    all_to_all x1, starting transfers between devices, on_device(): lax.all_to_all(jnp.broadcast_to(factors, (cands, factors.shape[1])), 'can...  4.47 us
  transfers between devices with their start and end apart: 5, of which 2 were waited for; matrix products, arithmetic and copies ran while one was open for 6% of the time, Pallas kernels for 0%

profile of v7, /device:TPU:128, one launch (start us, length us, event | category | flops | bytes accessed | tf_op | source)
XLA Modules:
  0.0 112.8 jit_solution(1203794576728499230)
XLA Ops:
  0.0 0.0 copy-start
  0.0 0.0 copy-start.1
  0.0 3.5 %collective-permute-start.1 = (bf16[2,128,128]{2,1,0:T(8,128)(2,1)}, bf16[2,128,128]{2,1,0:T(8,128)(2,1)S(1)}, u32[]{:S(2)}, u32[]{:S(2)}) collective-permute-start(bf16[2,128,128]{2,1,0:T(8,128)(2,1)} %param.5), channel_id=1, source_target_pairs={{0,1},{1,2},{2,3},{3,4},{4,5},{5,6},{6,7},{7,8},{8,9},{9,10},{10,1... | collective-permute-start | bytes 196616 | tf_op jit(solution)/shard_map/ppermute | solution.py:22
  3.5 5.2 %collective-permute-start = (bf16[2,128,128]{2,1,0:T(8,128)(2,1)}, bf16[2,128,128]{2,1,0:T(8,128)(2,1)S(1)}, u32[]{:S(2)}, u32[]{:S(2)}) collective-permute-start(bf16[2,128,128]{2,1,0:T(8,128)(2,1)} %param.5), channel_id=1, source_target_pairs={{0,8},{1,9},{2,10},{3,11},{4,12},{5,13},{6,14},{7,15},{8,16},{9,17... | collective-permute-start | bytes 196616 | tf_op jit(solution)/shard_map/ppermute | solution.py:22
  8.7 1.3 %broadcast_in_dim.62 = f32[8,1,64]{2,1,0:T(1,128)} broadcast(f32[64]{0:T(128)} %bitcast.7), dimensions={2} | broadcast | bytes 2304 | tf_op jit(solution)/shard_map/broadcast_in_dim | solution.py:154
  10.0 4.5 %all-to-all-start = ((f32[8,1,64]{2,1,0:T(1,128)}), f32[8,1,64]{2,1,0:T(1,128)S(1)}, u32[]{:S(2)}, u32[]{:S(2)}) async-start(f32[8,1,64]{2,1,0:T(1,128)} %broadcast_in_dim.62), calls=%async_computation | async-start | bytes 8192 | tf_op jit(solution)/shard_map/all_to_all | solution.py:153
  14.5 0.7 copy.8
  15.2 0.1 reduce
  15.4 0.7 sub.14
  16.0 0.1 convert_reduce_fusion.1
  16.1 0.1 convert_reduce_fusion
  16.2 0.1 select_reduce_fusion
  16.3 1.1 and_select_fusion.bias_ref
  17.4 0.0 collective-permute-done.1
  17.4 0.9 pad_maximum_fusion.1
  18.2 4.6 %collective-permute-start.2 = (bf16[2,256,128]{2,1,0:T(8,128)(2,1)S(1)}, bf16[2,256,128]{2,1,0:T(8,128)(2,1)S(1)}, u32[]{:S(2)}, u32[]{:S(2)}) collective-permute-start(bf16[2,256,128]{2,1,0:T(8,128)(2,1)S(1)} %pad_maximum_fusion.1), channel_id=1, source_target_pairs={{0,2},{1,3},{2,4},{3,5},{4,6},{5,7},{6,8},{7,9},{8,10},{9,11},{10,... | collective-permute-start | bytes 393224 | tf_op jit(solution)/shard_map/ppermute | solution.py:22
  22.9 0.0 copy-done
  22.9 0.7 constant_dynamic-slice_fusion.q_ref
  23.6 6.0 %collective-permute-done.2 = bf16[2,256,128]{2,1,0:T(8,128)(2,1)S(1)} collective-permute-done((bf16[2,256,128]{2,1,0:T(8,128)(2,1)S(1)}, bf16[2,256,128]{2,1,0:T(8,128)(2,1)S(1)}, u32[]{:S(2)}, u32[]{:S(2)}) %collective-permute-start.2) | collective-permute-done | bytes 131104 | tf_op jit(solution)/shard_map/ppermute | solution.py:22
  29.6 0.9 pad_maximum_fusion
  30.5 2.6 %collective-permute-start.3 = (bf16[2,512,128]{2,1,0:T(8,128)(2,1)S(1)}, bf16[2,512,128]{2,1,0:T(8,128)(2,1)S(1)}, u32[]{:S(2)}, u32[]{:S(2)}) collective-permute-start(bf16[2,512,128]{2,1,0:T(8,128)(2,1)S(1)} %pad_maximum_fusion), channel_id=1, source_target_pairs={{0,4},{1,5},{2,6},{3,7},{4,8},{5,9},{6,10},{7,11},{8,12},{9,13},{1... | collective-permute-start | bytes 786440 | tf_op jit(solution)/shard_map/ppermute | solution.py:22
  33.1 0.0 all-to-all-done
  33.1 0.7 pad_maximum_fusion.2
  33.8 0.0 collective-permute-done
  33.8 7.7 %collective-permute-done.3 = bf16[2,512,128]{2,1,0:T(8,128)(2,1)S(1)} collective-permute-done((bf16[2,512,128]{2,1,0:T(8,128)(2,1)S(1)}, bf16[2,512,128]{2,1,0:T(8,128)(2,1)S(1)}, u32[]{:S(2)}, u32[]{:S(2)}) %collective-permute-start.3) | collective-permute-done | bytes 262176 | tf_op jit(solution)/shard_map/ppermute | solution.py:22
  41.6 0.0 copy-done.1
  41.6 0.0 copy-start.2
  41.7 1.0 broadcast_in_dim.61.offset_ref
  42.7 0.0 copy-done.2
  42.7 32.6 %shard_map.49 = bf16[8,128,1024]{2,1,0:T(8,128)(2,1)} custom-call(bf16[128,1024]{1,0:T(8,128)(2,1)} %constant_dynamic-slice_fusion.q_ref, bf16[2,1152,128]{2,1,0:T(8,128)(2,1)} %copy-done.2, f32[1152,128]{1,0:T(8,128)} %broadcast_in_dim.61.offset_ref, f32[8,1,128]{2,1,0:T(1,128)} %bitcast.6, f32[128,1152]{1,0:T(8,128)} %and_select_fusion.bias_ref), custom_call_target="tpu_custom_call" | custom-call | flops 4831838208 | bytes 2949120 | tf_op jit(solution)/shard_map/pallas_call | solution.py:105
  75.3 31.8 %all_to_all.14.in_ref = bf16[8,128,1024]{2,1,0:T(8,128)(2,1)} all-to-all(bf16[8,128,1024]{2,1,0:T(8,128)(2,1)} %shard_map.49), channel_id=1, replica_groups=mesh['cand'=8,'doc'=64] {'cand'}, dimensions={0} | all-to-all | bytes 4194304 | tf_op jit(solution)/shard_map/all_to_all | solution.py:174
  107.2 5.6 %shard_map.50 = bf16[128,8192]{1,0:T(8,128)(2,1)} custom-call(bf16[8,128,1024]{2,1,0:T(8,128)(2,1)} %all_to_all.14.in_ref), custom_call_target="tpu_custom_call" | custom-call | tf_op jit(solution)/shard_map/pallas_call | solution.py:131
  (13 shorter events, 0.2 us)
Async XLA Ops:
  0.0 22.9 %copy-start = (bf16[128,8192]{1,0:T(8,128)(2,1)S(1)}, bf16[128,8192]{1,0:T(8,128)(2,1)}, u32[]{:S(2)}) copy-start(bf16[128,8192]{1,0:T(8,128)(2,1)} %param.4) | copy-start | bytes 6291460
  0.0 41.6 %copy-start.1 = (bf16[2,128,128]{2,1,0:T(8,128)(2,1)S(1)}, bf16[2,128,128]{2,1,0:T(8,128)(2,1)}, u32[]{:S(2)}) copy-start(bf16[2,128,128]{2,1,0:T(8,128)(2,1)} %param.5) | copy-start | bytes 196612
  0.0 17.4 %collective-permute-start.1 = (bf16[2,128,128]{2,1,0:T(8,128)(2,1)}, bf16[2,128,128]{2,1,0:T(8,128)(2,1)S(1)}, u32[]{:S(2)}, u32[]{:S(2)}) collective-permute-start(bf16[2,128,128]{2,1,0:T(8,128)(2,1)} %param.5), channel_id=1, source_target_pairs={{0,1},{1,2},{2,3},{3,4},{4,5},{5,6},{6,7},{7,8},{8,9},{9,10},{10,1... | collective-permute-start | bytes 196616 | tf_op jit(solution)/shard_map/ppermute | solution.py:22
  3.5 30.3 %collective-permute-start = (bf16[2,128,128]{2,1,0:T(8,128)(2,1)}, bf16[2,128,128]{2,1,0:T(8,128)(2,1)S(1)}, u32[]{:S(2)}, u32[]{:S(2)}) collective-permute-start(bf16[2,128,128]{2,1,0:T(8,128)(2,1)} %param.5), channel_id=1, source_target_pairs={{0,8},{1,9},{2,10},{3,11},{4,12},{5,13},{6,14},{7,15},{8,16},{9,17... | collective-permute-start | bytes 196616 | tf_op jit(solution)/shard_map/ppermute | solution.py:22
  10.0 23.1 %all-to-all-start = ((f32[8,1,64]{2,1,0:T(1,128)}), f32[8,1,64]{2,1,0:T(1,128)S(1)}, u32[]{:S(2)}, u32[]{:S(2)}) async-start(f32[8,1,64]{2,1,0:T(1,128)} %broadcast_in_dim.62), calls=%async_computation | async-start | bytes 8192 | tf_op jit(solution)/shard_map/all_to_all | solution.py:153
  18.2 11.4 %collective-permute-start.2 = (bf16[2,256,128]{2,1,0:T(8,128)(2,1)S(1)}, bf16[2,256,128]{2,1,0:T(8,128)(2,1)S(1)}, u32[]{:S(2)}, u32[]{:S(2)}) collective-permute-start(bf16[2,256,128]{2,1,0:T(8,128)(2,1)S(1)} %pad_maximum_fusion.1), channel_id=1, source_target_pairs={{0,2},{1,3},{2,4},{3,5},{4,6},{5,7},{6,8},{7,9},{8,10},{9,11},{10,... | collective-permute-start | bytes 393224 | tf_op jit(solution)/shard_map/ppermute | solution.py:22
  30.5 11.0 %collective-permute-start.3 = (bf16[2,512,128]{2,1,0:T(8,128)(2,1)S(1)}, bf16[2,512,128]{2,1,0:T(8,128)(2,1)S(1)}, u32[]{:S(2)}, u32[]{:S(2)}) collective-permute-start(bf16[2,512,128]{2,1,0:T(8,128)(2,1)S(1)} %pad_maximum_fusion), channel_id=1, source_target_pairs={{0,4},{1,5},{2,6},{3,7},{4,8},{5,9},{6,10},{7,11},{8,12},{9,13},{1... | collective-permute-start | bytes 786440 | tf_op jit(solution)/shard_map/ppermute | solution.py:22
  41.6 1.0 copy-start.2

commit v8 on v7

--- a/solution.py
+++ b/solution.py
@@ -51,7 +51,7 @@
     return jnp.where(((quadrant + 1) & 2) != 0, -base, base)
 
 
-def attention_kernel(q_ref, kv_ref, offset_ref, inverse_ref, bias_ref, out_ref):
+def attention_kernel(q_ref, k_ref, vt_ref, offset_ref, inverse_ref, bias_ref, out_ref):
     half_dim = HD // 2
     group_size = H // KVH
     query_rows = q_ref.shape[0]
@@ -61,9 +61,8 @@
     swapped = pltpu.roll(table, half_dim, 1)
     cosine = jnp.where(low, table, swapped)
     sine = jnp.where(low, -swapped, table)
-    keys = kv_ref[0].astype(jnp.float32)
+    keys = k_ref[...].astype(jnp.float32)
     key_rot = (keys * cosine + pltpu.roll(keys, half_dim, 1) * sine).astype(jnp.bfloat16)
-    values = kv_ref[1]
     first_query = angle.shape[0] - query_rows
     q_cos = cosine[first_query:]
     q_sin = sine[first_query:]
@@ -80,23 +79,25 @@
         axis=0,
     )
     scores = lax.dot_general(
-        stacked, key_rot, (((1,), (1,)), ((), ())), preferred_element_type=jnp.float32
+        key_rot, stacked, (((1,), (1,)), ((), ())), preferred_element_type=jnp.float32
     )
     weights = []
     totals = []
     for head in range(group_size):
-        part = scores[head * query_rows : (head + 1) * query_rows] * scale + bias
-        largest = jnp.max(part, axis=-1, keepdims=True)
+        part = scores[:, head * query_rows : (head + 1) * query_rows] * scale + bias
+        largest = jnp.max(part, axis=0, keepdims=True)
         expw = jnp.exp(part - largest)
-        totals.append(jnp.sum(expw, axis=-1, keepdims=True))
+        totals.append(jnp.sum(expw, axis=0, keepdims=True))
         weights.append(expw.astype(jnp.bfloat16))
-    numer = jnp.dot(jnp.concatenate(weights, axis=0), values, preferred_element_type=jnp.float32)
+    numer = jnp.dot(vt_ref[...], jnp.concatenate(weights, axis=1), preferred_element_type=jnp.float32)
     for head in range(group_size):
-        rows = numer[head * query_rows : (head + 1) * query_rows]
-        out_ref[0, :, head * HD : (head + 1) * HD] = (rows / totals[head]).astype(jnp.bfloat16)
+        cols = numer[:, head * query_rows : (head + 1) * query_rows] / totals[head]
+        out_ref[0, :, head * HD : (head + 1) * HD] = cols.T.astype(jnp.bfloat16)
 
 
 def attend_all(own_queries, window, offsets, inverse, bias):
+    keys = window[0]
+    values_t = window[1].T
     cands = inverse.shape[0]
     key_rows = window.shape[1]
     query_rows, width = own_queries.shape
@@ -108,10 +109,11 @@
         grid=(cands,),
         in_specs=[
             pl.BlockSpec((query_rows, width), lambda c: (0, 0)),
-            pl.BlockSpec(window.shape, lambda c: (0, 0, 0)),
+            pl.BlockSpec(keys.shape, lambda c: (0, 0)),
+            pl.BlockSpec(values_t.shape, lambda c: (0, 0)),
             pl.BlockSpec(offsets.shape, lambda c: (0, 0)),
             pl.BlockSpec((1, 1, HD), lambda c: (c, 0, 0)),
-            pl.BlockSpec(bias.shape, lambda c: (0, 0)),
+            pl.BlockSpec(bias.T.shape, lambda c: (0, 0)),
         ],
         out_specs=pl.BlockSpec((1, query_rows, width), lambda c: (c, 0, 0)),
         cost_estimate=pl.CostEstimate(
@@ -119,11 +121,19 @@
             transcendentals=cands * heads * query_rows * key_rows,
             bytes_accessed=window.size * 2 + own_queries.size * 2 + cands * query_rows * width * 2,
         ),
-    )(own_queries, window, offsets, inverse, bias)
+    )(own_queries, keys, values_t, offsets, inverse, bias.T)
 
 
-def place_kernel(in_ref, out_ref):
-    out_ref[...] = in_ref[0]
+def place_kernel(in_ref, out_ref, flags):
+    count, _, width = in_ref.shape
+    copies = [
+        pltpu.make_async_copy(in_ref.at[g], out_ref.at[:, pl.ds(g * width, width)], flags.at[g])
+        for g in range(count)
+    ]
+    for copy in copies:
+        copy.start()
+    for copy in copies:
+        copy.wait()
 
 
 def side_by_side(blocks):
@@ -131,9 +141,9 @@
     return pl.pallas_call(
         place_kernel,
         out_shape=jax.ShapeDtypeStruct((rows, count * width), blocks.dtype),
-        grid=(count,),
-        in_specs=[pl.BlockSpec((1, rows, width), lambda g: (g, 0, 0))],
-        out_specs=pl.BlockSpec((rows, width), lambda g: (0, g)),
+        in_specs=[pl.BlockSpec(memory_space=pl.ANY)],
+        out_specs=pl.BlockSpec(memory_space=pl.ANY),
+        scratch_shapes=[pltpu.SemaphoreType.DMA((count,))],
     )(blocks)
 
 

time: 113 us -> 168 us (1.49)
  Pallas kernels: 38.3 us -> 91.3 us
  local copies, waits for them, and re-layouts: 3.85 us -> 6.58 us
    pallas_call x1, Pallas kernels: 5.63 us -> 64.7 us  [side_by_side(): pl.pallas_call(place_kernel, out_shape=jax.ShapeDtypeStruct((rows, count...]
    pallas_call x1, Pallas kernels: 32.6 us -> 26.6 us  [attend_all(): pl.pallas_call(attention_kernel, out_shape=jax.ShapeDtypeStruct((cands, q...]
  transfers between devices with their start and end apart: 5 -> 5, of which waited for: 2 -> 2; matrix products, arithmetic and copies ran while one was open for 6% -> 4% of each run, Pallas kernels for 0% -> 0%
where the time goes in v8:
time: 168 us
  Pallas kernels  91.3 us (54%)
  blocking collectives  31.8 us (19%)
  starting transfers between devices  20.3 us (12%)
  waiting for transfers between devices  13.7 us (8%)
  local copies, waits for them, and re-layouts  6.58 us (4%)
  other arithmetic  3.87 us (2%)
    pallas_call x1, Pallas kernels, side_by_side(): pl.pallas_call(place_kernel, out_shape=jax.ShapeDtypeStruct((rows, count...  64.7 us
    all_to_all x1, blocking collectives, on_device(): gathered = lax.all_to_all(mixed, 'cand', 0, 0, tiled=True)  31.8 us
    pallas_call x1, Pallas kernels, attend_all(): pl.pallas_call(attention_kernel, out_shape=jax.ShapeDtypeStruct((cands, q...  26.6 us
    ppermute x4, starting transfers between devices, passed_along(): lax.ppermute(value, axis, [(source, source + steps) for source in range(f...  15.8 us
    ppermute x4, waiting for transfers between devices, passed_along(): lax.ppermute(value, axis, [(source, source + steps) for source in range(f...  13.7 us
    all_to_all x1, starting transfers between devices, on_device(): lax.all_to_all(jnp.broadcast_to(factors, (cands, factors.shape[1])), 'can...  4.47 us
  transfers between devices with their start and end apart: 5, of which 2 were waited for; matrix products, arithmetic and copies ran while one was open for 4% of the time, Pallas kernels for 0%

profile of v8, /device:TPU:128, one launch (start us, length us, event | category | flops | bytes accessed | tf_op | source)
XLA Modules:
  0.0 167.8 jit_solution(5937629966003324590)
XLA Ops:
  0.0 0.0 copy-start
  0.0 1.1 copy.26
  1.1 3.4 %collective-permute-start.1 = (bf16[2,128,128]{1,2,0:T(8,128)(2,1)S(1)}, bf16[2,128,128]{1,2,0:T(8,128)(2,1)S(1)}, u32[]{:S(2)}, u32[]{:S(2)}) collective-permute-start(bf16[2,128,128]{1,2,0:T(8,128)(2,1)S(1)} %copy.26), channel_id=1, source_target_pairs={{0,1},{1,2},{2,3},{3,4},{4,5},{5,6},{6,7},{7,8},{8,9},{9,10},{10,1... | collective-permute-start | bytes 196616 | tf_op jit(solution)/shard_map/ppermute | solution.py:22
  4.5 5.2 %collective-permute-start = (bf16[2,128,128]{1,2,0:T(8,128)(2,1)S(1)}, bf16[2,128,128]{1,2,0:T(8,128)(2,1)S(1)}, u32[]{:S(2)}, u32[]{:S(2)}) collective-permute-start(bf16[2,128,128]{1,2,0:T(8,128)(2,1)S(1)} %copy.26), channel_id=1, source_target_pairs={{0,8},{1,9},{2,10},{3,11},{4,12},{5,13},{6,14},{7,15},{8,16},{9,17... | collective-permute-start | bytes 196616 | tf_op jit(solution)/shard_map/ppermute | solution.py:22
  9.7 1.3 broadcast_in_dim.62
  11.0 4.5 %all-to-all-start = ((f32[8,1,64]{2,1,0:T(1,128)}), f32[8,1,64]{2,1,0:T(1,128)S(1)}, u32[]{:S(2)}, u32[]{:S(2)}) async-start(f32[8,1,64]{2,1,0:T(1,128)} %broadcast_in_dim.62), calls=%async_computation | async-start | bytes 8192 | tf_op jit(solution)/shard_map/all_to_all | solution.py:163
  15.4 0.7 copy.31
  16.2 0.1 reduce
  16.3 0.7 sub.14
  17.0 0.1 convert_reduce_fusion.1
  17.1 0.1 convert_reduce_fusion
  17.2 0.1 select_reduce_fusion
  17.3 2.0 %and_select_fusion.bias_ref = f32[1152,128]{1,0:T(8,128)} fusion(s32[128]{0:T(128)S(1)} %iota_add_fusion.1, s32[128]{0:T(128)S(1)} %compare_select_fusion, s32[1152]{0:T(1024)S(1)} %iota_add_fusion, s32[1152]{0:T(1024)S(1)} %get-tuple-element.6, pred[1152]{0:T(1024)(128)(4,1)S(1)} %get-tuple-element.5), kind=kLoop, calls=%fused_computation | loop fusion | flops 737280 | bytes 601216 | tf_op jit(solution)/shard_map/jit(_where)/select_n | solution.py:180
  19.3 0.0 collective-permute-done.1
  19.4 4.6 %collective-permute-start.2 = (bf16[2,256,128]{1,2,0:T(8,128)(2,1)S(1)}, bf16[2,256,128]{1,2,0:T(8,128)(2,1)S(1)}, u32[]{:S(2)}, u32[]{:S(2)}) collective-permute-start(bf16[2,256,128]{1,2,0:T(8,128)(2,1)S(1)} %pad_maximum_fusion.1), channel_id=1, source_target_pairs={{0,2},{1,3},{2,4},{3,5},{4,6},{5,7},{6,8},{7,9},{8,10},{9,11},{10,... | collective-permute-start | bytes 393224 | tf_op jit(solution)/shard_map/ppermute | solution.py:22
  24.0 0.0 copy-done
  24.0 0.7 constant_dynamic-slice_fusion.q_ref
  24.8 6.0 %collective-permute-done.2 = bf16[2,256,128]{1,2,0:T(8,128)(2,1)S(1)} collective-permute-done((bf16[2,256,128]{1,2,0:T(8,128)(2,1)S(1)}, bf16[2,256,128]{1,2,0:T(8,128)(2,1)S(1)}, u32[]{:S(2)}, u32[]{:S(2)}) %collective-permute-start.2) | collective-permute-done | bytes 131104 | tf_op jit(solution)/shard_map/ppermute | solution.py:22
  30.8 2.6 %collective-permute-start.3 = (bf16[2,512,128]{1,2,0:T(8,128)(2,1)S(1)}, bf16[2,512,128]{1,2,0:T(8,128)(2,1)S(1)}, u32[]{:S(2)}, u32[]{:S(2)}) collective-permute-start(bf16[2,512,128]{1,2,0:T(8,128)(2,1)S(1)} %pad_maximum_fusion), channel_id=1, source_target_pairs={{0,4},{1,5},{2,6},{3,7},{4,8},{5,9},{6,10},{7,11},{8,12},{9,13},{1... | collective-permute-start | bytes 786440 | tf_op jit(solution)/shard_map/ppermute | solution.py:22
  33.4 0.0 all-to-all-done
  33.4 0.7 pad_maximum_fusion.2
  34.1 0.0 collective-permute-done
  34.1 7.7 %collective-permute-done.3 = bf16[2,512,128]{1,2,0:T(8,128)(2,1)S(1)} collective-permute-done((bf16[2,512,128]{1,2,0:T(8,128)(2,1)S(1)}, bf16[2,512,128]{1,2,0:T(8,128)(2,1)S(1)}, u32[]{:S(2)}, u32[]{:S(2)}) %collective-permute-start.3) | collective-permute-done | bytes 262176 | tf_op jit(solution)/shard_map/ppermute | solution.py:22
  41.9 0.8 slice_bitcast_fusion
  42.7 0.9 copy.32.k_ref
  43.6 1.0 broadcast_in_dim.61.offset_ref
  44.6 26.6 %shard_map.49 = bf16[8,128,1024]{2,1,0:T(8,128)(2,1)} custom-call(bf16[128,1024]{1,0:T(8,128)(2,1)} %constant_dynamic-slice_fusion.q_ref, bf16[1152,128]{1,0:T(8,128)(2,1)} %copy.32.k_ref, bf16[128,1152]{1,0:T(8,128)(2,1)} %get-tuple-element.7.vt_ref, f32[1152,128]{1,0:T(8,128)} %broadcast_in_dim.61.offset_ref, f32[8,1,128]{2,1,0:T(1,128)} %bitcast.12, ...), custom_call_target="tpu_custom_call" | custom-call | flops 4831838208 | bytes 2949120 | tf_op jit(solution)/shard_map/pallas_call | solution.py:106
  71.2 31.8 %all_to_all.14.in_ref = bf16[8,128,1024]{2,1,0:T(8,128)(2,1)} all-to-all(bf16[8,128,1024]{2,1,0:T(8,128)(2,1)} %shard_map.49), channel_id=1, replica_groups=mesh['cand'=8,'doc'=64] {'cand'}, dimensions={0} | all-to-all | bytes 4194304 | tf_op jit(solution)/shard_map/all_to_all | solution.py:184
  103.1 64.7 %shard_map.50 = bf16[128,8192]{1,0:T(8,128)(2,1)} custom-call(bf16[8,128,1024]{2,1,0:T(8,128)(2,1)} %all_to_all.14.in_ref), custom_call_target="tpu_custom_call" | custom-call | tf_op jit(solution)/shard_map/pallas_call | solution.py:141
  (15 shorter events, 0.2 us)
Async XLA Ops:
  0.0 24.0 %copy-start = (bf16[128,8192]{1,0:T(8,128)(2,1)S(1)}, bf16[128,8192]{1,0:T(8,128)(2,1)}, u32[]{:S(2)}) copy-start(bf16[128,8192]{1,0:T(8,128)(2,1)} %param.4) | copy-start | bytes 6291460
  1.1 18.2 %collective-permute-start.1 = (bf16[2,128,128]{1,2,0:T(8,128)(2,1)S(1)}, bf16[2,128,128]{1,2,0:T(8,128)(2,1)S(1)}, u32[]{:S(2)}, u32[]{:S(2)}) collective-permute-start(bf16[2,128,128]{1,2,0:T(8,128)(2,1)S(1)} %copy.26), channel_id=1, source_target_pairs={{0,1},{1,2},{2,3},{3,4},{4,5},{5,6},{6,7},{7,8},{8,9},{9,10},{10,1... | collective-permute-start | bytes 196616 | tf_op jit(solution)/shard_map/ppermute | solution.py:22
  4.5 29.6 %collective-permute-start = (bf16[2,128,128]{1,2,0:T(8,128)(2,1)S(1)}, bf16[2,128,128]{1,2,0:T(8,128)(2,1)S(1)}, u32[]{:S(2)}, u32[]{:S(2)}) collective-permute-start(bf16[2,128,128]{1,2,0:T(8,128)(2,1)S(1)} %copy.26), channel_id=1, source_target_pairs={{0,8},{1,9},{2,10},{3,11},{4,12},{5,13},{6,14},{7,15},{8,16},{9,17... | collective-permute-start | bytes 196616 | tf_op jit(solution)/shard_map/ppermute | solution.py:22
  11.0 22.5 %all-to-all-start = ((f32[8,1,64]{2,1,0:T(1,128)}), f32[8,1,64]{2,1,0:T(1,128)S(1)}, u32[]{:S(2)}, u32[]{:S(2)}) async-start(f32[8,1,64]{2,1,0:T(1,128)} %broadcast_in_dim.62), calls=%async_computation | async-start | bytes 8192 | tf_op jit(solution)/shard_map/all_to_all | solution.py:163
  19.4 11.4 %collective-permute-start.2 = (bf16[2,256,128]{1,2,0:T(8,128)(2,1)S(1)}, bf16[2,256,128]{1,2,0:T(8,128)(2,1)S(1)}, u32[]{:S(2)}, u32[]{:S(2)}) collective-permute-start(bf16[2,256,128]{1,2,0:T(8,128)(2,1)S(1)} %pad_maximum_fusion.1), channel_id=1, source_target_pairs={{0,2},{1,3},{2,4},{3,5},{4,6},{5,7},{6,8},{7,9},{8,10},{9,11},{10,... | collective-permute-start | bytes 393224 | tf_op jit(solution)/shard_map/ppermute | solution.py:22
  30.8 11.0 %collective-permute-start.3 = (bf16[2,512,128]{1,2,0:T(8,128)(2,1)S(1)}, bf16[2,512,128]{1,2,0:T(8,128)(2,1)S(1)}, u32[]{:S(2)}, u32[]{:S(2)}) collective-permute-start(bf16[2,512,128]{1,2,0:T(8,128)(2,1)S(1)} %pad_maximum_fusion), channel_id=1, source_target_pairs={{0,4},{1,5},{2,6},{3,7},{4,8},{5,9},{6,10},{7,11},{8,12},{9,13},{1... | collective-permute-start | bytes 786440 | tf_op jit(solution)/shard_map/ppermute | solution.py:22

commit v9 on v8

--- a/solution.py
+++ b/solution.py
@@ -124,16 +124,8 @@
     )(own_queries, keys, values_t, offsets, inverse, bias.T)
 
 
-def place_kernel(in_ref, out_ref, flags):
-    count, _, width = in_ref.shape
-    copies = [
-        pltpu.make_async_copy(in_ref.at[g], out_ref.at[:, pl.ds(g * width, width)], flags.at[g])
-        for g in range(count)
-    ]
-    for copy in copies:
-        copy.start()
-    for copy in copies:
-        copy.wait()
+def place_kernel(in_ref, out_ref):
+    out_ref[...] = in_ref[0]
 
 
 def side_by_side(blocks):
@@ -141,9 +133,9 @@
     return pl.pallas_call(
         place_kernel,
         out_shape=jax.ShapeDtypeStruct((rows, count * width), blocks.dtype),
-        in_specs=[pl.BlockSpec(memory_space=pl.ANY)],
-        out_specs=pl.BlockSpec(memory_space=pl.ANY),
-        scratch_shapes=[pltpu.SemaphoreType.DMA((count,))],
+        grid=(count,),
+        in_specs=[pl.BlockSpec((1, rows, width), lambda g: (g, 0, 0))],
+        out_specs=pl.BlockSpec((rows, width), lambda g: (0, g)),
     )(blocks)
 
 

time: 168 us -> 109 us (0.65)
  Pallas kernels: 91.3 us -> 32.3 us
    pallas_call x1, Pallas kernels: 64.7 us -> 5.63 us  [side_by_side(): pl.pallas_call(place_kernel, out_shape=jax.ShapeDtypeStruct((rows, count...]
  transfers between devices with their start and end apart: 5 -> 5, of which waited for: 2 -> 2; matrix products, arithmetic and copies ran while one was open for 4% -> 6% of each run, Pallas kernels for 0% -> 0%
where the time goes in v9:
time: 109 us
  Pallas kernels  32.3 us (30%)
  blocking collectives  31.8 us (29%)
  starting transfers between devices  20.3 us (19%)
  waiting for transfers between devices  13.7 us (13%)
  local copies, waits for them, and re-layouts  6.58 us (6%)
  other arithmetic  3.87 us (4%)
    all_to_all x1, blocking collectives, on_device(): gathered = lax.all_to_all(mixed, 'cand', 0, 0, tiled=True)  31.8 us
    pallas_call x1, Pallas kernels, attend_all(): pl.pallas_call(attention_kernel, out_shape=jax.ShapeDtypeStruct((cands, q...  26.6 us
    ppermute x4, starting transfers between devices, passed_along(): lax.ppermute(value, axis, [(source, source + steps) for source in range(f...  15.8 us
    ppermute x4, waiting for transfers between devices, passed_along(): lax.ppermute(value, axis, [(source, source + steps) for source in range(f...  13.7 us
    pallas_call x1, Pallas kernels, side_by_side(): pl.pallas_call(place_kernel, out_shape=jax.ShapeDtypeStruct((rows, count...  5.63 us
    all_to_all x1, starting transfers between devices, on_device(): lax.all_to_all(jnp.broadcast_to(factors, (cands, factors.shape[1])), 'can...  4.47 us
  transfers between devices with their start and end apart: 5, of which 2 were waited for; matrix products, arithmetic and copies ran while one was open for 6% of the time, Pallas kernels for 0%

profile of v9, /device:TPU:128, one launch (start us, length us, event | category | flops | bytes accessed | tf_op | source)
XLA Modules:
  0.0 108.7 jit_solution(1285616182814998333)
XLA Ops:
  0.0 0.0 copy-start
  0.0 1.1 %copy.26 = bf16[2,128,128]{1,2,0:T(8,128)(2,1)S(1)} copy(bf16[2,128,128]{2,1,0:T(8,128)(2,1)} %param.5) | data formatting | bytes 131072 | tf_op args[1]
  1.1 3.4 %collective-permute-start.1 = (bf16[2,128,128]{1,2,0:T(8,128)(2,1)S(1)}, bf16[2,128,128]{1,2,0:T(8,128)(2,1)S(1)}, u32[]{:S(2)}, u32[]{:S(2)}) collective-permute-start(bf16[2,128,128]{1,2,0:T(8,128)(2,1)S(1)} %copy.26), channel_id=1, source_target_pairs={{0,1},{1,2},{2,3},{3,4},{4,5},{5,6},{6,7},{7,8},{8,9},{9,10},{10,1... | collective-permute-start | bytes 196616 | tf_op jit(solution)/shard_map/ppermute | solution.py:22
  4.5 5.2 %collective-permute-start = (bf16[2,128,128]{1,2,0:T(8,128)(2,1)S(1)}, bf16[2,128,128]{1,2,0:T(8,128)(2,1)S(1)}, u32[]{:S(2)}, u32[]{:S(2)}) collective-permute-start(bf16[2,128,128]{1,2,0:T(8,128)(2,1)S(1)} %copy.26), channel_id=1, source_target_pairs={{0,8},{1,9},{2,10},{3,11},{4,12},{5,13},{6,14},{7,15},{8,16},{9,17... | collective-permute-start | bytes 196616 | tf_op jit(solution)/shard_map/ppermute | solution.py:22
  9.7 1.3 %broadcast_in_dim.62 = f32[8,1,64]{2,1,0:T(1,128)} broadcast(f32[64]{0:T(128)} %bitcast.13), dimensions={2} | broadcast | bytes 2304 | tf_op jit(solution)/shard_map/broadcast_in_dim | solution.py:156
  11.0 4.5 %all-to-all-start = ((f32[8,1,64]{2,1,0:T(1,128)}), f32[8,1,64]{2,1,0:T(1,128)S(1)}, u32[]{:S(2)}, u32[]{:S(2)}) async-start(f32[8,1,64]{2,1,0:T(1,128)} %broadcast_in_dim.62), calls=%async_computation | async-start | bytes 8192 | tf_op jit(solution)/shard_map/all_to_all | solution.py:155
  15.4 0.7 copy.31
  16.2 0.1 reduce
  16.3 0.7 sub.14
  17.0 0.1 convert_reduce_fusion.1
  17.1 0.1 convert_reduce_fusion
  17.2 0.1 select_reduce_fusion
  17.3 2.0 %and_select_fusion.bias_ref = f32[1152,128]{1,0:T(8,128)} fusion(s32[128]{0:T(128)S(1)} %iota_add_fusion.1, s32[128]{0:T(128)S(1)} %compare_select_fusion, s32[1152]{0:T(1024)S(1)} %iota_add_fusion, s32[1152]{0:T(1024)S(1)} %get-tuple-element.6, pred[1152]{0:T(1024)(128)(4,1)S(1)} %get-tuple-element.5), kind=kLoop, calls=%fused_computation | loop fusion | flops 737280 | bytes 601216 | tf_op jit(solution)/shard_map/jit(_where)/select_n | solution.py:172
  19.3 0.0 collective-permute-done.1
  19.4 4.6 %collective-permute-start.2 = (bf16[2,256,128]{1,2,0:T(8,128)(2,1)S(1)}, bf16[2,256,128]{1,2,0:T(8,128)(2,1)S(1)}, u32[]{:S(2)}, u32[]{:S(2)}) collective-permute-start(bf16[2,256,128]{1,2,0:T(8,128)(2,1)S(1)} %pad_maximum_fusion.1), channel_id=1, source_target_pairs={{0,2},{1,3},{2,4},{3,5},{4,6},{5,7},{6,8},{7,9},{8,10},{9,11},{10,... | collective-permute-start | bytes 393224 | tf_op jit(solution)/shard_map/ppermute | solution.py:22
  24.0 0.0 copy-done
  24.0 0.7 constant_dynamic-slice_fusion.q_ref
  24.8 6.0 %collective-permute-done.2 = bf16[2,256,128]{1,2,0:T(8,128)(2,1)S(1)} collective-permute-done((bf16[2,256,128]{1,2,0:T(8,128)(2,1)S(1)}, bf16[2,256,128]{1,2,0:T(8,128)(2,1)S(1)}, u32[]{:S(2)}, u32[]{:S(2)}) %collective-permute-start.2) | collective-permute-done | bytes 131104 | tf_op jit(solution)/shard_map/ppermute | solution.py:22
  30.8 2.6 %collective-permute-start.3 = (bf16[2,512,128]{1,2,0:T(8,128)(2,1)S(1)}, bf16[2,512,128]{1,2,0:T(8,128)(2,1)S(1)}, u32[]{:S(2)}, u32[]{:S(2)}) collective-permute-start(bf16[2,512,128]{1,2,0:T(8,128)(2,1)S(1)} %pad_maximum_fusion), channel_id=1, source_target_pairs={{0,4},{1,5},{2,6},{3,7},{4,8},{5,9},{6,10},{7,11},{8,12},{9,13},{1... | collective-permute-start | bytes 786440 | tf_op jit(solution)/shard_map/ppermute | solution.py:22
  33.4 0.0 all-to-all-done
  33.4 0.7 pad_maximum_fusion.2
  34.1 0.0 collective-permute-done
  34.1 7.7 %collective-permute-done.3 = bf16[2,512,128]{1,2,0:T(8,128)(2,1)S(1)} collective-permute-done((bf16[2,512,128]{1,2,0:T(8,128)(2,1)S(1)}, bf16[2,512,128]{1,2,0:T(8,128)(2,1)S(1)}, u32[]{:S(2)}, u32[]{:S(2)}) %collective-permute-start.3) | collective-permute-done | bytes 262176 | tf_op jit(solution)/shard_map/ppermute | solution.py:22
  41.9 0.8 slice_bitcast_fusion
  42.7 0.9 copy.32.k_ref
  43.6 1.0 broadcast_in_dim.61.offset_ref
  44.6 26.6 %shard_map.49 = bf16[8,128,1024]{2,1,0:T(8,128)(2,1)} custom-call(bf16[128,1024]{1,0:T(8,128)(2,1)} %constant_dynamic-slice_fusion.q_ref, bf16[1152,128]{1,0:T(8,128)(2,1)} %copy.32.k_ref, bf16[128,1152]{1,0:T(8,128)(2,1)} %get-tuple-element.7.vt_ref, f32[1152,128]{1,0:T(8,128)} %broadcast_in_dim.61.offset_ref, f32[8,1,128]{2,1,0:T(1,128)} %bitcast.12, ...), custom_call_target="tpu_custom_call" | custom-call | flops 4831838208 | bytes 2949120 | tf_op jit(solution)/shard_map/pallas_call | solution.py:106
  71.2 31.8 %all_to_all.14.in_ref = bf16[8,128,1024]{2,1,0:T(8,128)(2,1)} all-to-all(bf16[8,128,1024]{2,1,0:T(8,128)(2,1)} %shard_map.49), channel_id=1, replica_groups=mesh['cand'=8,'doc'=64] {'cand'}, dimensions={0} | all-to-all | bytes 4194304 | tf_op jit(solution)/shard_map/all_to_all | solution.py:176
  103.1 5.6 %shard_map.50 = bf16[128,8192]{1,0:T(8,128)(2,1)} custom-call(bf16[8,128,1024]{2,1,0:T(8,128)(2,1)} %all_to_all.14.in_ref), custom_call_target="tpu_custom_call" | custom-call | tf_op jit(solution)/shard_map/pallas_call | solution.py:133
  (15 shorter events, 0.2 us)
Async XLA Ops:
  0.0 24.0 %copy-start = (bf16[128,8192]{1,0:T(8,128)(2,1)S(1)}, bf16[128,8192]{1,0:T(8,128)(2,1)}, u32[]{:S(2)}) copy-start(bf16[128,8192]{1,0:T(8,128)(2,1)} %param.4) | copy-start | bytes 6291460
  1.1 18.2 %collective-permute-start.1 = (bf16[2,128,128]{1,2,0:T(8,128)(2,1)S(1)}, bf16[2,128,128]{1,2,0:T(8,128)(2,1)S(1)}, u32[]{:S(2)}, u32[]{:S(2)}) collective-permute-start(bf16[2,128,128]{1,2,0:T(8,128)(2,1)S(1)} %copy.26), channel_id=1, source_target_pairs={{0,1},{1,2},{2,3},{3,4},{4,5},{5,6},{6,7},{7,8},{8,9},{9,10},{10,1... | collective-permute-start | bytes 196616 | tf_op jit(solution)/shard_map/ppermute | solution.py:22
  4.5 29.6 %collective-permute-start = (bf16[2,128,128]{1,2,0:T(8,128)(2,1)S(1)}, bf16[2,128,128]{1,2,0:T(8,128)(2,1)S(1)}, u32[]{:S(2)}, u32[]{:S(2)}) collective-permute-start(bf16[2,128,128]{1,2,0:T(8,128)(2,1)S(1)} %copy.26), channel_id=1, source_target_pairs={{0,8},{1,9},{2,10},{3,11},{4,12},{5,13},{6,14},{7,15},{8,16},{9,17... | collective-permute-start | bytes 196616 | tf_op jit(solution)/shard_map/ppermute | solution.py:22
  11.0 22.5 %all-to-all-start = ((f32[8,1,64]{2,1,0:T(1,128)}), f32[8,1,64]{2,1,0:T(1,128)S(1)}, u32[]{:S(2)}, u32[]{:S(2)}) async-start(f32[8,1,64]{2,1,0:T(1,128)} %broadcast_in_dim.62), calls=%async_computation | async-start | bytes 8192 | tf_op jit(solution)/shard_map/all_to_all | solution.py:155
  19.4 11.4 %collective-permute-start.2 = (bf16[2,256,128]{1,2,0:T(8,128)(2,1)S(1)}, bf16[2,256,128]{1,2,0:T(8,128)(2,1)S(1)}, u32[]{:S(2)}, u32[]{:S(2)}) collective-permute-start(bf16[2,256,128]{1,2,0:T(8,128)(2,1)S(1)} %pad_maximum_fusion.1), channel_id=1, source_target_pairs={{0,2},{1,3},{2,4},{3,5},{4,6},{5,7},{6,8},{7,9},{8,10},{9,11},{10,... | collective-permute-start | bytes 393224 | tf_op jit(solution)/shard_map/ppermute | solution.py:22
  30.8 11.0 %collective-permute-start.3 = (bf16[2,512,128]{1,2,0:T(8,128)(2,1)S(1)}, bf16[2,512,128]{1,2,0:T(8,128)(2,1)S(1)}, u32[]{:S(2)}, u32[]{:S(2)}) collective-permute-start(bf16[2,512,128]{1,2,0:T(8,128)(2,1)S(1)} %pad_maximum_fusion), channel_id=1, source_target_pairs={{0,4},{1,5},{2,6},{3,7},{4,8},{5,9},{6,10},{7,11},{8,12},{9,13},{1... | collective-permute-start | bytes 786440 | tf_op jit(solution)/shard_map/ppermute | solution.py:22

commit v10 on v9

--- a/solution.py
+++ b/solution.py
@@ -51,19 +51,18 @@
     return jnp.where(((quadrant + 1) & 2) != 0, -base, base)
 
 
-def attention_kernel(q_ref, k_ref, vt_ref, offset_ref, inverse_ref, bias_ref, out_ref):
+def attention_kernel(q_ref, k_ref, vt_ref, table_ref, bias_ref, out_ref):
     half_dim = HD // 2
     group_size = H // KVH
     query_rows = q_ref.shape[0]
-    angle = offset_ref[...] * inverse_ref[0]
-    low = lax.broadcasted_iota(jnp.int32, angle.shape, 1) < half_dim
-    table = cos_and_sin(angle, low)
+    table = table_ref[0]
+    low = lax.broadcasted_iota(jnp.int32, table.shape, 1) < half_dim
     swapped = pltpu.roll(table, half_dim, 1)
     cosine = jnp.where(low, table, swapped)
     sine = jnp.where(low, -swapped, table)
     keys = k_ref[...].astype(jnp.float32)
     key_rot = (keys * cosine + pltpu.roll(keys, half_dim, 1) * sine).astype(jnp.bfloat16)
-    first_query = angle.shape[0] - query_rows
+    first_query = table.shape[0] - query_rows
     q_cos = cosine[first_query:]
     q_sin = sine[first_query:]
     bias = bias_ref[...]
@@ -96,6 +95,9 @@
 
 
 def attend_all(own_queries, window, offsets, inverse, bias):
+    angle = offsets[None] * inverse
+    low = lax.broadcasted_iota(jnp.int32, angle.shape, 2) < HD // 2
+    table = cos_and_sin(angle, low)
     keys = window[0]
     values_t = window[1].T
     cands = inverse.shape[0]
@@ -111,8 +113,7 @@
             pl.BlockSpec((query_rows, width), lambda c: (0, 0)),
             pl.BlockSpec(keys.shape, lambda c: (0, 0)),
             pl.BlockSpec(values_t.shape, lambda c: (0, 0)),
-            pl.BlockSpec(offsets.shape, lambda c: (0, 0)),
-            pl.BlockSpec((1, 1, HD), lambda c: (c, 0, 0)),
+            pl.BlockSpec((1, key_rows, HD), lambda c: (c, 0, 0)),
             pl.BlockSpec(bias.T.shape, lambda c: (0, 0)),
         ],
         out_specs=pl.BlockSpec((1, query_rows, width), lambda c: (c, 0, 0)),
@@ -121,7 +122,7 @@
             transcendentals=cands * heads * query_rows * key_rows,
             bytes_accessed=window.size * 2 + own_queries.size * 2 + cands * query_rows * width * 2,
         ),
-    )(own_queries, keys, values_t, offsets, inverse, bias.T)
+    )(own_queries, keys, values_t, table, bias.T)
 
 
 def place_kernel(in_ref, out_ref):

time: 109 us -> 104 us (0.954)
  the two profiles are of different devices: /device:TPU:128 before, /device:TPU:96 now
where the time goes in v10:
time: 104 us
  blocking collectives  32.1 us (31%)
  Pallas kernels  26 us (25%)
  starting transfers between devices  23.9 us (23%)
  other arithmetic  10.4 us (10%)
  local copies, waits for them, and re-layouts  5.53 us (5%)
  waiting for transfers between devices  5.47 us (5%)
    all_to_all x1, blocking collectives, on_device(): gathered = lax.all_to_all(mixed, 'cand', 0, 0, tiled=True)  32.1 us
    pallas_call x1, Pallas kernels, attend_all(): pl.pallas_call(attention_kernel, out_shape=jax.ShapeDtypeStruct((cands, q...  20.4 us
    ppermute x4, starting transfers between devices, passed_along(): lax.ppermute(value, axis, [(source, source + steps) for source in range(f...  19.5 us
    select_n x1, other arithmetic, cos_and_sin(): return jnp.where(quadrant + 1 & 2 != 0, -base, base)  7.16 us
    pallas_call x1, Pallas kernels, side_by_side(): pl.pallas_call(place_kernel, out_shape=jax.ShapeDtypeStruct((rows, count...  5.63 us
    ppermute x4, waiting for transfers between devices, passed_along(): lax.ppermute(value, axis, [(source, source + steps) for source in range(f...  5.47 us
    all_to_all x1, starting transfers between devices, on_device(): lax.all_to_all(jnp.broadcast_to(factors, (cands, factors.shape[1])), 'can...  4.47 us
  transfers between devices with their start and end apart: 5, of which 1 were waited for; matrix products, arithmetic and copies ran while one was open for 13% of the time, Pallas kernels for 0%

profile of v10, /device:TPU:96, one launch (start us, length us, event | category | flops | bytes accessed | tf_op | source)
XLA Modules:
  0.0 103.6 jit_solution(11706127332192790151)
XLA Ops:
  0.0 0.0 copy-start
  0.0 1.1 %copy.26 = bf16[2,128,128]{1,2,0:T(8,128)(2,1)S(1)} copy(bf16[2,128,128]{2,1,0:T(8,128)(2,1)} %param.5) | data formatting | bytes 131072 | tf_op args[1]
  1.1 3.4 %collective-permute-start.1 = (bf16[2,128,128]{1,2,0:T(8,128)(2,1)S(1)}, bf16[2,128,128]{1,2,0:T(8,128)(2,1)S(1)}, u32[]{:S(2)}, u32[]{:S(2)}) collective-permute-start(bf16[2,128,128]{1,2,0:T(8,128)(2,1)S(1)} %copy.26), channel_id=1, source_target_pairs={{0,1},{1,2},{2,3},{3,4},{4,5},{5,6},{6,7},{7,8},{8,9},{9,10},{10,1... | collective-permute-start | bytes 196616 | tf_op jit(solution)/shard_map/ppermute | solution.py:22
  4.5 6.4 %collective-permute-start = (bf16[2,128,128]{1,2,0:T(8,128)(2,1)S(1)}, bf16[2,128,128]{1,2,0:T(8,128)(2,1)S(1)}, u32[]{:S(2)}, u32[]{:S(2)}) collective-permute-start(bf16[2,128,128]{1,2,0:T(8,128)(2,1)S(1)} %copy.26), channel_id=1, source_target_pairs={{0,8},{1,9},{2,10},{3,11},{4,12},{5,13},{6,14},{7,15},{8,16},{9,17... | collective-permute-start | bytes 196616 | tf_op jit(solution)/shard_map/ppermute | solution.py:22
  10.9 1.3 %broadcast_in_dim.64 = f32[8,1,64]{2,1,0:T(1,128)} broadcast(f32[64]{0:T(128)} %bitcast.11), dimensions={2} | broadcast | bytes 2304 | tf_op jit(solution)/shard_map/broadcast_in_dim | solution.py:157
  12.2 4.5 %all-to-all-start = ((f32[8,1,64]{2,1,0:T(1,128)}), f32[8,1,64]{2,1,0:T(1,128)S(1)}, u32[]{:S(2)}, u32[]{:S(2)}) async-start(f32[8,1,64]{2,1,0:T(1,128)} %broadcast_in_dim.64), calls=%async_computation | async-start | bytes 8192 | tf_op jit(solution)/shard_map/all_to_all | solution.py:156
  16.7 0.7 copy.31
  17.4 0.1 reduce
  17.6 0.7 sub.25
  18.2 0.1 convert_reduce_fusion.1
  18.3 0.1 convert_reduce_fusion
  18.4 0.1 select_reduce_fusion
  18.5 0.0 copy-done
  18.5 0.7 constant_dynamic-slice_fusion.q_ref
  19.3 2.0 %and_select_fusion.bias_ref = f32[1152,128]{1,0:T(8,128)} fusion(s32[128]{0:T(128)S(1)} %iota_add_fusion.1, s32[128]{0:T(128)S(1)} %compare_select_fusion, s32[1152]{0:T(1024)S(1)} %iota_add_fusion, s32[1152]{0:T(1024)S(1)} %get-tuple-element.6, pred[1152]{0:T(1024)(128)(4,1)S(1)} %get-tuple-element.5), kind=kLoop, calls=%fused_computation.34 | loop fusion | flops 737280 | bytes 601216 | tf_op jit(solution)/shard_map/jit(_where)/select_n | solution.py:173
  21.3 0.0 collective-permute-done.1
  21.3 4.6 %collective-permute-start.2 = (bf16[2,256,128]{1,2,0:T(8,128)(2,1)S(1)}, bf16[2,256,128]{1,2,0:T(8,128)(2,1)S(1)}, u32[]{:S(2)}, u32[]{:S(2)}) collective-permute-start(bf16[2,256,128]{1,2,0:T(8,128)(2,1)S(1)} %pad_maximum_fusion.1), channel_id=1, source_target_pairs={{0,2},{1,3},{2,4},{3,5},{4,6},{5,7},{6,8},{7,9},{8,10},{9,11},{10,... | collective-permute-start | bytes 393224 | tf_op jit(solution)/shard_map/ppermute | solution.py:22
  26.0 0.0 all-to-all-done
  26.0 0.1 pad_maximum_fusion.2
  26.1 5.5 %collective-permute-done.2 = bf16[2,256,128]{1,2,0:T(8,128)(2,1)S(1)} collective-permute-done((bf16[2,256,128]{1,2,0:T(8,128)(2,1)S(1)}, bf16[2,256,128]{1,2,0:T(8,128)(2,1)S(1)}, u32[]{:S(2)}, u32[]{:S(2)}) %collective-permute-start.2) | collective-permute-done | bytes 131104 | tf_op jit(solution)/shard_map/ppermute | solution.py:22
  31.5 5.0 %collective-permute-start.3 = (bf16[2,512,128]{1,2,0:T(8,128)(2,1)S(1)}, bf16[2,512,128]{1,2,0:T(8,128)(2,1)S(1)}, u32[]{:S(2)}, u32[]{:S(2)}) collective-permute-start(bf16[2,512,128]{1,2,0:T(8,128)(2,1)S(1)} %pad_maximum_fusion), channel_id=1, source_target_pairs={{0,4},{1,5},{2,6},{3,7},{4,8},{5,9},{6,10},{7,11},{8,12},{9,13},{1... | collective-permute-start | bytes 786440 | tf_op jit(solution)/shard_map/ppermute | solution.py:22
  36.6 7.2 %negate_select_fusion.table_ref = f32[8,1152,128]{2,1,0:T(8,128)} fusion(s32[128]{0:T(128)S(1)} %compare_select_fusion.1, f32[8,128]{1,0:T(8,128)S(1)} %pad_maximum_fusion.2, f32[1152]{0:T(1024)S(1)} %select_convert_fusion), kind=kLoop, calls=%fused_computation | loop fusion | flops 43646976 | bytes 4727808 | tf_op jit(solution)/shard_map/jit(_where)/select_n | solution.py:51
  43.8 0.0 collective-permute-done
  43.8 0.0 collective-permute-done.3
  43.9 0.8 slice_bitcast_fusion
  44.6 0.9 copy.32.k_ref
  45.5 20.4 %shard_map.49 = bf16[8,128,1024]{2,1,0:T(8,128)(2,1)} custom-call(bf16[128,1024]{1,0:T(8,128)(2,1)} %constant_dynamic-slice_fusion.q_ref, bf16[1152,128]{1,0:T(8,128)(2,1)} %copy.32.k_ref, bf16[128,1152]{1,0:T(8,128)(2,1)} %get-tuple-element.7.vt_ref, f32[8,1152,128]{2,1,0:T(8,128)} %negate_select_fusion.table_ref, f32[1152,128]{1,0:T(8,128)} %and_select_fusion.bias_ref), custom_call_target="tpu_custom_call" | custom-call | flops 4831838208 | bytes 2949120 | tf_op jit(solution)/shard_map/pallas_call | solution.py:108
  65.9 32.1 %all_to_all.14.in_ref = bf16[8,128,1024]{2,1,0:T(8,128)(2,1)} all-to-all(bf16[8,128,1024]{2,1,0:T(8,128)(2,1)} %shard_map.49), channel_id=1, replica_groups=mesh['cand'=8,'doc'=64] {'cand'}, dimensions={0} | all-to-all | bytes 4194304 | tf_op jit(solution)/shard_map/all_to_all | solution.py:177
  97.9 5.6 %shard_map.50 = bf16[128,8192]{1,0:T(8,128)(2,1)} custom-call(bf16[8,128,1024]{2,1,0:T(8,128)(2,1)} %all_to_all.14.in_ref), custom_call_target="tpu_custom_call" | custom-call | tf_op jit(solution)/shard_map/pallas_call | solution.py:134
  (16 shorter events, 0.2 us)
Async XLA Ops:
  0.0 18.5 %copy-start = (bf16[128,8192]{1,0:T(8,128)(2,1)S(1)}, bf16[128,8192]{1,0:T(8,128)(2,1)}, u32[]{:S(2)}) copy-start(bf16[128,8192]{1,0:T(8,128)(2,1)} %param.4) | copy-start | bytes 6291460
  1.1 20.2 %collective-permute-start.1 = (bf16[2,128,128]{1,2,0:T(8,128)(2,1)S(1)}, bf16[2,128,128]{1,2,0:T(8,128)(2,1)S(1)}, u32[]{:S(2)}, u32[]{:S(2)}) collective-permute-start(bf16[2,128,128]{1,2,0:T(8,128)(2,1)S(1)} %copy.26), channel_id=1, source_target_pairs={{0,1},{1,2},{2,3},{3,4},{4,5},{5,6},{6,7},{7,8},{8,9},{9,10},{10,1... | collective-permute-start | bytes 196616 | tf_op jit(solution)/shard_map/ppermute | solution.py:22
  4.5 39.2 %collective-permute-start = (bf16[2,128,128]{1,2,0:T(8,128)(2,1)S(1)}, bf16[2,128,128]{1,2,0:T(8,128)(2,1)S(1)}, u32[]{:S(2)}, u32[]{:S(2)}) collective-permute-start(bf16[2,128,128]{1,2,0:T(8,128)(2,1)S(1)} %copy.26), channel_id=1, source_target_pairs={{0,8},{1,9},{2,10},{3,11},{4,12},{5,13},{6,14},{7,15},{8,16},{9,17... | collective-permute-start | bytes 196616 | tf_op jit(solution)/shard_map/ppermute | solution.py:22
  12.2 13.8 %all-to-all-start = ((f32[8,1,64]{2,1,0:T(1,128)}), f32[8,1,64]{2,1,0:T(1,128)S(1)}, u32[]{:S(2)}, u32[]{:S(2)}) async-start(f32[8,1,64]{2,1,0:T(1,128)} %broadcast_in_dim.64), calls=%async_computation | async-start | bytes 8192 | tf_op jit(solution)/shard_map/all_to_all | solution.py:156
  21.3 10.2 %collective-permute-start.2 = (bf16[2,256,128]{1,2,0:T(8,128)(2,1)S(1)}, bf16[2,256,128]{1,2,0:T(8,128)(2,1)S(1)}, u32[]{:S(2)}, u32[]{:S(2)}) collective-permute-start(bf16[2,256,128]{1,2,0:T(8,128)(2,1)S(1)} %pad_maximum_fusion.1), channel_id=1, source_target_pairs={{0,2},{1,3},{2,4},{3,5},{4,6},{5,7},{6,8},{7,9},{8,10},{9,11},{10,... | collective-permute-start | bytes 393224 | tf_op jit(solution)/shard_map/ppermute | solution.py:22
  31.5 12.2 %collective-permute-start.3 = (bf16[2,512,128]{1,2,0:T(8,128)(2,1)S(1)}, bf16[2,512,128]{1,2,0:T(8,128)(2,1)S(1)}, u32[]{:S(2)}, u32[]{:S(2)}) collective-permute-start(bf16[2,512,128]{1,2,0:T(8,128)(2,1)S(1)} %pad_maximum_fusion), channel_id=1, source_target_pairs={{0,4},{1,5},{2,6},{3,7},{4,8},{5,9},{6,10},{7,11},{8,12},{9,13},{1... | collective-permute-start | bytes 786440 | tf_op jit(solution)/shard_map/ppermute | solution.py:22

commit v11 on v10

--- a/solution.py
+++ b/solution.py
@@ -126,17 +126,20 @@
 
 
 def place_kernel(in_ref, out_ref):
-    out_ref[...] = in_ref[0]
+    count, _, width = in_ref.shape
+    for g in range(count):
+        out_ref[:, g * width : (g + 1) * width] = in_ref[g]
 
 
 def side_by_side(blocks):
     count, rows, width = blocks.shape
+    step = count // 2
     return pl.pallas_call(
         place_kernel,
         out_shape=jax.ShapeDtypeStruct((rows, count * width), blocks.dtype),
-        grid=(count,),
-        in_specs=[pl.BlockSpec((1, rows, width), lambda g: (g, 0, 0))],
-        out_specs=pl.BlockSpec((rows, width), lambda g: (0, g)),
+        grid=(count // step,),
+        in_specs=[pl.BlockSpec((step, rows, width), lambda g: (g, 0, 0))],
+        out_specs=pl.BlockSpec((rows, step * width), lambda g: (0, g)),
     )(blocks)
 
 

time: 104 us -> 101 us (0.971)
  Pallas kernels: 26 us -> 23 us
    pallas_call x1, Pallas kernels: 5.63 us -> 2.61 us  [side_by_side(): pl.pallas_call(place_kernel, out_shape=jax.ShapeDtypeStruct((rows, count...]
where the time goes in v11:
time: 101 us
  blocking collectives  32.1 us (32%)
  starting transfers between devices  23.9 us (24%)
  Pallas kernels  23 us (23%)
  other arithmetic  10.4 us (10%)
  local copies, waits for them, and re-layouts  5.53 us (5%)
  waiting for transfers between devices  5.47 us (5%)
    all_to_all x1, blocking collectives, on_device(): gathered = lax.all_to_all(mixed, 'cand', 0, 0, tiled=True)  32.1 us
    pallas_call x1, Pallas kernels, attend_all(): pl.pallas_call(attention_kernel, out_shape=jax.ShapeDtypeStruct((cands, q...  20.4 us
    ppermute x4, starting transfers between devices, passed_along(): lax.ppermute(value, axis, [(source, source + steps) for source in range(f...  19.5 us
    select_n x1, other arithmetic, cos_and_sin(): return jnp.where(quadrant + 1 & 2 != 0, -base, base)  7.16 us
    ppermute x4, waiting for transfers between devices, passed_along(): lax.ppermute(value, axis, [(source, source + steps) for source in range(f...  5.47 us
    all_to_all x1, starting transfers between devices, on_device(): lax.all_to_all(jnp.broadcast_to(factors, (cands, factors.shape[1])), 'can...  4.47 us
    pallas_call x1, Pallas kernels, side_by_side(): pl.pallas_call(place_kernel, out_shape=jax.ShapeDtypeStruct((rows, count...  2.61 us
  transfers between devices with their start and end apart: 5, of which 1 were waited for; matrix products, arithmetic and copies ran while one was open for 13% of the time, Pallas kernels for 0%

profile of v11, /device:TPU:96, one launch (start us, length us, event | category | flops | bytes accessed | tf_op | source)
XLA Modules:
  0.0 100.5 jit_solution(12307778332222818203)
XLA Ops:
  0.0 0.0 copy-start
  0.0 1.1 %copy.26 = bf16[2,128,128]{1,2,0:T(8,128)(2,1)S(1)} copy(bf16[2,128,128]{2,1,0:T(8,128)(2,1)} %param.5) | data formatting | bytes 131072 | tf_op args[1]
  1.1 3.4 %collective-permute-start.1 = (bf16[2,128,128]{1,2,0:T(8,128)(2,1)S(1)}, bf16[2,128,128]{1,2,0:T(8,128)(2,1)S(1)}, u32[]{:S(2)}, u32[]{:S(2)}) collective-permute-start(bf16[2,128,128]{1,2,0:T(8,128)(2,1)S(1)} %copy.26), channel_id=1, source_target_pairs={{0,1},{1,2},{2,3},{3,4},{4,5},{5,6},{6,7},{7,8},{8,9},{9,10},{10,1... | collective-permute-start | bytes 196616 | tf_op jit(solution)/shard_map/ppermute | solution.py:22
  4.5 6.4 %collective-permute-start = (bf16[2,128,128]{1,2,0:T(8,128)(2,1)S(1)}, bf16[2,128,128]{1,2,0:T(8,128)(2,1)S(1)}, u32[]{:S(2)}, u32[]{:S(2)}) collective-permute-start(bf16[2,128,128]{1,2,0:T(8,128)(2,1)S(1)} %copy.26), channel_id=1, source_target_pairs={{0,8},{1,9},{2,10},{3,11},{4,12},{5,13},{6,14},{7,15},{8,16},{9,17... | collective-permute-start | bytes 196616 | tf_op jit(solution)/shard_map/ppermute | solution.py:22
  10.9 1.3 %broadcast_in_dim.64 = f32[8,1,64]{2,1,0:T(1,128)} broadcast(f32[64]{0:T(128)} %bitcast.11), dimensions={2} | broadcast | bytes 2304 | tf_op jit(solution)/shard_map/broadcast_in_dim | solution.py:160
  12.2 4.5 %all-to-all-start = ((f32[8,1,64]{2,1,0:T(1,128)}), f32[8,1,64]{2,1,0:T(1,128)S(1)}, u32[]{:S(2)}, u32[]{:S(2)}) async-start(f32[8,1,64]{2,1,0:T(1,128)} %broadcast_in_dim.64), calls=%async_computation | async-start | bytes 8192 | tf_op jit(solution)/shard_map/all_to_all | solution.py:159
  16.7 0.7 copy.31
  17.4 0.1 reduce
  17.6 0.7 sub.25
  18.2 0.1 convert_reduce_fusion.1
  18.3 0.1 convert_reduce_fusion
  18.4 0.1 select_reduce_fusion
  18.5 0.0 copy-done
  18.5 0.7 constant_dynamic-slice_fusion.q_ref
  19.3 2.0 %and_select_fusion.bias_ref = f32[1152,128]{1,0:T(8,128)} fusion(s32[128]{0:T(128)S(1)} %iota_add_fusion.1, s32[128]{0:T(128)S(1)} %compare_select_fusion, s32[1152]{0:T(1024)S(1)} %iota_add_fusion, s32[1152]{0:T(1024)S(1)} %get-tuple-element.6, pred[1152]{0:T(1024)(128)(4,1)S(1)} %get-tuple-element.5), kind=kLoop, calls=%fused_computation.34 | loop fusion | flops 737280 | bytes 601216 | tf_op jit(solution)/shard_map/jit(_where)/select_n | solution.py:176
  21.3 0.0 collective-permute-done.1
  21.3 4.6 %collective-permute-start.2 = (bf16[2,256,128]{1,2,0:T(8,128)(2,1)S(1)}, bf16[2,256,128]{1,2,0:T(8,128)(2,1)S(1)}, u32[]{:S(2)}, u32[]{:S(2)}) collective-permute-start(bf16[2,256,128]{1,2,0:T(8,128)(2,1)S(1)} %pad_maximum_fusion.1), channel_id=1, source_target_pairs={{0,2},{1,3},{2,4},{3,5},{4,6},{5,7},{6,8},{7,9},{8,10},{9,11},{10,... | collective-permute-start | bytes 393224 | tf_op jit(solution)/shard_map/ppermute | solution.py:22
  26.0 0.0 all-to-all-done
  26.0 0.1 pad_maximum_fusion.2
  26.1 5.5 %collective-permute-done.2 = bf16[2,256,128]{1,2,0:T(8,128)(2,1)S(1)} collective-permute-done((bf16[2,256,128]{1,2,0:T(8,128)(2,1)S(1)}, bf16[2,256,128]{1,2,0:T(8,128)(2,1)S(1)}, u32[]{:S(2)}, u32[]{:S(2)}) %collective-permute-start.2) | collective-permute-done | bytes 131104 | tf_op jit(solution)/shard_map/ppermute | solution.py:22
  31.5 5.0 %collective-permute-start.3 = (bf16[2,512,128]{1,2,0:T(8,128)(2,1)S(1)}, bf16[2,512,128]{1,2,0:T(8,128)(2,1)S(1)}, u32[]{:S(2)}, u32[]{:S(2)}) collective-permute-start(bf16[2,512,128]{1,2,0:T(8,128)(2,1)S(1)} %pad_maximum_fusion), channel_id=1, source_target_pairs={{0,4},{1,5},{2,6},{3,7},{4,8},{5,9},{6,10},{7,11},{8,12},{9,13},{1... | collective-permute-start | bytes 786440 | tf_op jit(solution)/shard_map/ppermute | solution.py:22
  36.6 7.2 %negate_select_fusion.table_ref = f32[8,1152,128]{2,1,0:T(8,128)} fusion(s32[128]{0:T(128)S(1)} %compare_select_fusion.1, f32[8,128]{1,0:T(8,128)S(1)} %pad_maximum_fusion.2, f32[1152]{0:T(1024)S(1)} %select_convert_fusion), kind=kLoop, calls=%fused_computation | loop fusion | flops 43646976 | bytes 4727808 | tf_op jit(solution)/shard_map/jit(_where)/select_n | solution.py:51
  43.8 0.0 collective-permute-done
  43.8 0.0 collective-permute-done.3
  43.9 0.8 slice_bitcast_fusion
  44.6 0.9 copy.32.k_ref
  45.5 20.4 %shard_map.49 = bf16[8,128,1024]{2,1,0:T(8,128)(2,1)} custom-call(bf16[128,1024]{1,0:T(8,128)(2,1)} %constant_dynamic-slice_fusion.q_ref, bf16[1152,128]{1,0:T(8,128)(2,1)} %copy.32.k_ref, bf16[128,1152]{1,0:T(8,128)(2,1)} %get-tuple-element.7.vt_ref, f32[8,1152,128]{2,1,0:T(8,128)} %negate_select_fusion.table_ref, f32[1152,128]{1,0:T(8,128)} %and_select_fusion.bias_ref), custom_call_target="tpu_custom_call" | custom-call | flops 4831838208 | bytes 2949120 | tf_op jit(solution)/shard_map/pallas_call | solution.py:108
  65.9 32.1 %all_to_all.14.in_ref = bf16[8,128,1024]{2,1,0:T(8,128)(2,1)} all-to-all(bf16[8,128,1024]{2,1,0:T(8,128)(2,1)} %shard_map.49), channel_id=1, replica_groups=mesh['cand'=8,'doc'=64] {'cand'}, dimensions={0} | all-to-all | bytes 4194304 | tf_op jit(solution)/shard_map/all_to_all | solution.py:180
  97.9 2.6 %shard_map.50 = bf16[128,8192]{1,0:T(8,128)(2,1)} custom-call(bf16[8,128,1024]{2,1,0:T(8,128)(2,1)} %all_to_all.14.in_ref), custom_call_target="tpu_custom_call" | custom-call | tf_op jit(solution)/shard_map/pallas_call | solution.py:137
  (16 shorter events, 0.2 us)
Async XLA Ops:
  0.0 18.5 %copy-start = (bf16[128,8192]{1,0:T(8,128)(2,1)S(1)}, bf16[128,8192]{1,0:T(8,128)(2,1)}, u32[]{:S(2)}) copy-start(bf16[128,8192]{1,0:T(8,128)(2,1)} %param.4) | copy-start | bytes 6291460
  1.1 20.2 %collective-permute-start.1 = (bf16[2,128,128]{1,2,0:T(8,128)(2,1)S(1)}, bf16[2,128,128]{1,2,0:T(8,128)(2,1)S(1)}, u32[]{:S(2)}, u32[]{:S(2)}) collective-permute-start(bf16[2,128,128]{1,2,0:T(8,128)(2,1)S(1)} %copy.26), channel_id=1, source_target_pairs={{0,1},{1,2},{2,3},{3,4},{4,5},{5,6},{6,7},{7,8},{8,9},{9,10},{10,1... | collective-permute-start | bytes 196616 | tf_op jit(solution)/shard_map/ppermute | solution.py:22
  4.5 39.2 %collective-permute-start = (bf16[2,128,128]{1,2,0:T(8,128)(2,1)S(1)}, bf16[2,128,128]{1,2,0:T(8,128)(2,1)S(1)}, u32[]{:S(2)}, u32[]{:S(2)}) collective-permute-start(bf16[2,128,128]{1,2,0:T(8,128)(2,1)S(1)} %copy.26), channel_id=1, source_target_pairs={{0,8},{1,9},{2,10},{3,11},{4,12},{5,13},{6,14},{7,15},{8,16},{9,17... | collective-permute-start | bytes 196616 | tf_op jit(solution)/shard_map/ppermute | solution.py:22
  12.2 13.8 %all-to-all-start = ((f32[8,1,64]{2,1,0:T(1,128)}), f32[8,1,64]{2,1,0:T(1,128)S(1)}, u32[]{:S(2)}, u32[]{:S(2)}) async-start(f32[8,1,64]{2,1,0:T(1,128)} %broadcast_in_dim.64), calls=%async_computation | async-start | bytes 8192 | tf_op jit(solution)/shard_map/all_to_all | solution.py:159
  21.3 10.2 %collective-permute-start.2 = (bf16[2,256,128]{1,2,0:T(8,128)(2,1)S(1)}, bf16[2,256,128]{1,2,0:T(8,128)(2,1)S(1)}, u32[]{:S(2)}, u32[]{:S(2)}) collective-permute-start(bf16[2,256,128]{1,2,0:T(8,128)(2,1)S(1)} %pad_maximum_fusion.1), channel_id=1, source_target_pairs={{0,2},{1,3},{2,4},{3,5},{4,6},{5,7},{6,8},{7,9},{8,10},{9,11},{10,... | collective-permute-start | bytes 393224 | tf_op jit(solution)/shard_map/ppermute | solution.py:22
  31.5 12.2 %collective-permute-start.3 = (bf16[2,512,128]{1,2,0:T(8,128)(2,1)S(1)}, bf16[2,512,128]{1,2,0:T(8,128)(2,1)S(1)}, u32[]{:S(2)}, u32[]{:S(2)}) collective-permute-start(bf16[2,512,128]{1,2,0:T(8,128)(2,1)S(1)} %pad_maximum_fusion), channel_id=1, source_target_pairs={{0,4},{1,5},{2,6},{3,7},{4,8},{5,9},{6,10},{7,11},{8,12},{9,13},{1... | collective-permute-start | bytes 786440 | tf_op jit(solution)/shard_map/ppermute | solution.py:22

commit v12 on v11

--- a/solution.py
+++ b/solution.py
@@ -5,12 +5,13 @@
 from jax import lax
 from jax.experimental import pallas as pl
 from jax.experimental.pallas import tpu as pltpu
-from jax.sharding import PartitionSpec as P
+from jax.sharding import Mesh, PartitionSpec as P
 
 H = 64
 KVH = 8
 HD = 128
 SPAN = 8
+CAND = ("chip", "core")
 
 
 ROPE_BASE = 500000.0
@@ -152,12 +153,12 @@
     row_count = queries.shape[0]
     group_width = queries.shape[1] // KVH
     device = lax.axis_index("doc")
-    group = lax.axis_index("cand")
+    group = lax.axis_index(CAND)
     query_index = device * row_count + jnp.arange(row_count, dtype=jnp.int32)
     key_index = (device - SPAN) * row_count + jnp.arange((SPAN + 1) * row_count, dtype=jnp.int32)
-    cands = lax.axis_size("cand")
+    cands = lax.axis_size(CAND)
     every_factor = lax.all_to_all(
-        jnp.broadcast_to(factors, (cands, factors.shape[1])), "cand", 0, 0, tiled=True
+        jnp.broadcast_to(factors, (cands, factors.shape[1])), CAND, 0, 0, tiled=True
     )
     far = passed_along(keys_values, "doc", SPAN)
     window = keys_values
@@ -176,13 +177,20 @@
     bias = jnp.where(allowed, 0.0, -1e30).astype(jnp.float32)
     offsets = jnp.broadcast_to(key_offset.astype(jnp.float32)[:, None], (key_offset.shape[0], HD))
     own_queries = lax.dynamic_slice_in_dim(queries, group * group_width, group_width, 1)
-    mixed = attend_all(own_queries, window, offsets, inverse_rows(every_factor), bias)
-    gathered = lax.all_to_all(mixed, "cand", 0, 0, tiled=True)
-    return side_by_side(gathered)[None]
+    cores = lax.axis_size("core")
+    chips = cands // cores
+    order = [chip * cores + core for core in range(cores) for chip in range(chips)]
+    mixed = attend_all(own_queries, window, offsets, inverse_rows(every_factor[jnp.array(order)]), bias)
+    mixed = mixed.reshape(cores, chips, row_count, group_width)
+    paired = lax.all_to_all(mixed, "core", 0, 0, tiled=True)
+    gathered = lax.all_to_all(paired, "chip", 1, 0, tiled=True)
+    return side_by_side(gathered.reshape(cands, row_count, group_width))[None]
 
 
 def solution(mesh):
-    placed = (P("doc", None), P(None, "doc", "cand"), P("cand", None), P())
+    cand = mesh.shape["cand"]
+    split = Mesh(mesh.devices.reshape(cand // 2, 2, mesh.shape["doc"]), ("chip", "core", "doc"))
+    placed = (P("doc", None), P(None, "doc", CAND), P(CAND, None), P())
     return jax.shard_map(
-        on_device, mesh=mesh, in_specs=placed, out_specs=P("cand", "doc", None), check_vma=False
+        on_device, mesh=split, in_specs=placed, out_specs=P(CAND, "doc", None), check_vma=False
     )

time: 101 us -> 108 us (1.069)
  the two profiles are of different devices: /device:TPU:96 before, /device:TPU:98 now
where the time goes in v12:
time: 108 us; the launch traced here: 107 us
  blocking collectives  37.6 us (35%)
  starting transfers between devices  23.7 us (22%)
  Pallas kernels  23 us (21%)
  other arithmetic  11.1 us (10%)
  local copies, waits for them, and re-layouts  6.25 us (6%)
  waiting for transfers between devices  5.74 us (5%)
    all_to_all x1, blocking collectives, on_device(): gathered = lax.all_to_all(paired, 'chip', 1, 0, tiled=True)  31 us
    pallas_call x1, Pallas kernels, attend_all(): pl.pallas_call(attention_kernel, out_shape=jax.ShapeDtypeStruct((cands, q...  20.4 us
    ppermute x4, starting transfers between devices, passed_along(): lax.ppermute(value, axis, [(source, source + steps) for source in range(f...  19.2 us
    select_n x1, other arithmetic, cos_and_sin(): return jnp.where(quadrant + 1 & 2 != 0, -base, base)  7.16 us
    all_to_all x1, blocking collectives, on_device(): paired = lax.all_to_all(mixed, 'core', 0, 0, tiled=True)  6.61 us
    ppermute x4, waiting for transfers between devices, passed_along(): lax.ppermute(value, axis, [(source, source + steps) for source in range(f...  5.74 us
    all_to_all x1, starting transfers between devices, on_device(): lax.all_to_all(jnp.broadcast_to(factors, (cands, factors.shape[1])), CAND...  4.47 us
    pallas_call x1, Pallas kernels, side_by_side(): pl.pallas_call(place_kernel, out_shape=jax.ShapeDtypeStruct((rows, count...  2.61 us
  transfers between devices with their start and end apart: 5, of which 1 were waited for; matrix products, arithmetic and copies ran while one was open for 13% of the time, Pallas kernels for 0%

profile of v12, /device:TPU:98, one launch (start us, length us, event | category | flops | bytes accessed | tf_op | source)
XLA Modules:
  0.0 107.5 jit_solution(17137475734912887555)
XLA Ops:
  0.0 0.0 copy-start
  0.0 1.1 %copy.38 = bf16[2,128,128]{1,2,0:T(8,128)(2,1)S(1)} copy(bf16[2,128,128]{2,1,0:T(8,128)(2,1)} %param.6) | data formatting | bytes 131072 | tf_op args[1]
  1.1 3.4 %collective-permute-start.1 = (bf16[2,128,128]{1,2,0:T(8,128)(2,1)S(1)}, bf16[2,128,128]{1,2,0:T(8,128)(2,1)S(1)}, u32[]{:S(2)}, u32[]{:S(2)}) collective-permute-start(bf16[2,128,128]{1,2,0:T(8,128)(2,1)S(1)} %copy.38), channel_id=1, source_target_pairs={{0,1},{1,2},{2,3},{3,4},{4,5},{5,6},{6,7},{7,8},{8,9},{9,10},{10,1... | collective-permute-start | bytes 196616 | tf_op jit(solution)/shard_map/ppermute | solution.py:23
  4.5 6.4 %collective-permute-start = (bf16[2,128,128]{1,2,0:T(8,128)(2,1)S(1)}, bf16[2,128,128]{1,2,0:T(8,128)(2,1)S(1)}, u32[]{:S(2)}, u32[]{:S(2)}) collective-permute-start(bf16[2,128,128]{1,2,0:T(8,128)(2,1)S(1)} %copy.38), channel_id=1, source_target_pairs={{0,8},{1,9},{2,10},{3,11},{4,12},{5,13},{6,14},{7,15},{8,16},{9,17... | collective-permute-start | bytes 196616 | tf_op jit(solution)/shard_map/ppermute | solution.py:23
  10.9 1.3 %broadcast_in_dim.67 = f32[8,1,64]{2,1,0:T(1,128)} broadcast(f32[64]{0:T(128)} %bitcast.19), dimensions={2} | broadcast | bytes 2304 | tf_op jit(solution)/shard_map/broadcast_in_dim | solution.py:161
  12.2 4.5 %all-to-all-start = ((f32[8,1,64]{2,1,0:T(1,128)}), f32[8,1,64]{2,1,0:T(1,128)S(1)}, u32[]{:S(2)}, u32[]{:S(2)}) async-start(f32[8,1,64]{2,1,0:T(1,128)} %broadcast_in_dim.67), calls=%async_computation | async-start | bytes 8192 | tf_op jit(solution)/shard_map/all_to_all | solution.py:160
  16.7 0.7 pad_clamp_fusion
  17.3 0.7 copy.43
  18.1 0.1 reduce
  18.2 0.7 sub.25
  18.9 0.1 convert_reduce_fusion.1
  19.0 0.1 convert_reduce_fusion
  19.1 0.1 select_reduce_fusion
  19.2 0.0 copy-done
  19.2 0.7 constant_dynamic-slice_fusion.q_ref
  19.9 2.0 %and_select_fusion.bias_ref = f32[1152,128]{1,0:T(8,128)} fusion(s32[128]{0:T(128)S(1)} %iota_add_fusion.1, s32[128]{0:T(128)S(1)} %compare_select_fusion, s32[1152]{0:T(1024)S(1)} %iota_add_fusion, s32[1152]{0:T(1024)S(1)} %get-tuple-element.6, pred[1152]{0:T(1024)(128)(4,1)S(1)} %get-tuple-element.5), kind=kLoop, calls=%fused_computation.35 | loop fusion | flops 737280 | bytes 601216 | tf_op jit(solution)/shard_map/jit(_where)/select_n | solution.py:177
  21.9 0.0 all-to-all-done
  21.9 0.6 gather_fusion
  22.5 0.0 collective-permute-done.1
  22.5 4.4 %collective-permute-start.2 = (bf16[2,256,128]{1,2,0:T(8,128)(2,1)S(1)}, bf16[2,256,128]{1,2,0:T(8,128)(2,1)S(1)}, u32[]{:S(2)}, u32[]{:S(2)}) collective-permute-start(bf16[2,256,128]{1,2,0:T(8,128)(2,1)S(1)} %pad_maximum_fusion.1), channel_id=1, source_target_pairs={{0,2},{1,3},{2,4},{3,5},{4,6},{5,7},{6,8},{7,9},{8,10},{9,11},{10,... | collective-permute-start | bytes 393224 | tf_op jit(solution)/shard_map/ppermute | solution.py:23
  26.9 0.1 pad_maximum_fusion.2
  27.0 5.7 %collective-permute-done.2 = bf16[2,256,128]{1,2,0:T(8,128)(2,1)S(1)} collective-permute-done((bf16[2,256,128]{1,2,0:T(8,128)(2,1)S(1)}, bf16[2,256,128]{1,2,0:T(8,128)(2,1)S(1)}, u32[]{:S(2)}, u32[]{:S(2)}) %collective-permute-start.2) | collective-permute-done | bytes 131104 | tf_op jit(solution)/shard_map/ppermute | solution.py:23
  32.8 5.0 %collective-permute-start.3 = (bf16[2,512,128]{1,2,0:T(8,128)(2,1)S(1)}, bf16[2,512,128]{1,2,0:T(8,128)(2,1)S(1)}, u32[]{:S(2)}, u32[]{:S(2)}) collective-permute-start(bf16[2,512,128]{1,2,0:T(8,128)(2,1)S(1)} %pad_maximum_fusion), channel_id=1, source_target_pairs={{0,4},{1,5},{2,6},{3,7},{4,8},{5,9},{6,10},{7,11},{8,12},{9,13},{1... | collective-permute-start | bytes 786440 | tf_op jit(solution)/shard_map/ppermute | solution.py:23
  37.8 7.2 %negate_select_fusion.table_ref = f32[8,1152,128]{2,1,0:T(8,128)} fusion(s32[128]{0:T(128)S(1)} %compare_select_fusion.1, f32[8,128]{1,0:T(8,128)S(1)} %pad_maximum_fusion.2, f32[1152]{0:T(1024)S(1)} %select_convert_fusion), kind=kLoop, calls=%fused_computation.1 | loop fusion | flops 43646976 | bytes 4727808 | tf_op jit(solution)/shard_map/jit(_where)/select_n | solution.py:52
  45.0 0.0 collective-permute-done
  45.0 0.0 collective-permute-done.3
  45.1 0.8 slice_bitcast_fusion
  45.9 0.9 copy.44.k_ref
  46.7 20.4 %shard_map.58 = bf16[8,128,1024]{2,1,0:T(8,128)(2,1)} custom-call(bf16[128,1024]{1,0:T(8,128)(2,1)} %constant_dynamic-slice_fusion.q_ref, bf16[1152,128]{1,0:T(8,128)(2,1)} %copy.44.k_ref, bf16[128,1152]{1,0:T(8,128)(2,1)} %get-tuple-element.7.vt_ref, f32[8,1152,128]{2,1,0:T(8,128)} %negate_select_fusion.table_ref, f32[1152,128]{1,0:T(8,128)} %and_select_fusion.bias_ref), custom_call_target="tpu_custom_call" | custom-call | flops 4831838208 | bytes 2949120 | tf_op jit(solution)/shard_map/pallas_call | solution.py:109
  67.1 6.6 %all_to_all.29 = bf16[2,4,128,1024]{3,2,1,0:T(8,128)(2,1)S(1)} all-to-all(bf16[2,4,128,1024]{3,2,1,0:T(8,128)(2,1)} %bitcast.17), channel_id=1, replica_groups=mesh['chip'=4,'core'=2,'doc'=64] {'core'}, dimensions={0} | all-to-all | bytes 4194304 | tf_op jit(solution)/shard_map/all_to_all | solution.py:185
  73.7 0.2 copy.45
  73.9 31.0 %all_to_all.30 = bf16[2,4,128,1024]{3,2,0,1:T(8,128)(2,1)} all-to-all(bf16[2,4,128,1024]{3,2,0,1:T(8,128)(2,1)S(1)} %copy.45), channel_id=1, replica_groups=mesh['chip'=4,'core'=2,'doc'=64] {'chip'}, dimensions={1} | all-to-all | bytes 4194304 | tf_op jit(solution)/shard_map/all_to_all | solution.py:186
  104.9 2.6 %shard_map.59 = bf16[128,8192]{1,0:T(8,128)(2,1)} custom-call(bf16[8,128,1024]{2,1,0:T(8,128)(2,1)} %bitcast.16), custom_call_target="tpu_custom_call" | custom-call | tf_op jit(solution)/shard_map/pallas_call | solution.py:138
  (16 shorter events, 0.2 us)
Async XLA Ops:
  0.0 19.2 %copy-start = (bf16[128,8192]{1,0:T(8,128)(2,1)S(1)}, bf16[128,8192]{1,0:T(8,128)(2,1)}, u32[]{:S(2)}) copy-start(bf16[128,8192]{1,0:T(8,128)(2,1)} %param.5) | copy-start | bytes 6291460
  1.1 21.4 %collective-permute-start.1 = (bf16[2,128,128]{1,2,0:T(8,128)(2,1)S(1)}, bf16[2,128,128]{1,2,0:T(8,128)(2,1)S(1)}, u32[]{:S(2)}, u32[]{:S(2)}) collective-permute-start(bf16[2,128,128]{1,2,0:T(8,128)(2,1)S(1)} %copy.38), channel_id=1, source_target_pairs={{0,1},{1,2},{2,3},{3,4},{4,5},{5,6},{6,7},{7,8},{8,9},{9,10},{10,1... | collective-permute-start | bytes 196616 | tf_op jit(solution)/shard_map/ppermute | solution.py:23
  4.5 40.5 %collective-permute-start = (bf16[2,128,128]{1,2,0:T(8,128)(2,1)S(1)}, bf16[2,128,128]{1,2,0:T(8,128)(2,1)S(1)}, u32[]{:S(2)}, u32[]{:S(2)}) collective-permute-start(bf16[2,128,128]{1,2,0:T(8,128)(2,1)S(1)} %copy.38), channel_id=1, source_target_pairs={{0,8},{1,9},{2,10},{3,11},{4,12},{5,13},{6,14},{7,15},{8,16},{9,17... | collective-permute-start | bytes 196616 | tf_op jit(solution)/shard_map/ppermute | solution.py:23
  12.2 9.8 %all-to-all-start = ((f32[8,1,64]{2,1,0:T(1,128)}), f32[8,1,64]{2,1,0:T(1,128)S(1)}, u32[]{:S(2)}, u32[]{:S(2)}) async-start(f32[8,1,64]{2,1,0:T(1,128)} %broadcast_in_dim.67), calls=%async_computation | async-start | bytes 8192 | tf_op jit(solution)/shard_map/all_to_all | solution.py:160
  22.5 10.2 %collective-permute-start.2 = (bf16[2,256,128]{1,2,0:T(8,128)(2,1)S(1)}, bf16[2,256,128]{1,2,0:T(8,128)(2,1)S(1)}, u32[]{:S(2)}, u32[]{:S(2)}) collective-permute-start(bf16[2,256,128]{1,2,0:T(8,128)(2,1)S(1)} %pad_maximum_fusion.1), channel_id=1, source_target_pairs={{0,2},{1,3},{2,4},{3,5},{4,6},{5,7},{6,8},{7,9},{8,10},{9,11},{10,... | collective-permute-start | bytes 393224 | tf_op jit(solution)/shard_map/ppermute | solution.py:23
  32.8 12.2 %collective-permute-start.3 = (bf16[2,512,128]{1,2,0:T(8,128)(2,1)S(1)}, bf16[2,512,128]{1,2,0:T(8,128)(2,1)S(1)}, u32[]{:S(2)}, u32[]{:S(2)}) collective-permute-start(bf16[2,512,128]{1,2,0:T(8,128)(2,1)S(1)} %pad_maximum_fusion), channel_id=1, source_target_pairs={{0,4},{1,5},{2,6},{3,7},{4,8},{5,9},{6,10},{7,11},{8,12},{9,13},{1... | collective-permute-start | bytes 786440 | tf_op jit(solution)/shard_map/ppermute | solution.py:23

commit v13 on v11

--- a/solution.py
+++ b/solution.py
@@ -51,7 +51,7 @@
     return jnp.where(((quadrant + 1) & 2) != 0, -base, base)
 
 
-def attention_kernel(q_ref, k_ref, vt_ref, table_ref, bias_ref, out_ref):
+def attention_kernel(q_ref, kv_ref, table_ref, bias_ref, out_ref):
     half_dim = HD // 2
     group_size = H // KVH
     query_rows = q_ref.shape[0]
@@ -60,7 +60,7 @@
     swapped = pltpu.roll(table, half_dim, 1)
     cosine = jnp.where(low, table, swapped)
     sine = jnp.where(low, -swapped, table)
-    keys = k_ref[...].astype(jnp.float32)
+    keys = kv_ref[0].astype(jnp.float32)
     key_rot = (keys * cosine + pltpu.roll(keys, half_dim, 1) * sine).astype(jnp.bfloat16)
     first_query = table.shape[0] - query_rows
     q_cos = cosine[first_query:]
@@ -88,7 +88,10 @@
         expw = jnp.exp(part - largest)
         totals.append(jnp.sum(expw, axis=0, keepdims=True))
         weights.append(expw.astype(jnp.bfloat16))
-    numer = jnp.dot(vt_ref[...], jnp.concatenate(weights, axis=1), preferred_element_type=jnp.float32)
+    numer = lax.dot_general(
+        kv_ref[1], jnp.concatenate(weights, axis=1), (((0,), (0,)), ((), ())),
+        preferred_element_type=jnp.float32,
+    )
     for head in range(group_size):
         cols = numer[:, head * query_rows : (head + 1) * query_rows] / totals[head]
         out_ref[0, :, head * HD : (head + 1) * HD] = cols.T.astype(jnp.bfloat16)
@@ -98,8 +101,6 @@
     angle = offsets[None] * inverse
     low = lax.broadcasted_iota(jnp.int32, angle.shape, 2) < HD // 2
     table = cos_and_sin(angle, low)
-    keys = window[0]
-    values_t = window[1].T
     cands = inverse.shape[0]
     key_rows = window.shape[1]
     query_rows, width = own_queries.shape
@@ -111,8 +112,7 @@
         grid=(cands,),
         in_specs=[
             pl.BlockSpec((query_rows, width), lambda c: (0, 0)),
-            pl.BlockSpec(keys.shape, lambda c: (0, 0)),
-            pl.BlockSpec(values_t.shape, lambda c: (0, 0)),
+            pl.BlockSpec(window.shape, lambda c: (0, 0, 0)),
             pl.BlockSpec((1, key_rows, HD), lambda c: (c, 0, 0)),
             pl.BlockSpec(bias.T.shape, lambda c: (0, 0)),
         ],
@@ -122,7 +122,7 @@
             transcendentals=cands * heads * query_rows * key_rows,
             bytes_accessed=window.size * 2 + own_queries.size * 2 + cands * query_rows * width * 2,
         ),
-    )(own_queries, keys, values_t, table, bias.T)
+    )(own_queries, window, table, bias.T)
 
 
 def place_kernel(in_ref, out_ref):

time: 101 us -> 101 us (level)
  local copies, waits for them, and re-layouts: 5.53 us -> 3.64 us
  other arithmetic: 10.4 us -> 12.1 us
    concatenate x2, other arithmetic: 0.04 us -> 1.71 us  [on_device(): jnp.concatenate([passed_along(window, 'doc', reach), window], axis=1)]
  transfers between devices with their start and end apart: 5 -> 5, of which waited for: 1 -> 1; matrix products, arithmetic and copies ran while one was open for 13% -> 15% of each run, Pallas kernels for 0% -> 0%
where the time goes in v13:
time: 101 us; the launch traced here: 100 us
  blocking collectives  32.1 us (32%)
  starting transfers between devices  24.1 us (24%)
  Pallas kernels  23 us (23%)
  other arithmetic  12.1 us (12%)
  waiting for transfers between devices  5.47 us (5%)
  local copies, waits for them, and re-layouts  3.64 us (4%)
    all_to_all x1, blocking collectives, on_device(): gathered = lax.all_to_all(mixed, 'cand', 0, 0, tiled=True)  32.1 us
    pallas_call x1, Pallas kernels, attend_all(): pl.pallas_call(attention_kernel, out_shape=jax.ShapeDtypeStruct((cands, q...  20.4 us
    ppermute x4, starting transfers between devices, passed_along(): lax.ppermute(value, axis, [(source, source + steps) for source in range(f...  19.6 us
    select_n x1, other arithmetic, cos_and_sin(): return jnp.where(quadrant + 1 & 2 != 0, -base, base)  7.16 us
    ppermute x4, waiting for transfers between devices, passed_along(): lax.ppermute(value, axis, [(source, source + steps) for source in range(f...  5.47 us
    all_to_all x1, starting transfers between devices, on_device(): lax.all_to_all(jnp.broadcast_to(factors, (cands, factors.shape[1])), 'can...  4.47 us
    pallas_call x1, Pallas kernels, side_by_side(): pl.pallas_call(place_kernel, out_shape=jax.ShapeDtypeStruct((rows, count...  2.61 us
  transfers between devices with their start and end apart: 5, of which 1 were waited for; matrix products, arithmetic and copies ran while one was open for 15% of the time, Pallas kernels for 0%

profile of v13, /device:TPU:96, one launch (start us, length us, event | category | flops | bytes accessed | tf_op | source)
XLA Modules:
  0.0 100.5 jit_solution(2842751749039154180)
XLA Ops:
  0.0 0.0 copy-start
  0.0 0.0 copy-start.1
  0.0 3.5 %collective-permute-start.1 = (bf16[2,128,128]{2,1,0:T(8,128)(2,1)}, bf16[2,128,128]{2,1,0:T(8,128)(2,1)S(1)}, u32[]{:S(2)}, u32[]{:S(2)}) collective-permute-start(bf16[2,128,128]{2,1,0:T(8,128)(2,1)} %param.5), channel_id=1, source_target_pairs={{0,1},{1,2},{2,3},{3,4},{4,5},{5,6},{6,7},{7,8},{8,9},{9,10},{10,1... | collective-permute-start | bytes 196616 | tf_op jit(solution)/shard_map/ppermute | solution.py:22
  3.5 6.4 %collective-permute-start = (bf16[2,128,128]{2,1,0:T(8,128)(2,1)}, bf16[2,128,128]{2,1,0:T(8,128)(2,1)S(1)}, u32[]{:S(2)}, u32[]{:S(2)}) collective-permute-start(bf16[2,128,128]{2,1,0:T(8,128)(2,1)} %param.5), channel_id=1, source_target_pairs={{0,8},{1,9},{2,10},{3,11},{4,12},{5,13},{6,14},{7,15},{8,16},{9,17... | collective-permute-start | bytes 196616 | tf_op jit(solution)/shard_map/ppermute | solution.py:22
  9.9 1.3 %broadcast_in_dim.64 = f32[8,1,64]{2,1,0:T(1,128)} broadcast(f32[64]{0:T(128)} %bitcast.5), dimensions={2} | broadcast | bytes 2304 | tf_op jit(solution)/shard_map/broadcast_in_dim | solution.py:160
  11.2 4.5 %all-to-all-start = ((f32[8,1,64]{2,1,0:T(1,128)}), f32[8,1,64]{2,1,0:T(1,128)S(1)}, u32[]{:S(2)}, u32[]{:S(2)}) async-start(f32[8,1,64]{2,1,0:T(1,128)} %broadcast_in_dim.64), calls=%async_computation | async-start | bytes 8192 | tf_op jit(solution)/shard_map/all_to_all | solution.py:159
  15.7 0.7 copy.8
  16.5 0.1 reduce
  16.6 0.7 sub.25
  17.2 0.1 convert_reduce_fusion.1
  17.3 0.1 convert_reduce_fusion
  17.4 0.1 select_reduce_fusion
  17.6 0.0 copy-done
  17.6 0.7 constant_dynamic-slice_fusion.q_ref
  18.3 2.0 %and_select_fusion.bias_ref = f32[1152,128]{1,0:T(8,128)} fusion(s32[128]{0:T(128)S(1)} %iota_add_fusion.1, s32[128]{0:T(128)S(1)} %compare_select_fusion, s32[1152]{0:T(1024)S(1)} %iota_add_fusion, s32[1152]{0:T(1024)S(1)} %get-tuple-element.6, pred[1152]{0:T(1024)(128)(4,1)S(1)} %get-tuple-element.5), kind=kLoop, calls=%fused_computation.34 | loop fusion | flops 737280 | bytes 601216 | tf_op jit(solution)/shard_map/jit(_where)/select_n | solution.py:176
  20.3 0.0 collective-permute-done.1
  20.3 0.8 pad_maximum_fusion.1
  21.2 4.6 %collective-permute-start.2 = (bf16[2,256,128]{2,1,0:T(8,128)(2,1)S(1)}, bf16[2,256,128]{2,1,0:T(8,128)(2,1)S(1)}, u32[]{:S(2)}, u32[]{:S(2)}) collective-permute-start(bf16[2,256,128]{2,1,0:T(8,128)(2,1)S(1)} %pad_maximum_fusion.1), channel_id=1, source_target_pairs={{0,2},{1,3},{2,4},{3,5},{4,6},{5,7},{6,8},{7,9},{8,10},{9,11},{10,... | collective-permute-start | bytes 393224 | tf_op jit(solution)/shard_map/ppermute | solution.py:22
  25.8 0.0 all-to-all-done
  25.8 0.1 pad_maximum_fusion.2
  25.9 5.5 %collective-permute-done.2 = bf16[2,256,128]{2,1,0:T(8,128)(2,1)S(1)} collective-permute-done((bf16[2,256,128]{2,1,0:T(8,128)(2,1)S(1)}, bf16[2,256,128]{2,1,0:T(8,128)(2,1)S(1)}, u32[]{:S(2)}, u32[]{:S(2)}) %collective-permute-start.2) | collective-permute-done | bytes 131104 | tf_op jit(solution)/shard_map/ppermute | solution.py:22
  31.4 0.9 pad_maximum_fusion
  32.2 5.0 %collective-permute-start.3 = (bf16[2,512,128]{2,1,0:T(8,128)(2,1)S(1)}, bf16[2,512,128]{2,1,0:T(8,128)(2,1)S(1)}, u32[]{:S(2)}, u32[]{:S(2)}) collective-permute-start(bf16[2,512,128]{2,1,0:T(8,128)(2,1)S(1)} %pad_maximum_fusion), channel_id=1, source_target_pairs={{0,4},{1,5},{2,6},{3,7},{4,8},{5,9},{6,10},{7,11},{8,12},{9,13},{1... | collective-permute-start | bytes 786440 | tf_op jit(solution)/shard_map/ppermute | solution.py:22
  37.3 7.2 %negate_select_fusion.table_ref = f32[8,1152,128]{2,1,0:T(8,128)} fusion(s32[128]{0:T(128)S(1)} %compare_select_fusion.1, f32[8,128]{1,0:T(8,128)S(1)} %pad_maximum_fusion.2, f32[1152]{0:T(1024)S(1)} %select_convert_fusion), kind=kLoop, calls=%fused_computation | loop fusion | flops 43646976 | bytes 4727808 | tf_op jit(solution)/shard_map/jit(_where)/select_n | solution.py:51
  44.4 0.0 collective-permute-done
  44.4 0.0 collective-permute-done.3
  44.5 0.0 copy-done.1
  44.6 0.0 copy-start.2
  44.6 0.8 copy-done.2
  45.4 20.4 %shard_map.49 = bf16[8,128,1024]{2,1,0:T(8,128)(2,1)} custom-call(bf16[128,1024]{1,0:T(8,128)(2,1)} %constant_dynamic-slice_fusion.q_ref, bf16[2,1152,128]{2,1,0:T(8,128)(2,1)} %copy-done.2, f32[8,1152,128]{2,1,0:T(8,128)} %negate_select_fusion.table_ref, f32[1152,128]{1,0:T(8,128)} %and_select_fusion.bias_ref), custom_call_target="tpu_custom_call" | custom-call | flops 4831838208 | bytes 2949120 | tf_op jit(solution)/shard_map/pallas_call | solution.py:109
  65.8 32.1 %all_to_all.14.in_ref = bf16[8,128,1024]{2,1,0:T(8,128)(2,1)} all-to-all(bf16[8,128,1024]{2,1,0:T(8,128)(2,1)} %shard_map.49), channel_id=1, replica_groups=mesh['cand'=8,'doc'=64] {'cand'}, dimensions={0} | all-to-all | bytes 4194304 | tf_op jit(solution)/shard_map/all_to_all | solution.py:180
  97.8 2.6 %shard_map.50 = bf16[128,8192]{1,0:T(8,128)(2,1)} custom-call(bf16[8,128,1024]{2,1,0:T(8,128)(2,1)} %all_to_all.14.in_ref), custom_call_target="tpu_custom_call" | custom-call | tf_op jit(solution)/shard_map/pallas_call | solution.py:137
  (14 shorter events, 0.2 us)
Async XLA Ops:
  0.0 17.6 %copy-start = (bf16[128,8192]{1,0:T(8,128)(2,1)S(1)}, bf16[128,8192]{1,0:T(8,128)(2,1)}, u32[]{:S(2)}) copy-start(bf16[128,8192]{1,0:T(8,128)(2,1)} %param.4) | copy-start | bytes 6291460
  0.0 44.5 %copy-start.1 = (bf16[2,128,128]{2,1,0:T(8,128)(2,1)S(1)}, bf16[2,128,128]{2,1,0:T(8,128)(2,1)}, u32[]{:S(2)}) copy-start(bf16[2,128,128]{2,1,0:T(8,128)(2,1)} %param.5) | copy-start | bytes 196612
  0.0 20.3 %collective-permute-start.1 = (bf16[2,128,128]{2,1,0:T(8,128)(2,1)}, bf16[2,128,128]{2,1,0:T(8,128)(2,1)S(1)}, u32[]{:S(2)}, u32[]{:S(2)}) collective-permute-start(bf16[2,128,128]{2,1,0:T(8,128)(2,1)} %param.5), channel_id=1, source_target_pairs={{0,1},{1,2},{2,3},{3,4},{4,5},{5,6},{6,7},{7,8},{8,9},{9,10},{10,1... | collective-permute-start | bytes 196616 | tf_op jit(solution)/shard_map/ppermute | solution.py:22
  3.5 40.9 %collective-permute-start = (bf16[2,128,128]{2,1,0:T(8,128)(2,1)}, bf16[2,128,128]{2,1,0:T(8,128)(2,1)S(1)}, u32[]{:S(2)}, u32[]{:S(2)}) collective-permute-start(bf16[2,128,128]{2,1,0:T(8,128)(2,1)} %param.5), channel_id=1, source_target_pairs={{0,8},{1,9},{2,10},{3,11},{4,12},{5,13},{6,14},{7,15},{8,16},{9,17... | collective-permute-start | bytes 196616 | tf_op jit(solution)/shard_map/ppermute | solution.py:22
  11.2 14.6 %all-to-all-start = ((f32[8,1,64]{2,1,0:T(1,128)}), f32[8,1,64]{2,1,0:T(1,128)S(1)}, u32[]{:S(2)}, u32[]{:S(2)}) async-start(f32[8,1,64]{2,1,0:T(1,128)} %broadcast_in_dim.64), calls=%async_computation | async-start | bytes 8192 | tf_op jit(solution)/shard_map/all_to_all | solution.py:159
  21.2 10.2 %collective-permute-start.2 = (bf16[2,256,128]{2,1,0:T(8,128)(2,1)S(1)}, bf16[2,256,128]{2,1,0:T(8,128)(2,1)S(1)}, u32[]{:S(2)}, u32[]{:S(2)}) collective-permute-start(bf16[2,256,128]{2,1,0:T(8,128)(2,1)S(1)} %pad_maximum_fusion.1), channel_id=1, source_target_pairs={{0,2},{1,3},{2,4},{3,5},{4,6},{5,7},{6,8},{7,9},{8,10},{9,11},{10,... | collective-permute-start | bytes 393224 | tf_op jit(solution)/shard_map/ppermute | solution.py:22
  32.2 12.2 %collective-permute-start.3 = (bf16[2,512,128]{2,1,0:T(8,128)(2,1)S(1)}, bf16[2,512,128]{2,1,0:T(8,128)(2,1)S(1)}, u32[]{:S(2)}, u32[]{:S(2)}) collective-permute-start(bf16[2,512,128]{2,1,0:T(8,128)(2,1)S(1)} %pad_maximum_fusion), channel_id=1, source_target_pairs={{0,4},{1,5},{2,6},{3,7},{4,8},{5,9},{6,10},{7,11},{8,12},{9,13},{1... | collective-permute-start | bytes 786440 | tf_op jit(solution)/shard_map/ppermute | solution.py:22
  44.6 0.8 copy-start.2

commit v14 on v13

--- a/solution.py
+++ b/solution.py
@@ -155,17 +155,21 @@
     group = lax.axis_index("cand")
     query_index = device * row_count + jnp.arange(row_count, dtype=jnp.int32)
     key_index = (device - SPAN) * row_count + jnp.arange((SPAN + 1) * row_count, dtype=jnp.int32)
-    cands = lax.axis_size("cand")
-    every_factor = lax.all_to_all(
-        jnp.broadcast_to(factors, (cands, factors.shape[1])), "cand", 0, 0, tiled=True
-    )
     far = passed_along(keys_values, "doc", SPAN)
     window = keys_values
     reach = 1
     while reach < SPAN:
         window = jnp.concatenate([passed_along(window, "doc", reach), window], axis=1)
+        if reach == 1:
+            window, factors, lengths, queries = lax.optimization_barrier(
+                (window, factors, lengths, queries)
+            )
         reach *= 2
     window = jnp.concatenate([far, window], axis=1)
+    cands = lax.axis_size("cand")
+    every_factor = lax.all_to_all(
+        jnp.broadcast_to(factors, (cands, factors.shape[1])), "cand", 0, 0, tiled=True
+    )
     query_doc, _ = locate(query_index, lengths)
     key_doc, key_offset = locate(key_index, lengths)
     allowed = (

time: 101 us -> 98.2 us (0.972)
  waiting for transfers between devices: 5.47 us -> 2.72 us
    ppermute x4, waiting for transfers between devices: 5.47 us -> 2.72 us  [passed_along(): lax.ppermute(value, axis, [(source, source + steps) for source in range(f...]
  transfers between devices with their start and end apart: 5 -> 5, of which waited for: 1 -> 1; matrix products, arithmetic and copies ran while one was open for 15% -> 14% of each run, Pallas kernels for 0% -> 0%
where the time goes in v14:
time: 98.2 us; the launch traced here: 97.8 us
  blocking collectives  32.1 us (33%)
  starting transfers between devices  25.1 us (26%)
  Pallas kernels  23 us (23%)
  other arithmetic  12.2 us (12%)
  waiting for transfers between devices  2.72 us (3%)
  local copies, waits for them, and re-layouts  2.71 us (3%)
    all_to_all x1, blocking collectives, on_device(): gathered = lax.all_to_all(mixed, 'cand', 0, 0, tiled=True)  32.1 us
    ppermute x4, starting transfers between devices, passed_along(): lax.ppermute(value, axis, [(source, source + steps) for source in range(f...  20.6 us
    pallas_call x1, Pallas kernels, attend_all(): pl.pallas_call(attention_kernel, out_shape=jax.ShapeDtypeStruct((cands, q...  20.4 us
    select_n x1, other arithmetic, cos_and_sin(): return jnp.where(quadrant + 1 & 2 != 0, -base, base)  7.16 us
    all_to_all x1, starting transfers between devices, on_device(): lax.all_to_all(jnp.broadcast_to(factors, (cands, factors.shape[1])), 'can...  4.47 us
    ppermute x4, waiting for transfers between devices, passed_along(): lax.ppermute(value, axis, [(source, source + steps) for source in range(f...  2.72 us
    pallas_call x1, Pallas kernels, side_by_side(): pl.pallas_call(place_kernel, out_shape=jax.ShapeDtypeStruct((rows, count...  2.61 us
    select_n x1, other arithmetic, on_device(): bias = jnp.where(allowed, 0.0, -1e+30).astype(jnp.float32)  2.04 us
  transfers between devices with their start and end apart: 5, of which 1 were waited for; matrix products, arithmetic and copies ran while one was open for 14% of the time, Pallas kernels for 0%

profile of v14, /device:TPU:96, one launch (start us, length us, event | category | flops | bytes accessed | tf_op | source)
XLA Modules:
  0.0 97.8 jit_solution(5612994836596987270)
XLA Ops:
  0.0 0.0 copy-start
  0.0 3.5 %collective-permute-start = (bf16[2,128,128]{2,1,0:T(8,128)(2,1)}, bf16[2,128,128]{2,1,0:T(8,128)(2,1)S(1)}, u32[]{:S(2)}, u32[]{:S(2)}) collective-permute-start(bf16[2,128,128]{2,1,0:T(8,128)(2,1)} %param.5), channel_id=1, source_target_pairs={{0,1},{1,2},{2,3},{3,4},{4,5},{5,6},{6,7},{7,8},{8,9},{9,10},{10,1... | collective-permute-start | bytes 196616 | tf_op jit(solution)/shard_map/ppermute | solution.py:22
  3.5 6.4 %collective-permute-start.1 = (bf16[2,128,128]{2,1,0:T(8,128)(2,1)}, bf16[2,128,128]{2,1,0:T(8,128)(2,1)S(1)}, u32[]{:S(2)}, u32[]{:S(2)}) collective-permute-start(bf16[2,128,128]{2,1,0:T(8,128)(2,1)} %param.5), channel_id=1, source_target_pairs={{0,8},{1,9},{2,10},{3,11},{4,12},{5,13},{6,14},{7,15},{8,16},{9,17... | collective-permute-start | bytes 196616 | tf_op jit(solution)/shard_map/ppermute | solution.py:22
  10.0 0.0 collective-permute-done
  10.0 0.9 pad_maximum_fusion.2
  10.9 0.7 copy.8
  11.6 0.1 reduce
  11.8 0.7 sub.25
  12.4 0.1 convert_reduce_fusion.1
  12.5 0.1 convert_reduce_fusion
  12.6 0.1 select_reduce_fusion
  12.7 1.3 %broadcast_in_dim.64 = f32[8,1,64]{2,1,0:T(1,128)} broadcast(f32[64]{0:T(128)} %bitcast.6), dimensions={2} | broadcast | bytes 2304 | tf_op jit(solution)/shard_map/broadcast_in_dim | solution.py:171
  14.0 4.5 %all-to-all-start = ((f32[8,1,64]{2,1,0:T(1,128)}), f32[8,1,64]{2,1,0:T(1,128)S(1)}, u32[]{:S(2)}, u32[]{:S(2)}) async-start(f32[8,1,64]{2,1,0:T(1,128)} %broadcast_in_dim.64), calls=%async_computation | async-start | bytes 8192 | tf_op jit(solution)/shard_map/all_to_all | solution.py:170
  18.4 4.6 %collective-permute-start.2 = (bf16[2,256,128]{2,1,0:T(8,128)(2,1)S(1)}, bf16[2,256,128]{2,1,0:T(8,128)(2,1)S(1)}, u32[]{:S(2)}, u32[]{:S(2)}) collective-permute-start(bf16[2,256,128]{2,1,0:T(8,128)(2,1)S(1)} %pad_maximum_fusion.2), channel_id=1, source_target_pairs={{0,2},{1,3},{2,4},{3,5},{4,6},{5,7},{6,8},{7,9},{8,10},{9,11},{10,... | collective-permute-start | bytes 393224 | tf_op jit(solution)/shard_map/ppermute | solution.py:22
  23.1 2.0 %and_select_fusion.bias_ref = f32[1152,128]{1,0:T(8,128)} fusion(s32[128]{0:T(128)S(1)} %iota_add_fusion.1, s32[128]{0:T(128)S(1)} %compare_select_fusion, s32[1152]{0:T(1024)S(1)} %iota_add_fusion, s32[1152]{0:T(1024)S(1)} %get-tuple-element.14, pred[1152]{0:T(1024)(128)(4,1)S(1)} %get-tuple-element.13), kind=kLoop, calls=%fused_computation.35 | loop fusion | flops 737280 | bytes 601216 | tf_op jit(solution)/shard_map/jit(_where)/select_n | solution.py:180
  25.1 0.0 copy-done
  25.1 0.7 constant_dynamic-slice_fusion.q_ref
  25.8 0.0 all-to-all-done
  25.8 0.1 pad_maximum_fusion.3
  25.9 2.7 %collective-permute-done.2 = bf16[2,256,128]{2,1,0:T(8,128)(2,1)S(1)} collective-permute-done((bf16[2,256,128]{2,1,0:T(8,128)(2,1)S(1)}, bf16[2,256,128]{2,1,0:T(8,128)(2,1)S(1)}, u32[]{:S(2)}, u32[]{:S(2)}) %collective-permute-start.2) | collective-permute-done | bytes 131104 | tf_op jit(solution)/shard_map/ppermute | solution.py:22
  28.7 6.1 %collective-permute-start.3 = (bf16[2,512,128]{2,1,0:T(8,128)(2,1)S(1)}, bf16[2,512,128]{2,1,0:T(8,128)(2,1)S(1)}, u32[]{:S(2)}, u32[]{:S(2)}) collective-permute-start(bf16[2,512,128]{2,1,0:T(8,128)(2,1)S(1)} %pad_maximum_fusion.1), channel_id=1, source_target_pairs={{0,4},{1,5},{2,6},{3,7},{4,8},{5,9},{6,10},{7,11},{8,12},{9,13},{1... | collective-permute-start | bytes 786440 | tf_op jit(solution)/shard_map/ppermute | solution.py:22
  34.7 7.2 %negate_select_fusion.table_ref = f32[8,1152,128]{2,1,0:T(8,128)} fusion(s32[128]{0:T(128)S(1)} %compare_select_fusion.1, f32[8,128]{1,0:T(8,128)S(1)} %pad_maximum_fusion.3, f32[1152]{0:T(1024)S(1)} %select_convert_fusion), kind=kLoop, calls=%fused_computation | loop fusion | flops 43646976 | bytes 4727808 | tf_op jit(solution)/shard_map/jit(_where)/select_n | solution.py:51
  41.9 0.0 collective-permute-done.1
  41.9 0.0 collective-permute-done.3
  41.9 0.9 pad_maximum_fusion.kv_ref
  42.8 20.4 %shard_map.46 = bf16[8,128,1024]{2,1,0:T(8,128)(2,1)} custom-call(bf16[128,1024]{1,0:T(8,128)(2,1)} %constant_dynamic-slice_fusion.q_ref, bf16[2,1152,128]{2,1,0:T(8,128)(2,1)} %pad_maximum_fusion.kv_ref, f32[8,1152,128]{2,1,0:T(8,128)} %negate_select_fusion.table_ref, f32[1152,128]{1,0:T(8,128)} %and_select_fusion.bias_ref), custom_call_target="tpu_custom_call" | custom-call | flops 4831838208 | bytes 2949120 | tf_op jit(solution)/shard_map/pallas_call | solution.py:109
  63.1 32.1 %all_to_all.14.in_ref = bf16[8,128,1024]{2,1,0:T(8,128)(2,1)} all-to-all(bf16[8,128,1024]{2,1,0:T(8,128)(2,1)} %shard_map.46), channel_id=1, replica_groups=mesh['cand'=8,'doc'=64] {'cand'}, dimensions={0} | all-to-all | bytes 4194304 | tf_op jit(solution)/shard_map/all_to_all | solution.py:184
  95.2 2.6 %shard_map.47 = bf16[128,8192]{1,0:T(8,128)(2,1)} custom-call(bf16[8,128,1024]{2,1,0:T(8,128)(2,1)} %all_to_all.14.in_ref), custom_call_target="tpu_custom_call" | custom-call | tf_op jit(solution)/shard_map/pallas_call | solution.py:137
  (10 shorter events, 0.1 us)
Async XLA Ops:
  0.0 25.1 %copy-start = (bf16[128,8192]{1,0:T(8,128)(2,1)S(1)}, bf16[128,8192]{1,0:T(8,128)(2,1)}, u32[]{:S(2)}) copy-start(bf16[128,8192]{1,0:T(8,128)(2,1)} %param.4) | copy-start | bytes 6291460
  0.0 10.0 %collective-permute-start = (bf16[2,128,128]{2,1,0:T(8,128)(2,1)}, bf16[2,128,128]{2,1,0:T(8,128)(2,1)S(1)}, u32[]{:S(2)}, u32[]{:S(2)}) collective-permute-start(bf16[2,128,128]{2,1,0:T(8,128)(2,1)} %param.5), channel_id=1, source_target_pairs={{0,1},{1,2},{2,3},{3,4},{4,5},{5,6},{6,7},{7,8},{8,9},{9,10},{10,1... | collective-permute-start | bytes 196616 | tf_op jit(solution)/shard_map/ppermute | solution.py:22
  3.5 38.4 %collective-permute-start.1 = (bf16[2,128,128]{2,1,0:T(8,128)(2,1)}, bf16[2,128,128]{2,1,0:T(8,128)(2,1)S(1)}, u32[]{:S(2)}, u32[]{:S(2)}) collective-permute-start(bf16[2,128,128]{2,1,0:T(8,128)(2,1)} %param.5), channel_id=1, source_target_pairs={{0,8},{1,9},{2,10},{3,11},{4,12},{5,13},{6,14},{7,15},{8,16},{9,17... | collective-permute-start | bytes 196616 | tf_op jit(solution)/shard_map/ppermute | solution.py:22
  14.0 11.9 %all-to-all-start = ((f32[8,1,64]{2,1,0:T(1,128)}), f32[8,1,64]{2,1,0:T(1,128)S(1)}, u32[]{:S(2)}, u32[]{:S(2)}) async-start(f32[8,1,64]{2,1,0:T(1,128)} %broadcast_in_dim.64), calls=%async_computation | async-start | bytes 8192 | tf_op jit(solution)/shard_map/all_to_all | solution.py:170
  18.4 10.2 %collective-permute-start.2 = (bf16[2,256,128]{2,1,0:T(8,128)(2,1)S(1)}, bf16[2,256,128]{2,1,0:T(8,128)(2,1)S(1)}, u32[]{:S(2)}, u32[]{:S(2)}) collective-permute-start(bf16[2,256,128]{2,1,0:T(8,128)(2,1)S(1)} %pad_maximum_fusion.2), channel_id=1, source_target_pairs={{0,2},{1,3},{2,4},{3,5},{4,6},{5,7},{6,8},{7,9},{8,10},{9,11},{10,... | collective-permute-start | bytes 393224 | tf_op jit(solution)/shard_map/ppermute | solution.py:22
  28.7 13.2 %collective-permute-start.3 = (bf16[2,512,128]{2,1,0:T(8,128)(2,1)S(1)}, bf16[2,512,128]{2,1,0:T(8,128)(2,1)S(1)}, u32[]{:S(2)}, u32[]{:S(2)}) collective-permute-start(bf16[2,512,128]{2,1,0:T(8,128)(2,1)S(1)} %pad_maximum_fusion.1), channel_id=1, source_target_pairs={{0,4},{1,5},{2,6},{3,7},{4,8},{5,9},{6,10},{7,11},{8,12},{9,13},{1... | collective-permute-start | bytes 786440 | tf_op jit(solution)/shard_map/ppermute | solution.py:22

commit v15 on v14

--- a/solution.py
+++ b/solution.py
@@ -156,15 +156,13 @@
     query_index = device * row_count + jnp.arange(row_count, dtype=jnp.int32)
     key_index = (device - SPAN) * row_count + jnp.arange((SPAN + 1) * row_count, dtype=jnp.int32)
     far = passed_along(keys_values, "doc", SPAN)
-    window = keys_values
-    reach = 1
-    while reach < SPAN:
-        window = jnp.concatenate([passed_along(window, "doc", reach), window], axis=1)
-        if reach == 1:
-            window, factors, lengths, queries = lax.optimization_barrier(
-                (window, factors, lengths, queries)
-            )
-        reach *= 2
+    quarter = SPAN // 2
+    near = jnp.concatenate(
+        [passed_along(keys_values, "doc", step) for step in range(quarter - 1, 0, -1)] + [keys_values],
+        axis=1,
+    )
+    near, factors, lengths, queries = lax.optimization_barrier((near, factors, lengths, queries))
+    window = jnp.concatenate([passed_along(near, "doc", quarter), near], axis=1)
     window = jnp.concatenate([far, window], axis=1)
     cands = lax.axis_size("cand")
     every_factor = lax.all_to_all(

time: 98.2 us -> 98.8 us (level)
  the two profiles are of different devices: /device:TPU:96 before, /device:TPU:1 now
where the time goes in v15:
time: 98.8 us; the launch traced here: 98.4 us
  blocking collectives  31.7 us (32%)
  starting transfers between devices  28.8 us (29%)
  Pallas kernels  23 us (23%)
  other arithmetic  12.1 us (12%)
  local copies, waits for them, and re-layouts  2.7 us (3%)
    all_to_all x1, blocking collectives, on_device(): gathered = lax.all_to_all(mixed, 'cand', 0, 0, tiled=True)  31.7 us
    ppermute x5, starting transfers between devices, passed_along(): lax.ppermute(value, axis, [(source, source + steps) for source in range(f...  22.5 us
    pallas_call x1, Pallas kernels, attend_all(): pl.pallas_call(attention_kernel, out_shape=jax.ShapeDtypeStruct((cands, q...  20.4 us
    select_n x1, other arithmetic, cos_and_sin(): return jnp.where(quadrant + 1 & 2 != 0, -base, base)  7.15 us
    all_to_all x1, starting transfers between devices, on_device(): lax.all_to_all(jnp.broadcast_to(factors, (cands, factors.shape[1])), 'can...  6.26 us
    pallas_call x1, Pallas kernels, side_by_side(): pl.pallas_call(place_kernel, out_shape=jax.ShapeDtypeStruct((rows, count...  2.61 us
    select_n x1, other arithmetic, on_device(): bias = jnp.where(allowed, 0.0, -1e+30).astype(jnp.float32)  2.04 us
  transfers between devices with their start and end apart: 6, of which 0 were waited for; matrix products, arithmetic and copies ran while one was open for 14% of the time, Pallas kernels for 0%

profile of v15, /device:TPU:1, one launch (start us, length us, event | category | flops | bytes accessed | tf_op | source)
XLA Modules:
  0.0 98.4 jit_solution(13423297100686795716)
XLA Ops:
  0.0 0.0 copy-start
  0.0 4.1 %collective-permute-start.2 = (bf16[2,128,128]{2,1,0:T(8,128)(2,1)}, bf16[2,128,128]{2,1,0:T(8,128)(2,1)S(1)}, u32[]{:S(2)}, u32[]{:S(2)}) collective-permute-start(bf16[2,128,128]{2,1,0:T(8,128)(2,1)} %param.5), channel_id=1, source_target_pairs={{0,1},{1,2},{2,3},{3,4},{4,5},{5,6},{6,7},{7,8},{8,9},{9,10},{10,1... | collective-permute-start | bytes 196616 | tf_op jit(solution)/shard_map/ppermute | solution.py:22
  4.1 4.4 %collective-permute-start.1 = (bf16[2,128,128]{2,1,0:T(8,128)(2,1)}, bf16[2,128,128]{2,1,0:T(8,128)(2,1)S(1)}, u32[]{:S(2)}, u32[]{:S(2)}) collective-permute-start(bf16[2,128,128]{2,1,0:T(8,128)(2,1)} %param.5), channel_id=1, source_target_pairs={{0,2},{1,3},{2,4},{3,5},{4,6},{5,7},{6,8},{7,9},{8,10},{9,11},{10,... | collective-permute-start | bytes 196616 | tf_op jit(solution)/shard_map/ppermute | solution.py:22
  8.4 4.4 %collective-permute-start = (bf16[2,128,128]{2,1,0:T(8,128)(2,1)}, bf16[2,128,128]{2,1,0:T(8,128)(2,1)S(1)}, u32[]{:S(2)}, u32[]{:S(2)}) collective-permute-start(bf16[2,128,128]{2,1,0:T(8,128)(2,1)} %param.5), channel_id=1, source_target_pairs={{0,3},{1,4},{2,5},{3,6},{4,7},{5,8},{6,9},{7,10},{8,11},{9,12},{10... | collective-permute-start | bytes 196616 | tf_op jit(solution)/shard_map/ppermute | solution.py:22
  12.9 4.9 %collective-permute-start.3 = (bf16[2,128,128]{2,1,0:T(8,128)(2,1)}, bf16[2,128,128]{2,1,0:T(8,128)(2,1)S(1)}, u32[]{:S(2)}, u32[]{:S(2)}) collective-permute-start(bf16[2,128,128]{2,1,0:T(8,128)(2,1)} %param.5), channel_id=1, source_target_pairs={{0,8},{1,9},{2,10},{3,11},{4,12},{5,13},{6,14},{7,15},{8,16},{9,17... | collective-permute-start | bytes 196616 | tf_op jit(solution)/shard_map/ppermute | solution.py:22
  17.8 0.0 collective-permute-done.2
  17.9 0.0 collective-permute-done.1
  17.9 0.0 collective-permute-done
  17.9 0.9 pad_maximum_fusion.1
  18.7 0.7 copy.8
  19.5 0.1 reduce
  19.6 0.7 sub.25
  20.3 0.1 convert_reduce_fusion.1
  20.4 0.1 convert_reduce_fusion
  20.5 0.1 select_reduce_fusion
  20.6 1.3 %broadcast_in_dim.64 = f32[8,1,64]{2,1,0:T(1,128)} broadcast(f32[64]{0:T(128)} %bitcast.6), dimensions={2} | broadcast | bytes 2304 | tf_op jit(solution)/shard_map/broadcast_in_dim | solution.py:169
  21.9 6.3 %all-to-all-start = ((f32[8,1,64]{2,1,0:T(1,128)}), f32[8,1,64]{2,1,0:T(1,128)S(1)}, u32[]{:S(2)}, u32[]{:S(2)}) async-start(f32[8,1,64]{2,1,0:T(1,128)} %broadcast_in_dim.64), calls=%async_computation | async-start | bytes 8192 | tf_op jit(solution)/shard_map/all_to_all | solution.py:168
  28.1 4.8 %collective-permute-start.4 = (bf16[2,512,128]{2,1,0:T(8,128)(2,1)S(1)}, bf16[2,512,128]{2,1,0:T(8,128)(2,1)S(1)}, u32[]{:S(2)}, u32[]{:S(2)}) collective-permute-start(bf16[2,512,128]{2,1,0:T(8,128)(2,1)S(1)} %pad_maximum_fusion.1), channel_id=1, source_target_pairs={{0,4},{1,5},{2,6},{3,7},{4,8},{5,9},{6,10},{7,11},{8,12},{9,13},{1... | collective-permute-start | bytes 786440 | tf_op jit(solution)/shard_map/ppermute | solution.py:22
  32.9 2.0 %and_select_fusion.bias_ref = f32[1152,128]{1,0:T(8,128)} fusion(s32[128]{0:T(128)S(1)} %iota_add_fusion.1, s32[128]{0:T(128)S(1)} %compare_select_fusion, s32[1152]{0:T(1024)S(1)} %iota_add_fusion, s32[1152]{0:T(1024)S(1)} %get-tuple-element.14, pred[1152]{0:T(1024)(128)(4,1)S(1)} %get-tuple-element.13), kind=kLoop, calls=%fused_computation.35 | loop fusion | flops 737280 | bytes 601216 | tf_op jit(solution)/shard_map/jit(_where)/select_n | solution.py:178
  34.9 0.0 copy-done
  34.9 0.7 constant_dynamic-slice_fusion.q_ref
  35.6 0.0 all-to-all-done
  35.6 0.1 pad_maximum_fusion.2
  35.7 7.1 %negate_select_fusion.table_ref = f32[8,1152,128]{2,1,0:T(8,128)} fusion(s32[128]{0:T(128)S(1)} %compare_select_fusion.1, f32[8,128]{1,0:T(8,128)S(1)} %pad_maximum_fusion.2, f32[1152]{0:T(1024)S(1)} %select_convert_fusion), kind=kLoop, calls=%fused_computation | loop fusion | flops 43646976 | bytes 4727808 | tf_op jit(solution)/shard_map/jit(_where)/select_n | solution.py:51
  42.9 0.0 collective-permute-done.3
  42.9 0.0 collective-permute-done.4
  42.9 0.9 pad_maximum_fusion.kv_ref
  43.8 20.4 %shard_map.46 = bf16[8,128,1024]{2,1,0:T(8,128)(2,1)} custom-call(bf16[128,1024]{1,0:T(8,128)(2,1)} %constant_dynamic-slice_fusion.q_ref, bf16[2,1152,128]{2,1,0:T(8,128)(2,1)} %pad_maximum_fusion.kv_ref, f32[8,1152,128]{2,1,0:T(8,128)} %negate_select_fusion.table_ref, f32[1152,128]{1,0:T(8,128)} %and_select_fusion.bias_ref), custom_call_target="tpu_custom_call" | custom-call | flops 4831838208 | bytes 2949120 | tf_op jit(solution)/shard_map/pallas_call | solution.py:109
  64.1 31.7 %all_to_all.14.in_ref = bf16[8,128,1024]{2,1,0:T(8,128)(2,1)} all-to-all(bf16[8,128,1024]{2,1,0:T(8,128)(2,1)} %shard_map.46), channel_id=1, replica_groups=mesh['cand'=8,'doc'=64] {'cand'}, dimensions={0} | all-to-all | bytes 4194304 | tf_op jit(solution)/shard_map/all_to_all | solution.py:182
  95.8 2.6 %shard_map.47 = bf16[128,8192]{1,0:T(8,128)(2,1)} custom-call(bf16[8,128,1024]{2,1,0:T(8,128)(2,1)} %all_to_all.14.in_ref), custom_call_target="tpu_custom_call" | custom-call | tf_op jit(solution)/shard_map/pallas_call | solution.py:137
  (9 shorter events, 0.1 us)
Async XLA Ops:
  0.0 34.9 %copy-start = (bf16[128,8192]{1,0:T(8,128)(2,1)S(1)}, bf16[128,8192]{1,0:T(8,128)(2,1)}, u32[]{:S(2)}) copy-start(bf16[128,8192]{1,0:T(8,128)(2,1)} %param.4) | copy-start | bytes 6291460
  0.0 17.8 %collective-permute-start.2 = (bf16[2,128,128]{2,1,0:T(8,128)(2,1)}, bf16[2,128,128]{2,1,0:T(8,128)(2,1)S(1)}, u32[]{:S(2)}, u32[]{:S(2)}) collective-permute-start(bf16[2,128,128]{2,1,0:T(8,128)(2,1)} %param.5), channel_id=1, source_target_pairs={{0,1},{1,2},{2,3},{3,4},{4,5},{5,6},{6,7},{7,8},{8,9},{9,10},{10,1... | collective-permute-start | bytes 196616 | tf_op jit(solution)/shard_map/ppermute | solution.py:22
  4.1 13.8 %collective-permute-start.1 = (bf16[2,128,128]{2,1,0:T(8,128)(2,1)}, bf16[2,128,128]{2,1,0:T(8,128)(2,1)S(1)}, u32[]{:S(2)}, u32[]{:S(2)}) collective-permute-start(bf16[2,128,128]{2,1,0:T(8,128)(2,1)} %param.5), channel_id=1, source_target_pairs={{0,2},{1,3},{2,4},{3,5},{4,6},{5,7},{6,8},{7,9},{8,10},{9,11},{10,... | collective-permute-start | bytes 196616 | tf_op jit(solution)/shard_map/ppermute | solution.py:22
  8.4 9.4 %collective-permute-start = (bf16[2,128,128]{2,1,0:T(8,128)(2,1)}, bf16[2,128,128]{2,1,0:T(8,128)(2,1)S(1)}, u32[]{:S(2)}, u32[]{:S(2)}) collective-permute-start(bf16[2,128,128]{2,1,0:T(8,128)(2,1)} %param.5), channel_id=1, source_target_pairs={{0,3},{1,4},{2,5},{3,6},{4,7},{5,8},{6,9},{7,10},{8,11},{9,12},{10... | collective-permute-start | bytes 196616 | tf_op jit(solution)/shard_map/ppermute | solution.py:22
  12.9 30.0 %collective-permute-start.3 = (bf16[2,128,128]{2,1,0:T(8,128)(2,1)}, bf16[2,128,128]{2,1,0:T(8,128)(2,1)S(1)}, u32[]{:S(2)}, u32[]{:S(2)}) collective-permute-start(bf16[2,128,128]{2,1,0:T(8,128)(2,1)} %param.5), channel_id=1, source_target_pairs={{0,8},{1,9},{2,10},{3,11},{4,12},{5,13},{6,14},{7,15},{8,16},{9,17... | collective-permute-start | bytes 196616 | tf_op jit(solution)/shard_map/ppermute | solution.py:22
  21.9 13.8 %all-to-all-start = ((f32[8,1,64]{2,1,0:T(1,128)}), f32[8,1,64]{2,1,0:T(1,128)S(1)}, u32[]{:S(2)}, u32[]{:S(2)}) async-start(f32[8,1,64]{2,1,0:T(1,128)} %broadcast_in_dim.64), calls=%async_computation | async-start | bytes 8192 | tf_op jit(solution)/shard_map/all_to_all | solution.py:168
  28.1 14.8 %collective-permute-start.4 = (bf16[2,512,128]{2,1,0:T(8,128)(2,1)S(1)}, bf16[2,512,128]{2,1,0:T(8,128)(2,1)S(1)}, u32[]{:S(2)}, u32[]{:S(2)}) collective-permute-start(bf16[2,512,128]{2,1,0:T(8,128)(2,1)S(1)} %pad_maximum_fusion.1), channel_id=1, source_target_pairs={{0,4},{1,5},{2,6},{3,7},{4,8},{5,9},{6,10},{7,11},{8,12},{9,13},{1... | collective-permute-start | bytes 786440 | tf_op jit(solution)/shard_map/ppermute | solution.py:22

commit v16 on v14

--- a/solution.py
+++ b/solution.py
@@ -51,7 +51,7 @@
     return jnp.where(((quadrant + 1) & 2) != 0, -base, base)
 
 
-def attention_kernel(q_ref, kv_ref, table_ref, bias_ref, out_ref):
+def attention_kernel(q_ref, far_ref, mid_ref, near_ref, table_ref, bias_ref, out_ref):
     half_dim = HD // 2
     group_size = H // KVH
     query_rows = q_ref.shape[0]
@@ -60,7 +60,7 @@
     swapped = pltpu.roll(table, half_dim, 1)
     cosine = jnp.where(low, table, swapped)
     sine = jnp.where(low, -swapped, table)
-    keys = kv_ref[0].astype(jnp.float32)
+    keys = jnp.concatenate([far_ref[0], mid_ref[0], near_ref[0]], axis=0).astype(jnp.float32)
     key_rot = (keys * cosine + pltpu.roll(keys, half_dim, 1) * sine).astype(jnp.bfloat16)
     first_query = table.shape[0] - query_rows
     q_cos = cosine[first_query:]
@@ -89,7 +89,7 @@
         totals.append(jnp.sum(expw, axis=0, keepdims=True))
         weights.append(expw.astype(jnp.bfloat16))
     numer = lax.dot_general(
-        kv_ref[1], jnp.concatenate(weights, axis=1), (((0,), (0,)), ((), ())),
+        jnp.concatenate([far_ref[1], mid_ref[1], near_ref[1]], axis=0), jnp.concatenate(weights, axis=1), (((0,), (0,)), ((), ())),
         preferred_element_type=jnp.float32,
     )
     for head in range(group_size):
@@ -97,12 +97,12 @@
         out_ref[0, :, head * HD : (head + 1) * HD] = cols.T.astype(jnp.bfloat16)
 
 
-def attend_all(own_queries, window, offsets, inverse, bias):
+def attend_all(own_queries, far, mid, near, offsets, inverse, bias):
     angle = offsets[None] * inverse
     low = lax.broadcasted_iota(jnp.int32, angle.shape, 2) < HD // 2
     table = cos_and_sin(angle, low)
     cands = inverse.shape[0]
-    key_rows = window.shape[1]
+    key_rows = far.shape[1] + mid.shape[1] + near.shape[1]
     query_rows, width = own_queries.shape
     heads = width // HD
     flops = cands * heads * 4 * query_rows * key_rows * HD
@@ -112,7 +112,9 @@
         grid=(cands,),
         in_specs=[
             pl.BlockSpec((query_rows, width), lambda c: (0, 0)),
-            pl.BlockSpec(window.shape, lambda c: (0, 0, 0)),
+            pl.BlockSpec(far.shape, lambda c: (0, 0, 0)),
+            pl.BlockSpec(mid.shape, lambda c: (0, 0, 0)),
+            pl.BlockSpec(near.shape, lambda c: (0, 0, 0)),
             pl.BlockSpec((1, key_rows, HD), lambda c: (c, 0, 0)),
             pl.BlockSpec(bias.T.shape, lambda c: (0, 0)),
         ],
@@ -120,9 +122,9 @@
         cost_estimate=pl.CostEstimate(
             flops=flops,
             transcendentals=cands * heads * query_rows * key_rows,
-            bytes_accessed=window.size * 2 + own_queries.size * 2 + cands * query_rows * width * 2,
+            bytes_accessed=(far.size + mid.size + near.size) * 2 + own_queries.size * 2 + cands * query_rows * width * 2,
         ),
-    )(own_queries, window, table, bias.T)
+    )(own_queries, far, mid, near, table, bias.T)
 
 
 def place_kernel(in_ref, out_ref):
@@ -159,13 +161,16 @@
     window = keys_values
     reach = 1
     while reach < SPAN:
+        if 2 * reach == SPAN:
+            mid = passed_along(window, "doc", reach)
+            reach *= 2
+            continue
         window = jnp.concatenate([passed_along(window, "doc", reach), window], axis=1)
         if reach == 1:
             window, factors, lengths, queries = lax.optimization_barrier(
                 (window, factors, lengths, queries)
             )
         reach *= 2
-    window = jnp.concatenate([far, window], axis=1)
     cands = lax.axis_size("cand")
     every_factor = lax.all_to_all(
         jnp.broadcast_to(factors, (cands, factors.shape[1])), "cand", 0, 0, tiled=True
@@ -180,7 +185,7 @@
     bias = jnp.where(allowed, 0.0, -1e30).astype(jnp.float32)
     offsets = jnp.broadcast_to(key_offset.astype(jnp.float32)[:, None], (key_offset.shape[0], HD))
     own_queries = lax.dynamic_slice_in_dim(queries, group * group_width, group_width, 1)
-    mixed = attend_all(own_queries, window, offsets, inverse_rows(every_factor), bias)
+    mixed = attend_all(own_queries, far, mid, window, offsets, inverse_rows(every_factor), bias)
     gathered = lax.all_to_all(mixed, "cand", 0, 0, tiled=True)
     return side_by_side(gathered)[None]
 

time: 98.2 us -> 98.8 us (level)
  the two profiles are of different devices: /device:TPU:96 before, /device:TPU:224 now
where the time goes in v16:
time: 98.8 us; the launch traced here: 98.4 us
  blocking collectives  32.1 us (32%)
  starting transfers between devices  25.1 us (25%)
  Pallas kernels  23.1 us (23%)
  other arithmetic  11.3 us (11%)
  local copies, waits for them, and re-layouts  4.07 us (4%)
  waiting for transfers between devices  2.72 us (3%)
    all_to_all x1, blocking collectives, on_device(): gathered = lax.all_to_all(mixed, 'cand', 0, 0, tiled=True)  32.1 us
    ppermute x4, starting transfers between devices, passed_along(): lax.ppermute(value, axis, [(source, source + steps) for source in range(f...  20.6 us
    pallas_call x1, Pallas kernels, attend_all(): pl.pallas_call(attention_kernel, out_shape=jax.ShapeDtypeStruct((cands, q...  20.5 us
    select_n x1, other arithmetic, cos_and_sin(): return jnp.where(quadrant + 1 & 2 != 0, -base, base)  7.16 us
    all_to_all x1, starting transfers between devices, on_device(): lax.all_to_all(jnp.broadcast_to(factors, (cands, factors.shape[1])), 'can...  4.47 us
    ppermute x4, waiting for transfers between devices, passed_along(): lax.ppermute(value, axis, [(source, source + steps) for source in range(f...  2.72 us
    pallas_call x1, Pallas kernels, side_by_side(): pl.pallas_call(place_kernel, out_shape=jax.ShapeDtypeStruct((rows, count...  2.61 us
    select_n x1, other arithmetic, on_device(): bias = jnp.where(allowed, 0.0, -1e+30).astype(jnp.float32)  2.05 us
  transfers between devices with their start and end apart: 5, of which 1 were waited for; matrix products, arithmetic and copies ran while one was open for 14% of the time, Pallas kernels for 0%

profile of v16, /device:TPU:224, one launch (start us, length us, event | category | flops | bytes accessed | tf_op | source)
XLA Modules:
  0.0 98.4 jit_solution(6239270745792551720)
XLA Ops:
  0.0 0.0 copy-start
  0.0 3.5 %collective-permute-start = (bf16[2,128,128]{2,1,0:T(8,128)(2,1)}, bf16[2,128,128]{2,1,0:T(8,128)(2,1)S(1)}, u32[]{:S(2)}, u32[]{:S(2)}) collective-permute-start(bf16[2,128,128]{2,1,0:T(8,128)(2,1)} %param.5), channel_id=1, source_target_pairs={{0,1},{1,2},{2,3},{3,4},{4,5},{5,6},{6,7},{7,8},{8,9},{9,10},{10,1... | collective-permute-start | bytes 196616 | tf_op jit(solution)/shard_map/ppermute | solution.py:22
  3.5 5.5 %collective-permute-start.1 = (bf16[2,128,128]{2,1,0:T(8,128)(2,1)}, bf16[2,128,128]{2,1,0:T(8,128)(2,1)S(1)}, u32[]{:S(2)}, u32[]{:S(2)}) collective-permute-start(bf16[2,128,128]{2,1,0:T(8,128)(2,1)} %param.5), channel_id=1, source_target_pairs={{0,8},{1,9},{2,10},{3,11},{4,12},{5,13},{6,14},{7,15},{8,16},{9,17... | collective-permute-start | bytes 196616 | tf_op jit(solution)/shard_map/ppermute | solution.py:22
  9.1 0.0 collective-permute-done
  9.1 0.9 pad_maximum_fusion
  10.0 0.7 copy.8
  10.7 0.1 reduce
  10.9 0.7 sub.25
  11.5 0.1 convert_reduce_fusion.1
  11.6 0.1 convert_reduce_fusion
  11.7 0.1 select_reduce_fusion
  11.8 1.3 %broadcast_in_dim.64 = f32[8,1,64]{2,1,0:T(1,128)} broadcast(f32[64]{0:T(128)} %bitcast.6), dimensions={2} | broadcast | bytes 2304 | tf_op jit(solution)/shard_map/broadcast_in_dim | solution.py:176
  13.1 4.5 %all-to-all-start = ((f32[8,1,64]{2,1,0:T(1,128)}), f32[8,1,64]{2,1,0:T(1,128)S(1)}, u32[]{:S(2)}, u32[]{:S(2)}) async-start(f32[8,1,64]{2,1,0:T(1,128)} %broadcast_in_dim.64), calls=%async_computation | async-start | bytes 8192 | tf_op jit(solution)/shard_map/all_to_all | solution.py:175
  17.5 4.6 %collective-permute-start.2 = (bf16[2,256,128]{2,1,0:T(8,128)(2,1)S(1)}, bf16[2,256,128]{2,1,0:T(8,128)(2,1)S(1)}, u32[]{:S(2)}, u32[]{:S(2)}) collective-permute-start(bf16[2,256,128]{2,1,0:T(8,128)(2,1)S(1)} %pad_maximum_fusion), channel_id=1, source_target_pairs={{0,2},{1,3},{2,4},{3,5},{4,6},{5,7},{6,8},{7,9},{8,10},{9,11},{10,... | collective-permute-start | bytes 393224 | tf_op jit(solution)/shard_map/ppermute | solution.py:22
  22.2 2.0 %and_select_fusion.bias_ref = f32[1152,128]{1,0:T(8,128)} fusion(s32[128]{0:T(128)S(1)} %iota_add_fusion.1, s32[128]{0:T(128)S(1)} %compare_select_fusion, s32[1152]{0:T(1024)S(1)} %iota_add_fusion, s32[1152]{0:T(1024)S(1)} %get-tuple-element.14, pred[1152]{0:T(1024)(128)(4,1)S(1)} %get-tuple-element.13), kind=kLoop, calls=%fused_computation.34 | loop fusion | flops 737280 | bytes 601216 | tf_op jit(solution)/shard_map/jit(_where)/select_n | solution.py:185
  24.2 0.0 copy-done
  24.2 0.7 constant_dynamic-slice_fusion.q_ref
  24.9 0.0 all-to-all-done
  24.9 0.1 pad_maximum_fusion.1
  25.0 2.7 %collective-permute-done.2 = bf16[2,256,128]{2,1,0:T(8,128)(2,1)S(1)} collective-permute-done((bf16[2,256,128]{2,1,0:T(8,128)(2,1)S(1)}, bf16[2,256,128]{2,1,0:T(8,128)(2,1)S(1)}, u32[]{:S(2)}, u32[]{:S(2)}) %collective-permute-start.2) | collective-permute-done | bytes 131104 | tf_op jit(solution)/shard_map/ppermute | solution.py:22
  27.8 0.0 copy-start.1
  27.8 7.0 %collective-permute-start.3 = (bf16[2,512,128]{2,1,0:T(8,128)(2,1)S(1)}, bf16[2,512,128]{2,1,0:T(8,128)(2,1)S(1)}, u32[]{:S(2)}, u32[]{:S(2)}) collective-permute-start(bf16[2,512,128]{2,1,0:T(8,128)(2,1)S(1)} %constant_dynamic-update-slice_fusion.near_ref), channel_id=1, source_target_pairs={{0,4},{1,5},{2,6},{3,7},{4,8},{5,9},{6,10},{7,11},{8,12},{9,13},{1... | collective-permute-start | bytes 786440 | tf_op jit(solution)/shard_map/ppermute | solution.py:22
  34.7 7.2 %negate_select_fusion.table_ref = f32[8,1152,128]{2,1,0:T(8,128)} fusion(s32[128]{0:T(128)S(1)} %compare_select_fusion.1, f32[8,128]{1,0:T(8,128)S(1)} %pad_maximum_fusion.1, f32[1152]{0:T(1024)S(1)} %select_convert_fusion), kind=kLoop, calls=%fused_computation | loop fusion | flops 43646976 | bytes 4727808 | tf_op jit(solution)/shard_map/jit(_where)/select_n | solution.py:51
  41.9 0.0 collective-permute-done.1.far_ref
  41.9 0.0 copy-start.3
  41.9 0.0 collective-permute-done.3.mid_ref
  41.9 0.0 copy-done.1
  41.9 0.6 copy-done.3
  42.5 0.0 copy-start.2
  42.5 0.7 copy-done.2
  43.3 20.5 %shard_map.46 = bf16[8,128,1024]{2,1,0:T(8,128)(2,1)} custom-call(bf16[128,1024]{1,0:T(8,128)(2,1)} %constant_dynamic-slice_fusion.q_ref, bf16[2,128,128]{2,1,0:T(8,128)(2,1)} %copy-done.3, bf16[2,512,128]{2,1,0:T(8,128)(2,1)} %copy-done.2, bf16[2,512,128]{2,1,0:T(8,128)(2,1)} %copy-done.1, f32[8,1152,128]{2,1,0:T(8,128)} %negate_select_fusion.table_ref, ...), custom_call_target="tpu_custom_call" | custom-call | flops 4831838208 | bytes 2949120 | tf_op jit(solution)/shard_map/pallas_call | solution.py:109
  63.7 32.1 %all_to_all.14.in_ref = bf16[8,128,1024]{2,1,0:T(8,128)(2,1)} all-to-all(bf16[8,128,1024]{2,1,0:T(8,128)(2,1)} %shard_map.46), channel_id=1, replica_groups=mesh['cand'=8,'doc'=64] {'cand'}, dimensions={0} | all-to-all | bytes 4194304 | tf_op jit(solution)/shard_map/all_to_all | solution.py:189
  95.8 2.6 %shard_map.47 = bf16[128,8192]{1,0:T(8,128)(2,1)} custom-call(bf16[8,128,1024]{2,1,0:T(8,128)(2,1)} %all_to_all.14.in_ref), custom_call_target="tpu_custom_call" | custom-call | tf_op jit(solution)/shard_map/pallas_call | solution.py:139
  (11 shorter events, 0.1 us)
Async XLA Ops:
  0.0 24.2 %copy-start = (bf16[128,8192]{1,0:T(8,128)(2,1)S(1)}, bf16[128,8192]{1,0:T(8,128)(2,1)}, u32[]{:S(2)}) copy-start(bf16[128,8192]{1,0:T(8,128)(2,1)} %param.4) | copy-start | bytes 6291460
  0.0 9.1 %collective-permute-start = (bf16[2,128,128]{2,1,0:T(8,128)(2,1)}, bf16[2,128,128]{2,1,0:T(8,128)(2,1)S(1)}, u32[]{:S(2)}, u32[]{:S(2)}) collective-permute-start(bf16[2,128,128]{2,1,0:T(8,128)(2,1)} %param.5), channel_id=1, source_target_pairs={{0,1},{1,2},{2,3},{3,4},{4,5},{5,6},{6,7},{7,8},{8,9},{9,10},{10,1... | collective-permute-start | bytes 196616 | tf_op jit(solution)/shard_map/ppermute | solution.py:22
  3.5 38.4 %collective-permute-start.1 = (bf16[2,128,128]{2,1,0:T(8,128)(2,1)}, bf16[2,128,128]{2,1,0:T(8,128)(2,1)S(1)}, u32[]{:S(2)}, u32[]{:S(2)}) collective-permute-start(bf16[2,128,128]{2,1,0:T(8,128)(2,1)} %param.5), channel_id=1, source_target_pairs={{0,8},{1,9},{2,10},{3,11},{4,12},{5,13},{6,14},{7,15},{8,16},{9,17... | collective-permute-start | bytes 196616 | tf_op jit(solution)/shard_map/ppermute | solution.py:22
  13.1 11.9 %all-to-all-start = ((f32[8,1,64]{2,1,0:T(1,128)}), f32[8,1,64]{2,1,0:T(1,128)S(1)}, u32[]{:S(2)}, u32[]{:S(2)}) async-start(f32[8,1,64]{2,1,0:T(1,128)} %broadcast_in_dim.64), calls=%async_computation | async-start | bytes 8192 | tf_op jit(solution)/shard_map/all_to_all | solution.py:175
  17.5 10.2 %collective-permute-start.2 = (bf16[2,256,128]{2,1,0:T(8,128)(2,1)S(1)}, bf16[2,256,128]{2,1,0:T(8,128)(2,1)S(1)}, u32[]{:S(2)}, u32[]{:S(2)}) collective-permute-start(bf16[2,256,128]{2,1,0:T(8,128)(2,1)S(1)} %pad_maximum_fusion), channel_id=1, source_target_pairs={{0,2},{1,3},{2,4},{3,5},{4,6},{5,7},{6,8},{7,9},{8,10},{9,11},{10,... | collective-permute-start | bytes 393224 | tf_op jit(solution)/shard_map/ppermute | solution.py:22
  27.8 14.1 %copy-start.1 = (bf16[2,512,128]{2,1,0:T(8,128)(2,1)}, bf16[2,512,128]{2,1,0:T(8,128)(2,1)S(1)}, u32[]{:S(2)}) copy-start(bf16[2,512,128]{2,1,0:T(8,128)(2,1)S(1)} %constant_dynamic-update-slice_fusion.near_ref) | copy-start | bytes 786436
  27.8 14.1 %collective-permute-start.3 = (bf16[2,512,128]{2,1,0:T(8,128)(2,1)S(1)}, bf16[2,512,128]{2,1,0:T(8,128)(2,1)S(1)}, u32[]{:S(2)}, u32[]{:S(2)}) collective-permute-start(bf16[2,512,128]{2,1,0:T(8,128)(2,1)S(1)} %constant_dynamic-update-slice_fusion.near_ref), channel_id=1, source_target_pairs={{0,4},{1,5},{2,6},{3,7},{4,8},{5,9},{6,10},{7,11},{8,12},{9,13},{1... | collective-permute-start | bytes 786440 | tf_op jit(solution)/shard_map/ppermute | solution.py:22
  41.9 0.6 copy-start.3
  42.5 0.7 copy-start.2

commit v17 on v14

--- a/solution.py
+++ b/solution.py
@@ -133,7 +133,7 @@
 
 def side_by_side(blocks):
     count, rows, width = blocks.shape
-    step = count // 2
+    step = count // 4
     return pl.pallas_call(
         place_kernel,
         out_shape=jax.ShapeDtypeStruct((rows, count * width), blocks.dtype),

time: 98.2 us -> 99.4 us (1.012)
  Pallas kernels: 23 us -> 24.1 us
    pallas_call x1, Pallas kernels: 2.61 us -> 3.77 us  [side_by_side(): pl.pallas_call(place_kernel, out_shape=jax.ShapeDtypeStruct((rows, count...]
where the time goes in v17:
time: 99.4 us; the launch traced here: 99 us
  blocking collectives  32.1 us (32%)
  starting transfers between devices  25.1 us (25%)
  Pallas kernels  24.1 us (24%)
  other arithmetic  12.2 us (12%)
  waiting for transfers between devices  2.72 us (3%)
  local copies, waits for them, and re-layouts  2.71 us (3%)
    all_to_all x1, blocking collectives, on_device(): gathered = lax.all_to_all(mixed, 'cand', 0, 0, tiled=True)  32.1 us
    ppermute x4, starting transfers between devices, passed_along(): lax.ppermute(value, axis, [(source, source + steps) for source in range(f...  20.6 us
    pallas_call x1, Pallas kernels, attend_all(): pl.pallas_call(attention_kernel, out_shape=jax.ShapeDtypeStruct((cands, q...  20.4 us
    select_n x1, other arithmetic, cos_and_sin(): return jnp.where(quadrant + 1 & 2 != 0, -base, base)  7.16 us
    all_to_all x1, starting transfers between devices, on_device(): lax.all_to_all(jnp.broadcast_to(factors, (cands, factors.shape[1])), 'can...  4.47 us
    pallas_call x1, Pallas kernels, side_by_side(): pl.pallas_call(place_kernel, out_shape=jax.ShapeDtypeStruct((rows, count...  3.77 us
    ppermute x4, waiting for transfers between devices, passed_along(): lax.ppermute(value, axis, [(source, source + steps) for source in range(f...  2.72 us
    select_n x1, other arithmetic, on_device(): bias = jnp.where(allowed, 0.0, -1e+30).astype(jnp.float32)  2.04 us
  transfers between devices with their start and end apart: 5, of which 1 were waited for; matrix products, arithmetic and copies ran while one was open for 14% of the time, Pallas kernels for 0%

profile of v17, /device:TPU:96, one launch (start us, length us, event | category | flops | bytes accessed | tf_op | source)
XLA Modules:
  0.0 99.0 jit_solution(11684779271742427951)
XLA Ops:
  0.0 0.0 copy-start
  0.0 3.5 %collective-permute-start = (bf16[2,128,128]{2,1,0:T(8,128)(2,1)}, bf16[2,128,128]{2,1,0:T(8,128)(2,1)S(1)}, u32[]{:S(2)}, u32[]{:S(2)}) collective-permute-start(bf16[2,128,128]{2,1,0:T(8,128)(2,1)} %param.5), channel_id=1, source_target_pairs={{0,1},{1,2},{2,3},{3,4},{4,5},{5,6},{6,7},{7,8},{8,9},{9,10},{10,1... | collective-permute-start | bytes 196616 | tf_op jit(solution)/shard_map/ppermute | solution.py:22
  3.5 6.4 %collective-permute-start.1 = (bf16[2,128,128]{2,1,0:T(8,128)(2,1)}, bf16[2,128,128]{2,1,0:T(8,128)(2,1)S(1)}, u32[]{:S(2)}, u32[]{:S(2)}) collective-permute-start(bf16[2,128,128]{2,1,0:T(8,128)(2,1)} %param.5), channel_id=1, source_target_pairs={{0,8},{1,9},{2,10},{3,11},{4,12},{5,13},{6,14},{7,15},{8,16},{9,17... | collective-permute-start | bytes 196616 | tf_op jit(solution)/shard_map/ppermute | solution.py:22
  10.0 0.0 collective-permute-done
  10.0 0.9 pad_maximum_fusion.2
  10.9 0.7 copy.8
  11.6 0.1 reduce
  11.8 0.7 sub.25
  12.4 0.1 convert_reduce_fusion.1
  12.5 0.1 convert_reduce_fusion
  12.6 0.1 select_reduce_fusion
  12.7 1.3 %broadcast_in_dim.64 = f32[8,1,64]{2,1,0:T(1,128)} broadcast(f32[64]{0:T(128)} %bitcast.6), dimensions={2} | broadcast | bytes 2304 | tf_op jit(solution)/shard_map/broadcast_in_dim | solution.py:171
  14.0 4.5 %all-to-all-start = ((f32[8,1,64]{2,1,0:T(1,128)}), f32[8,1,64]{2,1,0:T(1,128)S(1)}, u32[]{:S(2)}, u32[]{:S(2)}) async-start(f32[8,1,64]{2,1,0:T(1,128)} %broadcast_in_dim.64), calls=%async_computation | async-start | bytes 8192 | tf_op jit(solution)/shard_map/all_to_all | solution.py:170
  18.4 4.6 %collective-permute-start.2 = (bf16[2,256,128]{2,1,0:T(8,128)(2,1)S(1)}, bf16[2,256,128]{2,1,0:T(8,128)(2,1)S(1)}, u32[]{:S(2)}, u32[]{:S(2)}) collective-permute-start(bf16[2,256,128]{2,1,0:T(8,128)(2,1)S(1)} %pad_maximum_fusion.2), channel_id=1, source_target_pairs={{0,2},{1,3},{2,4},{3,5},{4,6},{5,7},{6,8},{7,9},{8,10},{9,11},{10,... | collective-permute-start | bytes 393224 | tf_op jit(solution)/shard_map/ppermute | solution.py:22
  23.1 2.0 %and_select_fusion.bias_ref = f32[1152,128]{1,0:T(8,128)} fusion(s32[128]{0:T(128)S(1)} %iota_add_fusion.1, s32[128]{0:T(128)S(1)} %compare_select_fusion, s32[1152]{0:T(1024)S(1)} %iota_add_fusion, s32[1152]{0:T(1024)S(1)} %get-tuple-element.14, pred[1152]{0:T(1024)(128)(4,1)S(1)} %get-tuple-element.13), kind=kLoop, calls=%fused_computation.35 | loop fusion | flops 737280 | bytes 601216 | tf_op jit(solution)/shard_map/jit(_where)/select_n | solution.py:180
  25.1 0.0 copy-done
  25.1 0.7 constant_dynamic-slice_fusion.q_ref
  25.8 0.0 all-to-all-done
  25.8 0.1 pad_maximum_fusion.3
  25.9 2.7 %collective-permute-done.2 = bf16[2,256,128]{2,1,0:T(8,128)(2,1)S(1)} collective-permute-done((bf16[2,256,128]{2,1,0:T(8,128)(2,1)S(1)}, bf16[2,256,128]{2,1,0:T(8,128)(2,1)S(1)}, u32[]{:S(2)}, u32[]{:S(2)}) %collective-permute-start.2) | collective-permute-done | bytes 131104 | tf_op jit(solution)/shard_map/ppermute | solution.py:22
  28.7 6.1 %collective-permute-start.3 = (bf16[2,512,128]{2,1,0:T(8,128)(2,1)S(1)}, bf16[2,512,128]{2,1,0:T(8,128)(2,1)S(1)}, u32[]{:S(2)}, u32[]{:S(2)}) collective-permute-start(bf16[2,512,128]{2,1,0:T(8,128)(2,1)S(1)} %pad_maximum_fusion.1), channel_id=1, source_target_pairs={{0,4},{1,5},{2,6},{3,7},{4,8},{5,9},{6,10},{7,11},{8,12},{9,13},{1... | collective-permute-start | bytes 786440 | tf_op jit(solution)/shard_map/ppermute | solution.py:22
  34.7 7.2 %negate_select_fusion.table_ref = f32[8,1152,128]{2,1,0:T(8,128)} fusion(s32[128]{0:T(128)S(1)} %compare_select_fusion.1, f32[8,128]{1,0:T(8,128)S(1)} %pad_maximum_fusion.3, f32[1152]{0:T(1024)S(1)} %select_convert_fusion), kind=kLoop, calls=%fused_computation | loop fusion | flops 43646976 | bytes 4727808 | tf_op jit(solution)/shard_map/jit(_where)/select_n | solution.py:51
  41.9 0.0 collective-permute-done.1
  41.9 0.0 collective-permute-done.3
  41.9 0.9 pad_maximum_fusion.kv_ref
  42.8 20.4 %shard_map.46 = bf16[8,128,1024]{2,1,0:T(8,128)(2,1)} custom-call(bf16[128,1024]{1,0:T(8,128)(2,1)} %constant_dynamic-slice_fusion.q_ref, bf16[2,1152,128]{2,1,0:T(8,128)(2,1)} %pad_maximum_fusion.kv_ref, f32[8,1152,128]{2,1,0:T(8,128)} %negate_select_fusion.table_ref, f32[1152,128]{1,0:T(8,128)} %and_select_fusion.bias_ref), custom_call_target="tpu_custom_call" | custom-call | flops 4831838208 | bytes 2949120 | tf_op jit(solution)/shard_map/pallas_call | solution.py:109
  63.1 32.1 %all_to_all.14.in_ref = bf16[8,128,1024]{2,1,0:T(8,128)(2,1)} all-to-all(bf16[8,128,1024]{2,1,0:T(8,128)(2,1)} %shard_map.46), channel_id=1, replica_groups=mesh['cand'=8,'doc'=64] {'cand'}, dimensions={0} | all-to-all | bytes 4194304 | tf_op jit(solution)/shard_map/all_to_all | solution.py:184
  95.2 3.8 %shard_map.47 = bf16[128,8192]{1,0:T(8,128)(2,1)} custom-call(bf16[8,128,1024]{2,1,0:T(8,128)(2,1)} %all_to_all.14.in_ref), custom_call_target="tpu_custom_call" | custom-call | tf_op jit(solution)/shard_map/pallas_call | solution.py:137
  (10 shorter events, 0.1 us)
Async XLA Ops:
  0.0 25.1 %copy-start = (bf16[128,8192]{1,0:T(8,128)(2,1)S(1)}, bf16[128,8192]{1,0:T(8,128)(2,1)}, u32[]{:S(2)}) copy-start(bf16[128,8192]{1,0:T(8,128)(2,1)} %param.4) | copy-start | bytes 6291460
  0.0 10.0 %collective-permute-start = (bf16[2,128,128]{2,1,0:T(8,128)(2,1)}, bf16[2,128,128]{2,1,0:T(8,128)(2,1)S(1)}, u32[]{:S(2)}, u32[]{:S(2)}) collective-permute-start(bf16[2,128,128]{2,1,0:T(8,128)(2,1)} %param.5), channel_id=1, source_target_pairs={{0,1},{1,2},{2,3},{3,4},{4,5},{5,6},{6,7},{7,8},{8,9},{9,10},{10,1... | collective-permute-start | bytes 196616 | tf_op jit(solution)/shard_map/ppermute | solution.py:22
  3.5 38.4 %collective-permute-start.1 = (bf16[2,128,128]{2,1,0:T(8,128)(2,1)}, bf16[2,128,128]{2,1,0:T(8,128)(2,1)S(1)}, u32[]{:S(2)}, u32[]{:S(2)}) collective-permute-start(bf16[2,128,128]{2,1,0:T(8,128)(2,1)} %param.5), channel_id=1, source_target_pairs={{0,8},{1,9},{2,10},{3,11},{4,12},{5,13},{6,14},{7,15},{8,16},{9,17... | collective-permute-start | bytes 196616 | tf_op jit(solution)/shard_map/ppermute | solution.py:22
  14.0 11.9 %all-to-all-start = ((f32[8,1,64]{2,1,0:T(1,128)}), f32[8,1,64]{2,1,0:T(1,128)S(1)}, u32[]{:S(2)}, u32[]{:S(2)}) async-start(f32[8,1,64]{2,1,0:T(1,128)} %broadcast_in_dim.64), calls=%async_computation | async-start | bytes 8192 | tf_op jit(solution)/shard_map/all_to_all | solution.py:170
  18.4 10.2 %collective-permute-start.2 = (bf16[2,256,128]{2,1,0:T(8,128)(2,1)S(1)}, bf16[2,256,128]{2,1,0:T(8,128)(2,1)S(1)}, u32[]{:S(2)}, u32[]{:S(2)}) collective-permute-start(bf16[2,256,128]{2,1,0:T(8,128)(2,1)S(1)} %pad_maximum_fusion.2), channel_id=1, source_target_pairs={{0,2},{1,3},{2,4},{3,5},{4,6},{5,7},{6,8},{7,9},{8,10},{9,11},{10,... | collective-permute-start | bytes 393224 | tf_op jit(solution)/shard_map/ppermute | solution.py:22
  28.7 13.2 %collective-permute-start.3 = (bf16[2,512,128]{2,1,0:T(8,128)(2,1)S(1)}, bf16[2,512,128]{2,1,0:T(8,128)(2,1)S(1)}, u32[]{:S(2)}, u32[]{:S(2)}) collective-permute-start(bf16[2,512,128]{2,1,0:T(8,128)(2,1)S(1)} %pad_maximum_fusion.1), channel_id=1, source_target_pairs={{0,4},{1,5},{2,6},{3,7},{4,8},{5,9},{6,10},{7,11},{8,12},{9,13},{1... | collective-permute-start | bytes 786440 | tf_op jit(solution)/shard_map/ppermute | solution.py:22

commit v18 on v17

--- a/solution.py
+++ b/solution.py
@@ -133,7 +133,7 @@
 
 def side_by_side(blocks):
     count, rows, width = blocks.shape
-    step = count // 4
+    step = count
     return pl.pallas_call(
         place_kernel,
         out_shape=jax.ShapeDtypeStruct((rows, count * width), blocks.dtype),

time: 99.4 us -> 98.7 us (level)
  no operation moved by 1% of the time
where the time goes in v18:
time: 98.7 us; the launch traced here: 98.2 us
  blocking collectives  32.1 us (33%)
  starting transfers between devices  25.1 us (25%)
  Pallas kernels  23.4 us (24%)
  other arithmetic  12.2 us (12%)
  waiting for transfers between devices  2.72 us (3%)
  local copies, waits for them, and re-layouts  2.71 us (3%)
    all_to_all x1, blocking collectives, on_device(): gathered = lax.all_to_all(mixed, 'cand', 0, 0, tiled=True)  32.1 us
    ppermute x4, starting transfers between devices, passed_along(): lax.ppermute(value, axis, [(source, source + steps) for source in range(f...  20.6 us
    pallas_call x1, Pallas kernels, attend_all(): pl.pallas_call(attention_kernel, out_shape=jax.ShapeDtypeStruct((cands, q...  20.4 us
    select_n x1, other arithmetic, cos_and_sin(): return jnp.where(quadrant + 1 & 2 != 0, -base, base)  7.16 us
    all_to_all x1, starting transfers between devices, on_device(): lax.all_to_all(jnp.broadcast_to(factors, (cands, factors.shape[1])), 'can...  4.47 us
    pallas_call x1, Pallas kernels, side_by_side(): pl.pallas_call(place_kernel, out_shape=jax.ShapeDtypeStruct((rows, count...  3.04 us
    ppermute x4, waiting for transfers between devices, passed_along(): lax.ppermute(value, axis, [(source, source + steps) for source in range(f...  2.72 us
    select_n x1, other arithmetic, on_device(): bias = jnp.where(allowed, 0.0, -1e+30).astype(jnp.float32)  2.04 us
  transfers between devices with their start and end apart: 5, of which 1 were waited for; matrix products, arithmetic and copies ran while one was open for 14% of the time, Pallas kernels for 0%

profile of v18, /device:TPU:96, one launch (start us, length us, event | category | flops | bytes accessed | tf_op | source)
XLA Modules:
  0.0 98.2 jit_solution(7166589778954119750)
XLA Ops:
  0.0 0.0 copy-start
  0.0 3.5 %collective-permute-start = (bf16[2,128,128]{2,1,0:T(8,128)(2,1)}, bf16[2,128,128]{2,1,0:T(8,128)(2,1)S(1)}, u32[]{:S(2)}, u32[]{:S(2)}) collective-permute-start(bf16[2,128,128]{2,1,0:T(8,128)(2,1)} %param.5), channel_id=1, source_target_pairs={{0,1},{1,2},{2,3},{3,4},{4,5},{5,6},{6,7},{7,8},{8,9},{9,10},{10,1... | collective-permute-start | bytes 196616 | tf_op jit(solution)/shard_map/ppermute | solution.py:22
  3.5 6.4 %collective-permute-start.1 = (bf16[2,128,128]{2,1,0:T(8,128)(2,1)}, bf16[2,128,128]{2,1,0:T(8,128)(2,1)S(1)}, u32[]{:S(2)}, u32[]{:S(2)}) collective-permute-start(bf16[2,128,128]{2,1,0:T(8,128)(2,1)} %param.5), channel_id=1, source_target_pairs={{0,8},{1,9},{2,10},{3,11},{4,12},{5,13},{6,14},{7,15},{8,16},{9,17... | collective-permute-start | bytes 196616 | tf_op jit(solution)/shard_map/ppermute | solution.py:22
  10.0 0.0 collective-permute-done
  10.0 0.9 pad_maximum_fusion.2
  10.9 0.7 copy.8
  11.6 0.1 reduce
  11.8 0.7 sub.25
  12.4 0.1 convert_reduce_fusion.1
  12.5 0.1 convert_reduce_fusion
  12.6 0.1 select_reduce_fusion
  12.7 1.3 %broadcast_in_dim.64 = f32[8,1,64]{2,1,0:T(1,128)} broadcast(f32[64]{0:T(128)} %bitcast.6), dimensions={2} | broadcast | bytes 2304 | tf_op jit(solution)/shard_map/broadcast_in_dim | solution.py:171
  14.0 4.5 %all-to-all-start = ((f32[8,1,64]{2,1,0:T(1,128)}), f32[8,1,64]{2,1,0:T(1,128)S(1)}, u32[]{:S(2)}, u32[]{:S(2)}) async-start(f32[8,1,64]{2,1,0:T(1,128)} %broadcast_in_dim.64), calls=%async_computation | async-start | bytes 8192 | tf_op jit(solution)/shard_map/all_to_all | solution.py:170
  18.4 4.6 %collective-permute-start.2 = (bf16[2,256,128]{2,1,0:T(8,128)(2,1)S(1)}, bf16[2,256,128]{2,1,0:T(8,128)(2,1)S(1)}, u32[]{:S(2)}, u32[]{:S(2)}) collective-permute-start(bf16[2,256,128]{2,1,0:T(8,128)(2,1)S(1)} %pad_maximum_fusion.2), channel_id=1, source_target_pairs={{0,2},{1,3},{2,4},{3,5},{4,6},{5,7},{6,8},{7,9},{8,10},{9,11},{10,... | collective-permute-start | bytes 393224 | tf_op jit(solution)/shard_map/ppermute | solution.py:22
  23.1 2.0 %and_select_fusion.bias_ref = f32[1152,128]{1,0:T(8,128)} fusion(s32[128]{0:T(128)S(1)} %iota_add_fusion.1, s32[128]{0:T(128)S(1)} %compare_select_fusion, s32[1152]{0:T(1024)S(1)} %iota_add_fusion, s32[1152]{0:T(1024)S(1)} %get-tuple-element.14, pred[1152]{0:T(1024)(128)(4,1)S(1)} %get-tuple-element.13), kind=kLoop, calls=%fused_computation.35 | loop fusion | flops 737280 | bytes 601216 | tf_op jit(solution)/shard_map/jit(_where)/select_n | solution.py:180
  25.1 0.0 copy-done
  25.1 0.7 constant_dynamic-slice_fusion.q_ref
  25.8 0.0 all-to-all-done
  25.8 0.1 pad_maximum_fusion.3
  25.9 2.7 %collective-permute-done.2 = bf16[2,256,128]{2,1,0:T(8,128)(2,1)S(1)} collective-permute-done((bf16[2,256,128]{2,1,0:T(8,128)(2,1)S(1)}, bf16[2,256,128]{2,1,0:T(8,128)(2,1)S(1)}, u32[]{:S(2)}, u32[]{:S(2)}) %collective-permute-start.2) | collective-permute-done | bytes 131104 | tf_op jit(solution)/shard_map/ppermute | solution.py:22
  28.7 6.1 %collective-permute-start.3 = (bf16[2,512,128]{2,1,0:T(8,128)(2,1)S(1)}, bf16[2,512,128]{2,1,0:T(8,128)(2,1)S(1)}, u32[]{:S(2)}, u32[]{:S(2)}) collective-permute-start(bf16[2,512,128]{2,1,0:T(8,128)(2,1)S(1)} %pad_maximum_fusion.1), channel_id=1, source_target_pairs={{0,4},{1,5},{2,6},{3,7},{4,8},{5,9},{6,10},{7,11},{8,12},{9,13},{1... | collective-permute-start | bytes 786440 | tf_op jit(solution)/shard_map/ppermute | solution.py:22
  34.7 7.2 %negate_select_fusion.table_ref = f32[8,1152,128]{2,1,0:T(8,128)} fusion(s32[128]{0:T(128)S(1)} %compare_select_fusion.1, f32[8,128]{1,0:T(8,128)S(1)} %pad_maximum_fusion.3, f32[1152]{0:T(1024)S(1)} %select_convert_fusion), kind=kLoop, calls=%fused_computation | loop fusion | flops 43646976 | bytes 4727808 | tf_op jit(solution)/shard_map/jit(_where)/select_n | solution.py:51
  41.9 0.0 collective-permute-done.1
  41.9 0.0 collective-permute-done.3
  41.9 0.9 pad_maximum_fusion.kv_ref
  42.8 20.4 %shard_map.46 = bf16[8,128,1024]{2,1,0:T(8,128)(2,1)} custom-call(bf16[128,1024]{1,0:T(8,128)(2,1)} %constant_dynamic-slice_fusion.q_ref, bf16[2,1152,128]{2,1,0:T(8,128)(2,1)} %pad_maximum_fusion.kv_ref, f32[8,1152,128]{2,1,0:T(8,128)} %negate_select_fusion.table_ref, f32[1152,128]{1,0:T(8,128)} %and_select_fusion.bias_ref), custom_call_target="tpu_custom_call" | custom-call | flops 4831838208 | bytes 2949120 | tf_op jit(solution)/shard_map/pallas_call | solution.py:109
  63.1 32.1 %all_to_all.14.in_ref = bf16[8,128,1024]{2,1,0:T(8,128)(2,1)} all-to-all(bf16[8,128,1024]{2,1,0:T(8,128)(2,1)} %shard_map.46), channel_id=1, replica_groups=mesh['cand'=8,'doc'=64] {'cand'}, dimensions={0} | all-to-all | bytes 4194304 | tf_op jit(solution)/shard_map/all_to_all | solution.py:184
  95.2 3.0 %shard_map.47 = bf16[128,8192]{1,0:T(8,128)(2,1)} custom-call(bf16[8,128,1024]{2,1,0:T(8,128)(2,1)} %all_to_all.14.in_ref), custom_call_target="tpu_custom_call" | custom-call | tf_op jit(solution)/shard_map/pallas_call | solution.py:137
  (10 shorter events, 0.1 us)
Async XLA Ops:
  0.0 25.1 %copy-start = (bf16[128,8192]{1,0:T(8,128)(2,1)S(1)}, bf16[128,8192]{1,0:T(8,128)(2,1)}, u32[]{:S(2)}) copy-start(bf16[128,8192]{1,0:T(8,128)(2,1)} %param.4) | copy-start | bytes 6291460
  0.0 10.0 %collective-permute-start = (bf16[2,128,128]{2,1,0:T(8,128)(2,1)}, bf16[2,128,128]{2,1,0:T(8,128)(2,1)S(1)}, u32[]{:S(2)}, u32[]{:S(2)}) collective-permute-start(bf16[2,128,128]{2,1,0:T(8,128)(2,1)} %param.5), channel_id=1, source_target_pairs={{0,1},{1,2},{2,3},{3,4},{4,5},{5,6},{6,7},{7,8},{8,9},{9,10},{10,1... | collective-permute-start | bytes 196616 | tf_op jit(solution)/shard_map/ppermute | solution.py:22
  3.5 38.4 %collective-permute-start.1 = (bf16[2,128,128]{2,1,0:T(8,128)(2,1)}, bf16[2,128,128]{2,1,0:T(8,128)(2,1)S(1)}, u32[]{:S(2)}, u32[]{:S(2)}) collective-permute-start(bf16[2,128,128]{2,1,0:T(8,128)(2,1)} %param.5), channel_id=1, source_target_pairs={{0,8},{1,9},{2,10},{3,11},{4,12},{5,13},{6,14},{7,15},{8,16},{9,17... | collective-permute-start | bytes 196616 | tf_op jit(solution)/shard_map/ppermute | solution.py:22
  14.0 11.9 %all-to-all-start = ((f32[8,1,64]{2,1,0:T(1,128)}), f32[8,1,64]{2,1,0:T(1,128)S(1)}, u32[]{:S(2)}, u32[]{:S(2)}) async-start(f32[8,1,64]{2,1,0:T(1,128)} %broadcast_in_dim.64), calls=%async_computation | async-start | bytes 8192 | tf_op jit(solution)/shard_map/all_to_all | solution.py:170
  18.4 10.2 %collective-permute-start.2 = (bf16[2,256,128]{2,1,0:T(8,128)(2,1)S(1)}, bf16[2,256,128]{2,1,0:T(8,128)(2,1)S(1)}, u32[]{:S(2)}, u32[]{:S(2)}) collective-permute-start(bf16[2,256,128]{2,1,0:T(8,128)(2,1)S(1)} %pad_maximum_fusion.2), channel_id=1, source_target_pairs={{0,2},{1,3},{2,4},{3,5},{4,6},{5,7},{6,8},{7,9},{8,10},{9,11},{10,... | collective-permute-start | bytes 393224 | tf_op jit(solution)/shard_map/ppermute | solution.py:22
  28.7 13.2 %collective-permute-start.3 = (bf16[2,512,128]{2,1,0:T(8,128)(2,1)S(1)}, bf16[2,512,128]{2,1,0:T(8,128)(2,1)S(1)}, u32[]{:S(2)}, u32[]{:S(2)}) collective-permute-start(bf16[2,512,128]{2,1,0:T(8,128)(2,1)S(1)} %pad_maximum_fusion.1), channel_id=1, source_target_pairs={{0,4},{1,5},{2,6},{3,7},{4,8},{5,9},{6,10},{7,11},{8,12},{9,13},{1... | collective-permute-start | bytes 786440 | tf_op jit(solution)/shard_map/ppermute | solution.py:22
